TPU v7x, 32 devices: a whole 2x2x4 slice. The times are simulated.
32 devices in a mesh: groups: 2 (over x), dp: 4 (over y, core), hidden: 4 (over z).
Axes of the slice: x: 2, y: 2, z: 4, core: 2. Of those that a mesh axis runs over, the one named last changes fastest.
Arguments:
- activations: bfloat16 [24576, 8192], P(('groups', 'dp'), 'hidden'), parts along dimension 0, may hold values from -6 to 6
- cotangent: bfloat16 [24576, 8192], P(('groups', 'dp'), 'hidden'), parts along dimension 0
- up_factor_matrix: bfloat16 [8192, 64], P('hidden'), may hold values from -0.0625 to 0.0625
- input_sketch: bfloat16 [8192, 128], P('hidden'), may hold values from -0.0625 to 0.0625
- rank_sketch: float32 [64, 32], replicated, may hold values from -0.75 to 0.75
Outputs:
- features: bfloat16 [48, 4096], P(('groups', 'dp'), 'hidden'), parts along dimension 0
- scores: float32 [48, 24], P(('groups', 'dp'), 'hidden'), parts along dimension 0
There are 2 independent parts, one for each index of `groups`. A program takes and returns all parts, laid end to end along the dimension named above; an argument that names none is the same for every part. Nothing has to cross between parts.
All inputs are finite; a program needn't handle non-finite values.
Results may differ from a plain program's by a relative error of at most 0.0017.
Values may be sent and summed in bfloat16 or wider, within the bound.
No kernel may reach another device: no remote copies, remote signals or barrier semaphores. Data moves between devices by JAX's collectives and lax.ppermute only.
A program may use at most 64 MiB of HBM per device.

v0:
```python
import math

import jax
import jax.numpy as jnp
from jax import lax
from jax.sharding import PartitionSpec as P

FEAT = 4096
SEQ = 512


epsilon = 1e-05


def outer_product_sums(rank_rows, input_rows, examples):
    rank_rows = rank_rows.reshape(examples, SEQ, rank_rows.shape[1])
    input_rows = input_rows.reshape(examples, SEQ, input_rows.shape[1])
    return jnp.einsum("esa,esb->eab", rank_rows, input_rows, precision=lax.Precision.HIGHEST)


def per_device(activations, cotangent, up_factor_matrix, input_sketch, rank_sketch):
    shards = lax.axis_size("hidden")
    own_cols = rank_sketch.shape[1] // shards
    examples = activations.shape[0] // SEQ
    backward_pass = jnp.dot(cotangent, up_factor_matrix, preferred_element_type=jnp.float32)
    rank_part = jnp.dot(backward_pass, rank_sketch, precision=lax.Precision.HIGHEST)
    input_part = jnp.dot(activations, input_sketch, preferred_element_type=jnp.float32)
    rank_full, input_full = lax.psum((rank_part, input_part), "hidden")
    rank_own = lax.dynamic_slice_in_dim(rank_full, lax.axis_index("hidden") * own_cols, own_cols, 1)
    feat_block = outer_product_sums(rank_own, input_full, examples)
    features = feat_block.reshape(examples, -1).astype(jnp.bfloat16)
    widened = features.astype(jnp.float32)
    all_count = examples * lax.axis_size("dp")
    squares = lax.psum(jnp.sum(widened * widened, axis=0), "dp")
    weighted = widened * (1.0 / (squares / all_count + epsilon))
    partial_scores = jnp.dot(
        weighted,
        lax.all_gather(features, "dp", axis=0, tiled=True).astype(jnp.float32).T,
        precision=lax.Precision.HIGHEST,
    )
    scores = lax.psum_scatter(
        partial_scores / math.sqrt(FEAT), "hidden", scatter_dimension=1, tiled=True
    )
    return (features, scores)


def solution(mesh):
    placed = (
        P(("groups", "dp"), "hidden"),
        P(("groups", "dp"), "hidden"),
        P("hidden", None),
        P("hidden", None),
        P(),
    )
    return jax.shard_map(
        per_device,
        mesh=mesh,
        in_specs=placed,
        out_specs=(P(("groups", "dp"), "hidden"), P(("groups", "dp"), "hidden")),
        check_vma=False,
    )
```

profile of v0, /device:TPU:0, one launch (start us, length us, event | category | flops | bytes accessed | tf_op | source)
XLA Modules:
  0.0 139.6 jit_solution(18415344260464060510)
XLA Ops:
  7.2 0.0 copy-start
  7.2 0.0 copy-start.2
  7.2 0.0 all-reduce.4.cloned.1.call-start
  7.2 0.0 copy-start.3
  7.2 8.6 %fusion.3 = f32[3072,64]{0,1:T(8,128)S(1)} fusion(bf16[3072,2048]{1,0:T(8,128)(2,1)} %param.6, bf16[2048,64]{0,1:T(8,128)(2,1)} %param.7), kind=kOutput, calls=%fused_computation.10 | convolution fusion | flops 805306368 | bytes 13631488 | tf_op jit(solution)/shard_map/dot_general | solution.py:25
  15.9 0.0 copy-done.2
  15.9 0.0 copy-start.4
  15.9 1.3 fusion.4
  17.2 0.0 copy-done
  17.2 0.0 copy-done.3
  17.2 4.6 %fusion.5 = f32[3072,128]{1,0:T(8,128)} fusion(bf16[3072,2048]{1,0:T(8,128)(2,1)S(1)} %copy-done.3, bf16[2048,128]{1,0:T(8,128)(2,1)S(1)} %copy-done), kind=kOutput, calls=%fused_computation.12 | convolution fusion | flops 1610612736 | bytes 14680064 | tf_op jit(solution)/shard_map/dot_general | solution.py:27
  21.8 0.0 all-reduce.4.cloned.1.call-update
  21.8 0.0 copy-done.4
  21.8 0.6 dynamic-slice
  23.1 83.5 %all-reduce.4.cloned.1.call-done = (f32[3072,32]{0,1:T(8,128)}, f32[6,512,128]{2,1,0:T(8,128)}) async-done(((f32[3072,32]{0,1:T(8,128)}, f32[6,512,128]{2,1,0:T(8,128)}), (f32[3072,32]{0,1:T(8,128)}, f32[6,512,128]{2,1,0:T(8,128)})) %all-reduce.4.cloned.1.call-update) | async-done | bytes 1966096 | tf_op jit(solution)/shard_map/psum | solution.py:28
  106.6 0.9 constant_dynamic-slice_fusion.1
  107.5 2.3 %multiply_reduce_fusion = (f32[8,128]{1,0:T(8,128)S(1)}, bf16[6,8,128]{2,1,0:T(8,128)(2,1)S(1)}) fusion(f32[6,512,8]{1,2,0:T(8,128)S(1)} %bitcast.20, f32[6,512,128]{2,1,0:T(8,128)} %get-tuple-element.3), kind=kOutput, calls=%fused_computation.4 | convolution fusion | flops 37772288 | bytes 1687552 | tf_op jit(solution)/shard_map/esa,esb->eab/dot_general | solution.py:18
  109.8 0.0 copy-start.1
  109.8 5.2 %all-gather = bf16[4,6,1024]{2,1,0:T(8,128)(2,1)S(1)} all-gather(bf16[1,6,1024]{2,1,0:T(8,128)(2,1)S(1)} %reshape.16), channel_id=1, replica_groups=mesh['groups'=2,'dp'=4,'hidden'=4] {'dp'}, dimensions={0}, use_global_device_ids=true | all-gather | bytes 61440 | tf_op jit(solution)/shard_map/all_gather | solution.py:38
  115.1 7.1 %psum.23 = f32[1024]{0:T(1024)S(1)} all-reduce(f32[1024]{0:T(1024)S(1)} %bitcast.24), channel_id=1, replica_groups=mesh['groups'=2,'dp'=4,'hidden'=4] {'dp'}, use_global_device_ids=true, to_apply=%region_3.0 | all-reduce | flops 1024 | bytes 8192 | tf_op jit(solution)/shard_map/psum | solution.py:34
  122.2 0.1 convolution_multiply_fusion
  122.3 9.8 %all-reduce = f32[6,24]{1,0:T(8,128)S(1)} all-reduce(f32[6,24]{1,0:T(8,128)S(1)} %convolution_multiply_fusion), channel_id=2, replica_groups=mesh['groups'=2,'dp'=4,'hidden'=4] {'hidden'}, use_global_device_ids=true, to_apply=%region_4.0.clone | all-reduce | flops 144 | bytes 1152
  132.1 0.7 constant_dynamic-slice_fusion
  132.8 0.0 copy-done.1
  (4 shorter events, 0.1 us)
Async XLA Ops:
  7.2 10.0 %copy-start = (bf16[2048,128]{1,0:T(8,128)(2,1)S(1)}, bf16[2048,128]{1,0:T(8,128)(2,1)}, u32[]{:S(2)}) copy-start(bf16[2048,128]{1,0:T(8,128)(2,1)} %param.8) | copy-start | bytes 1572868
  7.2 8.7 %copy-start.2 = (f32[64,32]{0,1:T(8,128)S(1)}, f32[64,32]{0,1:T(8,128)}, u32[]{:S(2)}) copy-start(f32[64,32]{0,1:T(8,128)} %param.9) | copy-start | bytes 24580
  7.2 99.4 %all-reduce.4.cloned.1.call-start = ((), (), s32[]{:S(2)}) async-start(), calls=%async_computation | async-start | bytes 3932160 | tf_op jit(solution)/shard_map/psum | solution.py:28
  7.2 10.0 %copy-start.3 = (bf16[3072,2048]{1,0:T(8,128)(2,1)S(1)}, bf16[3072,2048]{1,0:T(8,128)(2,1)}, u32[]{:S(2)}) copy-start(bf16[3072,2048]{1,0:T(8,128)(2,1)} %param.5) | copy-start | bytes 37748740
  15.9 5.9 %copy-start.4 = (u32[32]{0:T(128)S(1)}, u32[32]{0:T(128)}, u32[]{:S(2)}) copy-start(u32[32]{0:T(128)} %constant.24) | copy-start | bytes 388
  109.8 22.9 %copy-start.1 = (bf16[1,6,8,128]{3,1,2,0:T(8,128)(2,1)}, bf16[1,6,8,128]{3,1,2,0:T(8,128)(2,1)S(1)}, u32[]{:S(2)}) copy-start(bf16[1,6,8,128]{3,1,2,0:T(8,128)(2,1)S(1)} %copy.11) | copy-start | bytes 36868
Sparse Core Ops, SparseCore 0:
  21.9 84.5 all-reduce.3
where the time goes:
time: 140 us
  waiting for transfers between devices  83.5 us (60%)
  blocking collectives  22.1 us (16%)
  matrix products  16.9 us (12%)
  between operations  14.8 us (11%)
  local copies, waits for them, and re-layouts  2.26 us (2%)
    psum x1, waiting for transfers between devices, per_device(): rank_full, input_full = lax.psum((rank_part, input_part), 'hidden')  83.5 us
    unnamed x1, blocking collectives  9.77 us
    dot_general x1, matrix products, per_device(): jnp.dot(cotangent, up_factor_matrix, preferred_element_type=jnp.float32)  8.64 us
    psum x1, blocking collectives, per_device(): squares = lax.psum(jnp.sum(widened * widened, axis=0), 'dp')  7.08 us
    all_gather x1, blocking collectives, per_device(): lax.all_gather(features, 'dp', axis=0, tiled=True).astype(jnp.float32)  5.24 us
    dot_general x1, matrix products, per_device(): jnp.dot(activations, input_sketch, preferred_element_type=jnp.float32)  4.58 us
  transfers between devices with their start and end apart: 1, of which 1 were waited for; matrix products, arithmetic and copies ran while one was open for 0% of the time, Pallas kernels for 0%

commit v1 on v0

v1 whole, which is shorter than its diff:
```python
import math

import jax
import jax.numpy as jnp
from jax import lax
from jax.sharding import PartitionSpec as P

SEQ = 512
epsilon = 1e-05
HI = lax.Precision.HIGHEST


def partial_features(activations, cotangent, up_factor_matrix, input_sketch, rank_sketch):
    examples = activations.shape[0] // SEQ
    backward_pass = jnp.dot(cotangent, up_factor_matrix, preferred_element_type=jnp.float32)
    rank_part = jnp.dot(backward_pass, rank_sketch, precision=HI)
    rank_full = lax.psum(rank_part, "hidden")
    input_part = jnp.dot(activations, input_sketch, preferred_element_type=jnp.float32)
    rank_rows = rank_full.reshape(examples, SEQ, rank_full.shape[1])
    input_rows = input_part.reshape(examples, SEQ, input_part.shape[1])
    return jnp.einsum("esa,esb->eab", rank_rows, input_rows, precision=HI)


def per_device(activations, cotangent, up_factor_matrix, input_sketch, rank_sketch):
    examples = activations.shape[0] // SEQ
    partial = partial_features(activations, cotangent, up_factor_matrix, input_sketch, rank_sketch)
    own = lax.psum_scatter(partial, "hidden", scatter_dimension=1, tiled=True)
    features = own.reshape(examples, -1).astype(jnp.bfloat16)
    widened = features.astype(jnp.float32)
    every = lax.all_gather(features, "dp", axis=0, tiled=True).astype(jnp.float32)
    all_count = every.shape[0]
    weight = 1.0 / (jnp.sum(every * every, axis=0) / all_count + epsilon)
    partial_scores = jnp.dot(widened * weight, every.T, precision=HI)
    feat_total = features.shape[1] * lax.axis_size("hidden")
    scores = lax.psum_scatter(partial_scores / math.sqrt(feat_total), "hidden", scatter_dimension=1, tiled=True)
    return (features, scores)


def solution(mesh):
    placed = (
        P(("groups", "dp"), "hidden"),
        P(("groups", "dp"), "hidden"),
        P("hidden", None),
        P("hidden", None),
        P(),
    )
    return jax.shard_map(
        per_device,
        mesh=mesh,
        in_specs=placed,
        out_specs=(P(("groups", "dp"), "hidden"), P(("groups", "dp"), "hidden")),
        check_vma=False,
    )
```

time: 140 us -> 103 us (0.74)
  waiting for transfers between devices: 83.5 us -> 51.4 us
  blocking collectives: 22.1 us -> 14.1 us
  other arithmetic: 0.01 us -> 1.51 us
    psum x1, waiting for transfers between devices: 83.5 us -> 33.3 us  [partial_features(): rank_full = lax.psum(rank_part, 'hidden')]
    reduce_scatter x0 -> x1, waiting for transfers between devices: none -> 18 us  [per_device(): own = lax.psum_scatter(partial, 'hidden', scatter_dimension=1, tiled=True)]
    psum x1 -> x0, blocking collectives: 7.08 us -> none  [per_device(): squares = lax.psum(jnp.sum(widened * widened, axis=0), 'dp')]
  transfers between devices with their start and end apart: 1 -> 2, of which waited for: 1 -> 2; matrix products, arithmetic and copies ran while one was open for 0% -> 7% of each run, Pallas kernels for 0% -> 0%
where the time goes in v1:
time: 103 us; the launch traced here: 102 us
  waiting for transfers between devices  51.4 us (50%)
  matrix products  18.2 us (18%)
  between operations  14.8 us (14%)
  blocking collectives  14.1 us (14%)
  local copies, waits for them, and re-layouts  2.12 us (2%)
  other arithmetic  1.51 us (1%)
    psum x1, waiting for transfers between devices, partial_features(): rank_full = lax.psum(rank_part, 'hidden')  33.3 us
    reduce_scatter x1, waiting for transfers between devices, per_device(): own = lax.psum_scatter(partial, 'hidden', scatter_dimension=1, tiled=True)  18 us
    unnamed x1, blocking collectives  8.87 us
    dot_general x1, matrix products, partial_features(): jnp.dot(cotangent, up_factor_matrix, preferred_element_type=jnp.float32)  8.54 us
    dot_general x1, matrix products, partial_features(): jnp.dot(activations, input_sketch, preferred_element_type=jnp.float32)  6.43 us
    all_gather x1, blocking collectives, per_device(): lax.all_gather(features, 'dp', axis=0, tiled=True).astype(jnp.float32)  5.24 us
    dot_general x1, matrix products, partial_features(): return jnp.einsum('esa,esb->eab', rank_rows, input_rows, precision=HI)  2.56 us
  transfers between devices with their start and end apart: 2, of which 2 were waited for; matrix products, arithmetic and copies ran while one was open for 7% of the time, Pallas kernels for 0%

profile of v1, /device:TPU:0, one launch (start us, length us, event | category | flops | bytes accessed | tf_op | source)
XLA Modules:
  0.0 102.2 jit_solution(1430355380435664496)
XLA Ops:
  7.2 0.0 copy-start
  7.2 0.0 copy-start.2
  7.2 0.0 all-reduce.3.cloned.1.call-start
  7.2 8.5 %fusion.3 = f32[3072,64]{0,1:T(8,128)S(1)} fusion(bf16[3072,2048]{1,0:T(8,128)(2,1)} %param.6, bf16[2048,64]{0,1:T(8,128)(2,1)} %param.7), kind=kOutput, calls=%fused_computation.9 | convolution fusion | flops 805306368 | bytes 13631488 | tf_op jit(solution)/shard_map/dot_general | solution.py:15
  15.8 0.0 copy-done.2
  15.8 0.0 copy-start.3
  15.8 0.6 fusion.4
  16.4 0.8 copy.16
  17.1 0.0 all-reduce.3.cloned.1.call-update
  17.2 0.0 reduce-scatter.3.cloned.1.call-start
  17.2 0.0 copy-done
  17.2 6.4 %fusion.5 = f32[3072,128]{1,0:T(8,128)S(1)} fusion(bf16[3072,2048]{1,0:T(8,128)(2,1)} %param.5, bf16[2048,128]{1,0:T(8,128)(2,1)S(1)} %copy-done), kind=kOutput, calls=%fused_computation.11 | convolution fusion | flops 1610612736 | bytes 14680064 | tf_op jit(solution)/shard_map/dot_general | solution.py:18
  23.7 33.3 %all-reduce.3.cloned.1.call-done = f32[6,512,32]{1,2,0:T(8,128)} async-done(((f32[6,512,32]{1,2,0:T(8,128)}), f32[6,512,32]{1,2,0:T(8,128)}) %all-reduce.3.cloned.1.call-update) | async-done | bytes 393232 | tf_op jit(solution)/shard_map/psum | solution.py:17
  57.0 2.6 %fusion.6 = f32[6,32,128]{2,1,0:T(8,128)} fusion(f32[6,512,32]{1,2,0:T(8,128)} %all-reduce.3.cloned.1.call-done, f32[6,512,128]{2,1,0:T(8,128)S(1)} %bitcast.23), kind=kOutput, calls=%fused_computation.12 | convolution fusion | flops 150994944 | bytes 2064384 | tf_op jit(solution)/shard_map/esa,esb->eab/dot_general | solution.py:21
  59.5 0.0 reduce-scatter.3.cloned.1.call-update
  59.6 0.0 copy-done.3
  59.6 0.6 dynamic-slice
  60.8 18.0 %reduce-scatter.3.cloned.1.call-done = f32[6,8,128]{2,1,0:T(8,128)} async-done(((f32[6,32,128]{2,1,0:T(8,128)}), f32[6,8,128]{2,1,0:T(8,128)}) %reduce-scatter.3.cloned.1.call-update) | async-done | bytes 24592 | tf_op jit(solution)/shard_map/reduce_scatter | solution.py:27
  78.9 0.7 convert_element_type.12
  79.6 5.2 %all-gather = bf16[4,6,1024]{2,1,0:T(8,128)(2,1)S(1)} all-gather(bf16[1,6,1024]{2,1,0:T(8,128)(2,1)S(1)} %reshape.19), channel_id=1, replica_groups=mesh['groups'=2,'dp'=4,'hidden'=4] {'dp'}, dimensions={0}, use_global_device_ids=true | all-gather | bytes 61440 | tf_op jit(solution)/shard_map/all_gather | solution.py:30
  84.9 0.7 convert_bitcast_fusion
  85.7 0.0 copy-start.1
  85.7 0.1 convolution_multiply_fusion
  85.8 8.9 %all-reduce = f32[6,24]{1,0:T(8,128)S(1)} all-reduce(f32[6,24]{1,0:T(8,128)S(1)} %convolution_multiply_fusion), channel_id=3, replica_groups=mesh['groups'=2,'dp'=4,'hidden'=4] {'hidden'}, use_global_device_ids=true, to_apply=%region_3.0.clone | all-reduce | flops 144 | bytes 1152
  94.7 0.7 constant_dynamic-slice_fusion
  95.4 0.0 copy-done.1
  (5 shorter events, 0.1 us)
Async XLA Ops:
  7.2 10.0 %copy-start = (bf16[2048,128]{1,0:T(8,128)(2,1)S(1)}, bf16[2048,128]{1,0:T(8,128)(2,1)}, u32[]{:S(2)}) copy-start(bf16[2048,128]{1,0:T(8,128)(2,1)} %param.8) | copy-start | bytes 1572868
  7.2 8.6 %copy-start.2 = (f32[64,32]{0,1:T(8,128)S(1)}, f32[64,32]{0,1:T(8,128)}, u32[]{:S(2)}) copy-start(f32[64,32]{0,1:T(8,128)} %param.9) | copy-start | bytes 24580
  7.2 49.8 %all-reduce.3.cloned.1.call-start = ((), (), s32[]{:S(2)}) async-start(), calls=%async_computation.1 | async-start | bytes 786432 | tf_op jit(solution)/shard_map/psum | solution.py:17
  15.8 43.8 %copy-start.3 = (u32[32]{0:T(128)S(1)}, u32[32]{0:T(128)}, u32[]{:S(2)}) copy-start(u32[32]{0:T(128)} %constant.14) | copy-start | bytes 388
  17.2 61.7 %reduce-scatter.3.cloned.1.call-start = ((), (), s32[]{:S(2)}) async-start(), calls=%async_computation.2 | async-start | bytes 122880 | tf_op jit(solution)/shard_map/reduce_scatter | solution.py:27
  85.7 9.7 %copy-start.1 = (bf16[1,6,8,128]{3,1,2,0:T(8,128)(2,1)}, bf16[1,6,8,128]{3,1,2,0:T(8,128)(2,1)S(1)}, u32[]{:S(2)}) copy-start(bf16[1,6,8,128]{3,1,2,0:T(8,128)(2,1)S(1)} %copy.17) | copy-start | bytes 36868
Sparse Core Ops, SparseCore 0:
  17.3 39.6 all-reduce.2
  59.7 19.1 reduce-scatter.2

commit v2 on v1

v2 whole, which is shorter than its diff:
```python
import math

import jax
import jax.numpy as jnp
from jax import lax
from jax.sharding import PartitionSpec as P

SEQ = 512
epsilon = 1e-05
HI = lax.Precision.HIGHEST


def exchange(blocks, axis):
    n = lax.axis_size(axis)
    me = lax.axis_index(axis)
    got = [lax.dynamic_index_in_dim(blocks, me, 0, keepdims=False)]
    for d in range(1, n):
        piece = lax.dynamic_index_in_dim(blocks, (me + d) % n, 0, keepdims=False)
        got.append(lax.ppermute(piece, axis, [(i, (i + d) % n) for i in range(n)]))
    return got


def reduce_scatter(blocks, axis):
    got = exchange(blocks, axis)
    acc = got[0]
    for g in got[1:]:
        acc = acc + g
    return acc


def all_gather(x, axis):
    n = lax.axis_size(axis)
    me = lax.axis_index(axis)
    out = jnp.zeros((n,) + x.shape, x.dtype)
    out = lax.dynamic_update_index_in_dim(out, x, me, 0)
    for d in range(1, n):
        got = lax.ppermute(x, axis, [(i, (i + d) % n) for i in range(n)])
        out = lax.dynamic_update_index_in_dim(out, got, (me - d) % n, 0)
    return out


def all_reduce(x, axis):
    n = lax.axis_size(axis)
    acc = reduce_scatter(x.reshape((n, -1) + x.shape[1:]), axis)
    return all_gather(acc, axis).reshape(x.shape)


def per_device(activations, cotangent, up_factor_matrix, input_sketch, rank_sketch):
    shards = lax.axis_size("hidden")
    examples = activations.shape[0] // SEQ
    backward_pass = jnp.dot(cotangent, up_factor_matrix, preferred_element_type=jnp.float32)
    rank_part = jnp.dot(backward_pass, rank_sketch, precision=HI)
    rank_full = all_reduce(rank_part, "hidden")
    input_part = jnp.dot(activations, input_sketch, preferred_element_type=jnp.float32)
    rank_rows = rank_full.reshape(examples, SEQ, rank_full.shape[1])
    input_rows = input_part.reshape(examples, SEQ, input_part.shape[1])
    partial = jnp.einsum("esa,esb->eab", rank_rows, input_rows, precision=HI)
    own_a = partial.shape[1] // shards
    blocks = partial.reshape(examples, shards, own_a, -1).transpose(1, 0, 2, 3)
    own = reduce_scatter(blocks, "hidden")
    features = own.reshape(examples, -1).astype(jnp.bfloat16)
    widened = features.astype(jnp.float32)
    every = all_gather(features, "dp").reshape(-1, features.shape[1]).astype(jnp.float32)
    all_count = every.shape[0]
    weight = 1.0 / (jnp.sum(every * every, axis=0) / all_count + epsilon)
    partial_scores = jnp.dot(widened * weight, every.T, precision=HI)
    feat_total = features.shape[1] * shards
    score_blocks = partial_scores.reshape(examples, shards, -1).transpose(1, 0, 2)
    scores = reduce_scatter(score_blocks, "hidden") / math.sqrt(feat_total)
    return (features, scores)


def solution(mesh):
    placed = (
        P(("groups", "dp"), "hidden"),
        P(("groups", "dp"), "hidden"),
        P("hidden", None),
        P("hidden", None),
        P(),
    )
    return jax.shard_map(
        per_device,
        mesh=mesh,
        in_specs=placed,
        out_specs=(P(("groups", "dp"), "hidden"), P(("groups", "dp"), "hidden")),
        check_vma=False,
    )
```

time: 103 us -> 63.6 us (0.62)
  waiting for transfers between devices: 51.4 us -> 12.1 us
  starting transfers between devices: 0.08 us -> 23.4 us
  blocking collectives: 14.1 us -> 0 us
  between operations: 14.8 us -> 1.03 us
  local copies, waits for them, and re-layouts: 2.12 us -> 9.84 us
  matrix products: 18.2 us -> 16.3 us
    psum x1 -> x0, waiting for transfers between devices: 33.3 us -> none  [partial_features(): rank_full = lax.psum(rank_part, 'hidden')]
    ppermute x0 -> x15, starting transfers between devices: none -> 23.4 us  [the longest x9 15.5 us: exchange(): got.append(lax.ppermute(piece, axis, [(i, (i + d) % n) for i in range(n)]))]
    reduce_scatter x1 -> x0, waiting for transfers between devices: 18 us -> none  [per_device(): own = lax.psum_scatter(partial, 'hidden', scatter_dimension=1, tiled=True)]
    ppermute x0 -> x15, waiting for transfers between devices: none -> 12.1 us  [the longest x9 10.7 us: exchange(): got.append(lax.ppermute(piece, axis, [(i, (i + d) % n) for i in range(n)]))]
    unnamed x1 -> x0, blocking collectives: 8.87 us -> none
    dynamic_update_slice x0 -> x8, local copies, waits for them, and re-layouts: none -> 8.54 us  [the longest x6 6.4 us: all_gather(): out = lax.dynamic_update_index_in_dim(out, got, (me - d) % n, 0)]
    all_gather x1 -> x0, blocking collectives: 5.24 us -> none  [per_device(): lax.all_gather(features, 'dp', axis=0, tiled=True).astype(jnp.float32)]
    dot_general x4, matrix products: 18.1 us -> 15.8 us  [the longest x1 6.54 us: per_device(): jnp.dot(cotangent, up_factor_matrix, preferred_element_type=jnp.float32)]
  transfers between devices with their start and end apart: 2 -> 15, of which waited for: 2 -> 12; matrix products, arithmetic and copies ran while one was open for 7% -> 21% of each run, Pallas kernels for 0% -> 0%
where the time goes in v2:
time: 63.6 us; the launch traced here: 63.4 us
  starting transfers between devices  23.4 us (37%)
  matrix products  16.3 us (26%)
  waiting for transfers between devices  12.1 us (19%)
  local copies, waits for them, and re-layouts  9.84 us (15%)
  between operations  1.03 us (2%)
  other arithmetic  0.68 us (1%)
    ppermute x9, starting transfers between devices, exchange(): got.append(lax.ppermute(piece, axis, [(i, (i + d) % n) for i in range(n)]))  15.5 us
    ppermute x9, waiting for transfers between devices, exchange(): got.append(lax.ppermute(piece, axis, [(i, (i + d) % n) for i in range(n)]))  10.7 us
    ppermute x6, starting transfers between devices, all_gather(): got = lax.ppermute(x, axis, [(i, (i + d) % n) for i in range(n)])  7.93 us
    dot_general x1, matrix products, per_device(): jnp.dot(cotangent, up_factor_matrix, preferred_element_type=jnp.float32)  6.54 us
    dot_general x1, matrix products, per_device(): jnp.dot(activations, input_sketch, preferred_element_type=jnp.float32)  6.42 us
    dynamic_update_slice x6, local copies, waits for them, and re-layouts, all_gather(): out = lax.dynamic_update_index_in_dim(out, got, (me - d) % n, 0)  6.4 us
    dynamic_update_slice x2, local copies, waits for them, and re-layouts, all_gather(): out = lax.dynamic_update_index_in_dim(out, x, me, 0)  2.13 us
    dot_general x1, matrix products, per_device(): rank_part = jnp.dot(backward_pass, rank_sketch, precision=HI)  1.73 us
  transfers between devices with their start and end apart: 15, of which 12 were waited for; matrix products, arithmetic and copies ran while one was open for 21% of the time, Pallas kernels for 0%

profile of v2, /device:TPU:0, one launch (start us, length us, event | category | flops | bytes accessed | tf_op | source)
XLA Modules:
  0.0 63.4 jit_solution(15159923762347830584)
XLA Ops:
  0.7 6.5 %fusion.9 = f32[3072,64]{1,0:T(8,128)S(1)} fusion(bf16[3072,2048]{1,0:T(8,128)(2,1)} %param.6, bf16[2048,64]{0,1:T(8,128)(2,1)} %param.7), kind=kOutput, calls=%fused_computation.34 | convolution fusion | flops 805306368 | bytes 13631488 | tf_op jit(solution)/shard_map/dot_general | solution.py:51
  7.3 1.7 %fusion.10 = f32[3072,32]{0,1:T(8,128)S(1)} fusion(f32[3072,64]{1,0:T(8,128)S(1)} %fusion.9, f32[64,32]{0,1:T(8,128)S(1)} %copy-done.1), kind=kOutput, calls=%fused_computation.35 | convolution fusion | flops 75497472 | bytes 1187840 | tf_op jit(solution)/shard_map/dot_general | solution.py:52
  9.6 3.1 %collective-permute-start = (f32[768,32]{0,1:T(8,128)S(1)}, f32[768,32]{0,1:T(8,128)S(1)}, u32[]{:S(2)}, u32[]{:S(2)}) collective-permute-start(f32[768,32]{0,1:T(8,128)S(1)} %bitcast.81), channel_id=1, source_target_pairs={{0,1},{1,2},{2,3},{3,0},{4,5},{5,6},{6,7},{7,4},{8,9},{9,10},{10,1... | collective-permute-start | bytes 294920 | tf_op jit(solution)/shard_map/ppermute | solution.py:19
  12.7 2.6 %collective-permute-start.1 = (f32[768,32]{0,1:T(8,128)S(1)}, f32[768,32]{0,1:T(8,128)S(1)}, u32[]{:S(2)}, u32[]{:S(2)}) collective-permute-start(f32[768,32]{0,1:T(8,128)S(1)} %bitcast.82), channel_id=1, source_target_pairs={{0,2},{1,3},{2,0},{3,1},{4,6},{5,7},{6,4},{7,5},{8,10},{9,11},{10,... | collective-permute-start | bytes 294920 | tf_op jit(solution)/shard_map/ppermute | solution.py:19
  15.3 1.4 %collective-permute-start.2 = (f32[768,32]{0,1:T(8,128)S(1)}, f32[768,32]{0,1:T(8,128)S(1)}, u32[]{:S(2)}, u32[]{:S(2)}) collective-permute-start(f32[768,32]{0,1:T(8,128)S(1)} %bitcast.83), channel_id=1, source_target_pairs={{0,3},{1,0},{2,1},{3,2},{4,7},{5,4},{6,5},{7,6},{8,11},{9,8},{10,9... | collective-permute-start | bytes 294920 | tf_op jit(solution)/shard_map/ppermute | solution.py:19
  16.7 1.6 %collective-permute-done = f32[768,32]{0,1:T(8,128)S(1)} collective-permute-done((f32[768,32]{0,1:T(8,128)S(1)}, f32[768,32]{0,1:T(8,128)S(1)}, u32[]{:S(2)}, u32[]{:S(2)}) %collective-permute-start) | collective-permute-done | bytes 98336 | tf_op jit(solution)/shard_map/ppermute | solution.py:19
  18.3 3.6 %collective-permute-done.1 = f32[768,32]{0,1:T(8,128)S(1)} collective-permute-done((f32[768,32]{0,1:T(8,128)S(1)}, f32[768,32]{0,1:T(8,128)S(1)}, u32[]{:S(2)}, u32[]{:S(2)}) %collective-permute-start.1) | collective-permute-done | bytes 98336 | tf_op jit(solution)/shard_map/ppermute | solution.py:19
  22.0 2.5 %collective-permute-start.3 = (f32[768,32]{0,1:T(8,128)S(1)}, f32[768,32]{0,1:T(8,128)S(1)}, u32[]{:S(2)}, u32[]{:S(2)}) collective-permute-start(f32[768,32]{0,1:T(8,128)S(1)} %fusion.2), channel_id=1, source_target_pairs={{0,1},{1,2},{2,3},{3,0},{4,5},{5,6},{6,7},{7,4},{8,9},{9,10},{10,1... | collective-permute-start | bytes 294920 | tf_op jit(solution)/shard_map/ppermute | solution.py:37
  24.5 1.6 %collective-permute-start.4 = (f32[768,32]{0,1:T(8,128)S(1)}, f32[768,32]{0,1:T(8,128)S(1)}, u32[]{:S(2)}, u32[]{:S(2)}) collective-permute-start(f32[768,32]{0,1:T(8,128)S(1)} %fusion.2), channel_id=1, source_target_pairs={{0,2},{1,3},{2,0},{3,1},{4,6},{5,7},{6,4},{7,5},{8,10},{9,11},{10,... | collective-permute-start | bytes 294920 | tf_op jit(solution)/shard_map/ppermute | solution.py:37
  26.2 0.8 %collective-permute-start.5 = (f32[768,32]{0,1:T(8,128)S(1)}, f32[768,32]{0,1:T(8,128)S(1)}, u32[]{:S(2)}, u32[]{:S(2)}) collective-permute-start(f32[768,32]{0,1:T(8,128)S(1)} %fusion.2), channel_id=1, source_target_pairs={{0,3},{1,0},{2,1},{3,2},{4,7},{5,4},{6,5},{7,6},{8,11},{9,8},{10,9... | collective-permute-start | bytes 294920 | tf_op jit(solution)/shard_map/ppermute | solution.py:37
  27.0 6.4 %fusion.11 = f32[3072,128]{1,0:T(8,128)S(1)} fusion(bf16[3072,2048]{1,0:T(8,128)(2,1)} %param.5, bf16[2048,128]{1,0:T(8,128)(2,1)S(1)} %copy-done), kind=kOutput, calls=%fused_computation.36 | convolution fusion | flops 1610612736 | bytes 14680064 | tf_op jit(solution)/shard_map/dot_general | solution.py:54
  33.6 2.1 %dynamic_update_slice.26 = f32[4,768,32]{1,0,2:T(4,128)S(1)} dynamic-update-slice(f32[4,768,32]{1,0,2:T(4,128)S(1)} %broadcast_in_dim.31, f32[1,768,32]{1,0,2:T(1,128)S(1)} %copy.7, s32[]{:T(128)S(6)} %select_n.98, s32[]{:T(128)} %constant.129.clone.1, s32[]{:T(128)} %constant.129.clone.1) | dynamic-update-slice | bytes 196612 | tf_op jit(solution)/shard_map/jit(dynamic_update_index_in_dim)/dynamic_update_slice | solution.py:35
  36.0 2.1 %dynamic_update_slice.27 = f32[4,768,32]{1,0,2:T(4,128)S(1)} dynamic-update-slice(f32[4,768,32]{1,0,2:T(4,128)S(1)} %dynamic_update_slice.26, f32[1,768,32]{1,0,2:T(1,128)S(1)} %copy.8, s32[]{:T(128)S(6)} %select_n.106, s32[]{:T(128)} %constant.129.clone.1, s32[]{:T(128)} %constant.129.clone.1) | dynamic-update-slice | bytes 196612 | tf_op jit(solution)/shard_map/jit(dynamic_update_index_in_dim)/dynamic_update_slice | solution.py:38
  38.1 2.1 %dynamic_update_slice.28 = f32[4,768,32]{1,0,2:T(4,128)S(1)} dynamic-update-slice(f32[4,768,32]{1,0,2:T(4,128)S(1)} %dynamic_update_slice.27, f32[1,768,32]{1,0,2:T(1,128)S(1)} %copy.9, s32[]{:T(128)S(6)} %select_n.108, s32[]{:T(128)} %constant.129.clone.1, s32[]{:T(128)} %constant.129.clone.1) | dynamic-update-slice | bytes 196612 | tf_op jit(solution)/shard_map/jit(dynamic_update_index_in_dim)/dynamic_update_slice | solution.py:38
  40.4 2.1 %dynamic_update_slice.29 = f32[4,768,32]{1,0,2:T(4,128)S(1)} dynamic-update-slice(f32[4,768,32]{1,0,2:T(4,128)S(1)} %dynamic_update_slice.28, f32[1,768,32]{1,0,2:T(1,128)S(1)} %broadcast_in_dim.35, s32[]{:T(128)S(6)} %select_n.110, s32[]{:T(128)} %constant.129.clone.1, s32[]{:T(128)} %constant.129.clone.1) | dynamic-update-slice | bytes 196612 | tf_op jit(solution)/shard_map/jit(dynamic_update_index_in_dim)/dynamic_update_slice | solution.py:38
  42.7 1.1 %convolution_bitcast_fusion = f32[6,4,8,128]{3,2,1,0:T(8,128)S(1)} fusion(f32[6,512,128]{2,1,0:T(8,128)S(1)} %bitcast.76, f32[6,512,32]{1,0,2:T(8,128)S(1)} %reshape_reshape.3), kind=kOutput, calls=%fused_computation | convolution fusion | flops 150994944 | bytes 2064384 | tf_op jit(solution)/shard_map/esa,esb->eab/dot_general | solution.py:57
  43.8 1.3 %collective-permute-start.6 = (f32[6,8,128]{2,1,0:T(8,128)S(1)}, f32[6,8,128]{2,1,0:T(8,128)S(1)}, u32[]{:S(2)}, u32[]{:S(2)}) collective-permute-start(f32[6,8,128]{2,1,0:T(8,128)S(1)} %get-tuple-element.6), channel_id=1, source_target_pairs={{0,1},{1,2},{2,3},{3,0},{4,5},{5,6},{6,7},{7,4},{8,9},{9,10},{10,1... | collective-permute-start | bytes 73736 | tf_op jit(solution)/shard_map/ppermute | solution.py:19
  45.1 1.3 %collective-permute-start.7 = (f32[6,8,128]{2,1,0:T(8,128)S(1)}, f32[6,8,128]{2,1,0:T(8,128)S(1)}, u32[]{:S(2)}, u32[]{:S(2)}) collective-permute-start(f32[6,8,128]{2,1,0:T(8,128)S(1)} %get-tuple-element.8), channel_id=1, source_target_pairs={{0,2},{1,3},{2,0},{3,1},{4,6},{5,7},{6,4},{7,5},{8,10},{9,11},{10,... | collective-permute-start | bytes 73736 | tf_op jit(solution)/shard_map/ppermute | solution.py:19
  46.4 1.4 %collective-permute-start.8 = (f32[6,8,128]{2,1,0:T(8,128)S(1)}, f32[6,8,128]{2,1,0:T(8,128)S(1)}, u32[]{:S(2)}, u32[]{:S(2)}) collective-permute-start(f32[6,8,128]{2,1,0:T(8,128)S(1)} %get-tuple-element.7), channel_id=1, source_target_pairs={{0,3},{1,0},{2,1},{3,2},{4,7},{5,4},{6,5},{7,6},{8,11},{9,8},{10,9... | collective-permute-start | bytes 73736 | tf_op jit(solution)/shard_map/ppermute | solution.py:19
  47.8 1.8 %collective-permute-done.6 = f32[6,8,128]{2,1,0:T(8,128)S(1)} collective-permute-done((f32[6,8,128]{2,1,0:T(8,128)S(1)}, f32[6,8,128]{2,1,0:T(8,128)S(1)}, u32[]{:S(2)}, u32[]{:S(2)}) %collective-permute-start.6) | collective-permute-done | bytes 24608 | tf_op jit(solution)/shard_map/ppermute | solution.py:19
  49.6 0.7 %collective-permute-done.7 = f32[6,8,128]{2,1,0:T(8,128)S(1)} collective-permute-done((f32[6,8,128]{2,1,0:T(8,128)S(1)}, f32[6,8,128]{2,1,0:T(8,128)S(1)}, u32[]{:S(2)}, u32[]{:S(2)}) %collective-permute-start.7) | collective-permute-done | bytes 24608 | tf_op jit(solution)/shard_map/ppermute | solution.py:19
  50.6 1.6 %collective-permute-start.10 = (bf16[6,1024]{1,0:T(8,128)(2,1)S(1)}, bf16[6,1024]{1,0:T(8,128)(2,1)S(1)}, u32[]{:S(2)}, u32[]{:S(2)}) collective-permute-start(bf16[6,1024]{1,0:T(8,128)(2,1)S(1)} %bitcast.85), channel_id=1, source_target_pairs={{0,8},{4,12},{8,0},{12,4},{1,9},{5,13},{9,1},{13,5},{2,10},{6,14},... | collective-permute-start | bytes 36872 | tf_op jit(solution)/shard_map/ppermute | solution.py:37
  52.2 1.4 %collective-permute-start.11 = (bf16[6,1024]{1,0:T(8,128)(2,1)S(1)}, bf16[6,1024]{1,0:T(8,128)(2,1)S(1)}, u32[]{:S(2)}, u32[]{:S(2)}) collective-permute-start(bf16[6,1024]{1,0:T(8,128)(2,1)S(1)} %bitcast.86), channel_id=1, source_target_pairs={{0,12},{4,0},{8,4},{12,8},{1,13},{5,1},{9,5},{13,9},{2,14},{6,2},{... | collective-permute-start | bytes 36872 | tf_op jit(solution)/shard_map/ppermute | solution.py:37
  53.8 0.7 %collective-permute-done.10 = bf16[6,1024]{1,0:T(8,128)(2,1)S(1)} collective-permute-done((bf16[6,1024]{1,0:T(8,128)(2,1)S(1)}, bf16[6,1024]{1,0:T(8,128)(2,1)S(1)}, u32[]{:S(2)}, u32[]{:S(2)}) %collective-permute-start.10) | collective-permute-done | bytes 12320 | tf_op jit(solution)/shard_map/ppermute | solution.py:37
  54.4 0.6 collective-permute-done.11
  55.6 1.7 %collective-permute-start.12 = (f32[6,6]{1,0:T(8,128)S(1)}, f32[6,6]{1,0:T(8,128)S(1)}, u32[]{:S(2)}, u32[]{:S(2)}) collective-permute-start(f32[6,6]{1,0:T(8,128)S(1)} %get-tuple-element.9), channel_id=1, source_target_pairs={{0,1},{1,2},{2,3},{3,0},{4,5},{5,6},{6,7},{7,4},{8,9},{9,10},{10,1... | collective-permute-start | bytes 440 | tf_op jit(solution)/shard_map/ppermute | solution.py:19
  57.3 1.9 %collective-permute-start.13 = (f32[6,6]{1,0:T(8,128)S(1)}, f32[6,6]{1,0:T(8,128)S(1)}, u32[]{:S(2)}, u32[]{:S(2)}) collective-permute-start(f32[6,6]{1,0:T(8,128)S(1)} %get-tuple-element.11), channel_id=1, source_target_pairs={{0,2},{1,3},{2,0},{3,1},{4,6},{5,7},{6,4},{7,5},{8,10},{9,11},{10,... | collective-permute-start | bytes 440 | tf_op jit(solution)/shard_map/ppermute | solution.py:19
  59.2 0.8 %collective-permute-start.14 = (f32[6,6]{1,0:T(8,128)S(1)}, f32[6,6]{1,0:T(8,128)S(1)}, u32[]{:S(2)}, u32[]{:S(2)}) collective-permute-start(f32[6,6]{1,0:T(8,128)S(1)} %get-tuple-element.10), channel_id=1, source_target_pairs={{0,3},{1,0},{2,1},{3,2},{4,7},{5,4},{6,5},{7,6},{8,11},{9,8},{10,9... | collective-permute-start | bytes 440 | tf_op jit(solution)/shard_map/ppermute | solution.py:19
  60.0 1.0 %collective-permute-done.12 = f32[6,6]{1,0:T(8,128)S(1)} collective-permute-done((f32[6,6]{1,0:T(8,128)S(1)}, f32[6,6]{1,0:T(8,128)S(1)}, u32[]{:S(2)}, u32[]{:S(2)}) %collective-permute-start.12) | collective-permute-done | bytes 176 | tf_op jit(solution)/shard_map/ppermute | solution.py:19
  61.1 0.8 %collective-permute-done.13 = f32[6,6]{1,0:T(8,128)S(1)} collective-permute-done((f32[6,6]{1,0:T(8,128)S(1)}, f32[6,6]{1,0:T(8,128)S(1)}, u32[]{:S(2)}, u32[]{:S(2)}) %collective-permute-start.13) | collective-permute-done | bytes 176 | tf_op jit(solution)/shard_map/ppermute | solution.py:19
  61.8 1.0 %collective-permute-done.14 = f32[6,6]{1,0:T(8,128)S(1)} collective-permute-done((f32[6,6]{1,0:T(8,128)S(1)}, f32[6,6]{1,0:T(8,128)S(1)}, u32[]{:S(2)}, u32[]{:S(2)}) %collective-permute-start.14) | collective-permute-done | bytes 176 | tf_op jit(solution)/shard_map/ppermute | solution.py:19
  62.8 0.6 fusion.8
  (40 shorter events, 2.4 us)
Async XLA Ops:
  0.6 26.3 %copy-start = (bf16[2048,128]{1,0:T(8,128)(2,1)S(1)}, bf16[2048,128]{1,0:T(8,128)(2,1)}, u32[]{:S(2)}) copy-start(bf16[2048,128]{1,0:T(8,128)(2,1)} %param.8) | copy-start | bytes 1572868
  0.7 6.6 %copy-start.1 = (f32[64,32]{0,1:T(8,128)S(1)}, f32[64,32]{0,1:T(8,128)}, u32[]{:S(2)}) copy-start(f32[64,32]{0,1:T(8,128)} %param.9) | copy-start | bytes 24580
  9.6 8.7 %collective-permute-start = (f32[768,32]{0,1:T(8,128)S(1)}, f32[768,32]{0,1:T(8,128)S(1)}, u32[]{:S(2)}, u32[]{:S(2)}) collective-permute-start(f32[768,32]{0,1:T(8,128)S(1)} %bitcast.81), channel_id=1, source_target_pairs={{0,1},{1,2},{2,3},{3,0},{4,5},{5,6},{6,7},{7,4},{8,9},{9,10},{10,1... | collective-permute-start | bytes 294920 | tf_op jit(solution)/shard_map/ppermute | solution.py:19
  12.7 9.2 %collective-permute-start.1 = (f32[768,32]{0,1:T(8,128)S(1)}, f32[768,32]{0,1:T(8,128)S(1)}, u32[]{:S(2)}, u32[]{:S(2)}) collective-permute-start(f32[768,32]{0,1:T(8,128)S(1)} %bitcast.82), channel_id=1, source_target_pairs={{0,2},{1,3},{2,0},{3,1},{4,6},{5,7},{6,4},{7,5},{8,10},{9,11},{10,... | collective-permute-start | bytes 294920 | tf_op jit(solution)/shard_map/ppermute | solution.py:19
  15.3 6.7 %collective-permute-start.2 = (f32[768,32]{0,1:T(8,128)S(1)}, f32[768,32]{0,1:T(8,128)S(1)}, u32[]{:S(2)}, u32[]{:S(2)}) collective-permute-start(f32[768,32]{0,1:T(8,128)S(1)} %bitcast.83), channel_id=1, source_target_pairs={{0,3},{1,0},{2,1},{3,2},{4,7},{5,4},{6,5},{7,6},{8,11},{9,8},{10,9... | collective-permute-start | bytes 294920 | tf_op jit(solution)/shard_map/ppermute | solution.py:19
  22.0 13.7 %collective-permute-start.3 = (f32[768,32]{0,1:T(8,128)S(1)}, f32[768,32]{0,1:T(8,128)S(1)}, u32[]{:S(2)}, u32[]{:S(2)}) collective-permute-start(f32[768,32]{0,1:T(8,128)S(1)} %fusion.2), channel_id=1, source_target_pairs={{0,1},{1,2},{2,3},{3,0},{4,5},{5,6},{6,7},{7,4},{8,9},{9,10},{10,1... | collective-permute-start | bytes 294920 | tf_op jit(solution)/shard_map/ppermute | solution.py:37
  24.5 11.4 %collective-permute-start.4 = (f32[768,32]{0,1:T(8,128)S(1)}, f32[768,32]{0,1:T(8,128)S(1)}, u32[]{:S(2)}, u32[]{:S(2)}) collective-permute-start(f32[768,32]{0,1:T(8,128)S(1)} %fusion.2), channel_id=1, source_target_pairs={{0,2},{1,3},{2,0},{3,1},{4,6},{5,7},{6,4},{7,5},{8,10},{9,11},{10,... | collective-permute-start | bytes 294920 | tf_op jit(solution)/shard_map/ppermute | solution.py:37
  26.2 14.1 %collective-permute-start.5 = (f32[768,32]{0,1:T(8,128)S(1)}, f32[768,32]{0,1:T(8,128)S(1)}, u32[]{:S(2)}, u32[]{:S(2)}) collective-permute-start(f32[768,32]{0,1:T(8,128)S(1)} %fusion.2), channel_id=1, source_target_pairs={{0,3},{1,0},{2,1},{3,2},{4,7},{5,4},{6,5},{7,6},{8,11},{9,8},{10,9... | collective-permute-start | bytes 294920 | tf_op jit(solution)/shard_map/ppermute | solution.py:37
  43.8 5.8 %collective-permute-start.6 = (f32[6,8,128]{2,1,0:T(8,128)S(1)}, f32[6,8,128]{2,1,0:T(8,128)S(1)}, u32[]{:S(2)}, u32[]{:S(2)}) collective-permute-start(f32[6,8,128]{2,1,0:T(8,128)S(1)} %get-tuple-element.6), channel_id=1, source_target_pairs={{0,1},{1,2},{2,3},{3,0},{4,5},{5,6},{6,7},{7,4},{8,9},{9,10},{10,1... | collective-permute-start | bytes 73736 | tf_op jit(solution)/shard_map/ppermute | solution.py:19
  45.1 5.2 %collective-permute-start.7 = (f32[6,8,128]{2,1,0:T(8,128)S(1)}, f32[6,8,128]{2,1,0:T(8,128)S(1)}, u32[]{:S(2)}, u32[]{:S(2)}) collective-permute-start(f32[6,8,128]{2,1,0:T(8,128)S(1)} %get-tuple-element.8), channel_id=1, source_target_pairs={{0,2},{1,3},{2,0},{3,1},{4,6},{5,7},{6,4},{7,5},{8,10},{9,11},{10,... | collective-permute-start | bytes 73736 | tf_op jit(solution)/shard_map/ppermute | solution.py:19
  46.4 4.0 %collective-permute-start.8 = (f32[6,8,128]{2,1,0:T(8,128)S(1)}, f32[6,8,128]{2,1,0:T(8,128)S(1)}, u32[]{:S(2)}, u32[]{:S(2)}) collective-permute-start(f32[6,8,128]{2,1,0:T(8,128)S(1)} %get-tuple-element.7), channel_id=1, source_target_pairs={{0,3},{1,0},{2,1},{3,2},{4,7},{5,4},{6,5},{7,6},{8,11},{9,8},{10,9... | collective-permute-start | bytes 73736 | tf_op jit(solution)/shard_map/ppermute | solution.py:19
  50.5 12.9 %copy-start.2 = (bf16[1,6,8,128]{3,1,2,0:T(8,128)(2,1)}, bf16[1,6,8,128]{3,1,2,0:T(8,128)(2,1)S(1)}, u32[]{:S(2)}) copy-start(bf16[1,6,8,128]{3,1,2,0:T(8,128)(2,1)S(1)} %copy.26) | copy-start | bytes 36868
  50.5 3.2 %collective-permute-start.9 = (bf16[6,1024]{1,0:T(8,128)(2,1)S(1)}, bf16[6,1024]{1,0:T(8,128)(2,1)S(1)}, u32[]{:S(2)}, u32[]{:S(2)}) collective-permute-start(bf16[6,1024]{1,0:T(8,128)(2,1)S(1)} %bitcast.84), channel_id=1, source_target_pairs={{0,4},{4,8},{8,12},{12,0},{1,5},{5,9},{9,13},{13,1},{2,6},{6,10},{... | collective-permute-start | bytes 36872 | tf_op jit(solution)/shard_map/ppermute | solution.py:37
  50.6 3.8 %collective-permute-start.10 = (bf16[6,1024]{1,0:T(8,128)(2,1)S(1)}, bf16[6,1024]{1,0:T(8,128)(2,1)S(1)}, u32[]{:S(2)}, u32[]{:S(2)}) collective-permute-start(bf16[6,1024]{1,0:T(8,128)(2,1)S(1)} %bitcast.85), channel_id=1, source_target_pairs={{0,8},{4,12},{8,0},{12,4},{1,9},{5,13},{9,1},{13,5},{2,10},{6,14},... | collective-permute-start | bytes 36872 | tf_op jit(solution)/shard_map/ppermute | solution.py:37
  52.2 2.8 %collective-permute-start.11 = (bf16[6,1024]{1,0:T(8,128)(2,1)S(1)}, bf16[6,1024]{1,0:T(8,128)(2,1)S(1)}, u32[]{:S(2)}, u32[]{:S(2)}) collective-permute-start(bf16[6,1024]{1,0:T(8,128)(2,1)S(1)} %bitcast.86), channel_id=1, source_target_pairs={{0,12},{4,0},{8,4},{12,8},{1,13},{5,1},{9,5},{13,9},{2,14},{6,2},{... | collective-permute-start | bytes 36872 | tf_op jit(solution)/shard_map/ppermute | solution.py:37
  55.6 5.4 %collective-permute-start.12 = (f32[6,6]{1,0:T(8,128)S(1)}, f32[6,6]{1,0:T(8,128)S(1)}, u32[]{:S(2)}, u32[]{:S(2)}) collective-permute-start(f32[6,6]{1,0:T(8,128)S(1)} %get-tuple-element.9), channel_id=1, source_target_pairs={{0,1},{1,2},{2,3},{3,0},{4,5},{5,6},{6,7},{7,4},{8,9},{9,10},{10,1... | collective-permute-start | bytes 440 | tf_op jit(solution)/shard_map/ppermute | solution.py:19
  57.3 4.5 %collective-permute-start.13 = (f32[6,6]{1,0:T(8,128)S(1)}, f32[6,6]{1,0:T(8,128)S(1)}, u32[]{:S(2)}, u32[]{:S(2)}) collective-permute-start(f32[6,6]{1,0:T(8,128)S(1)} %get-tuple-element.11), channel_id=1, source_target_pairs={{0,2},{1,3},{2,0},{3,1},{4,6},{5,7},{6,4},{7,5},{8,10},{9,11},{10,... | collective-permute-start | bytes 440 | tf_op jit(solution)/shard_map/ppermute | solution.py:19
  59.2 3.6 %collective-permute-start.14 = (f32[6,6]{1,0:T(8,128)S(1)}, f32[6,6]{1,0:T(8,128)S(1)}, u32[]{:S(2)}, u32[]{:S(2)}) collective-permute-start(f32[6,6]{1,0:T(8,128)S(1)} %get-tuple-element.10), channel_id=1, source_target_pairs={{0,3},{1,0},{2,1},{3,2},{4,7},{5,4},{6,5},{7,6},{8,11},{9,8},{10,9... | collective-permute-start | bytes 440 | tf_op jit(solution)/shard_map/ppermute | solution.py:19

commit v3 on v2

--- a/solution.py
+++ b/solution.py
@@ -47,17 +47,25 @@
 
 def per_device(activations, cotangent, up_factor_matrix, input_sketch, rank_sketch):
     shards = lax.axis_size("hidden")
+    me = lax.axis_index("hidden")
     examples = activations.shape[0] // SEQ
-    backward_pass = jnp.dot(cotangent, up_factor_matrix, preferred_element_type=jnp.float32)
-    rank_part = jnp.dot(backward_pass, rank_sketch, precision=HI)
-    rank_full = all_reduce(rank_part, "hidden")
+    backward_t = lax.dot_general(up_factor_matrix, cotangent, (((0,), (1,)), ((), ())),
+                                 preferred_element_type=jnp.float32)
+    rank_t = lax.dot_general(rank_sketch, backward_t, (((0,), (0,)), ((), ())), precision=HI)
+    own_a = rank_t.shape[0] // shards
+    rank_own = reduce_scatter(rank_t.reshape(shards, own_a, -1), "hidden")
     input_part = jnp.dot(activations, input_sketch, preferred_element_type=jnp.float32)
-    rank_rows = rank_full.reshape(examples, SEQ, rank_full.shape[1])
     input_rows = input_part.reshape(examples, SEQ, input_part.shape[1])
-    partial = jnp.einsum("esa,esb->eab", rank_rows, input_rows, precision=HI)
-    own_a = partial.shape[1] // shards
-    blocks = partial.reshape(examples, shards, own_a, -1).transpose(1, 0, 2, 3)
-    own = reduce_scatter(blocks, "hidden")
+
+    def outer(rank_block):
+        rows = rank_block.reshape(own_a, examples, SEQ)
+        return jnp.einsum("aes,esb->eab", rows, input_rows, precision=HI)
+
+    own = outer(rank_own)
+    for d in range(1, shards):
+        visiting = lax.ppermute(rank_own, "hidden", [(i, (i + d) % shards) for i in range(shards)])
+        back = [(i, (i - d) % shards) for i in range(shards)]
+        own = own + lax.ppermute(outer(visiting), "hidden", back)
     features = own.reshape(examples, -1).astype(jnp.bfloat16)
     widened = features.astype(jnp.float32)
     every = all_gather(features, "dp").reshape(-1, features.shape[1]).astype(jnp.float32)

time: 63.6 us -> 60.2 us (0.947)
  local copies, waits for them, and re-layouts: 9.84 us -> 0.14 us
  matrix products: 16.3 us -> 19.6 us
  starting transfers between devices: 23.4 us -> 26.4 us
    ppermute x0 -> x6, starting transfers between devices: none -> 11.7 us  [the longest x3 6.64 us: per_device(): own = own + lax.ppermute(outer(visiting), 'hidden', back)]
    dynamic_update_slice x6 -> x3, local copies, waits for them, and re-layouts: 6.4 us -> 0.01 us  [all_gather(): out = lax.dynamic_update_index_in_dim(out, got, (me - d) % n, 0)]
    ppermute x6 -> x3, starting transfers between devices: 7.93 us -> 3.03 us  [all_gather(): got = lax.ppermute(x, axis, [(i, (i + d) % n) for i in range(n)])]
    ppermute x9 -> x6, starting transfers between devices: 15.5 us -> 11.7 us  [exchange(): got.append(lax.ppermute(piece, axis, [(i, (i + d) % n) for i in range(n)]))]
    ppermute x0 -> x6, waiting for transfers between devices: none -> 3.68 us  [the longest x3 2.02 us: per_device(): lax.ppermute(rank_own, 'hidden', [(i, (i + d) % shards) for i in range(sh...]
    ppermute x9 -> x6, waiting for transfers between devices: 10.7 us -> 7.35 us  [exchange(): got.append(lax.ppermute(piece, axis, [(i, (i + d) % n) for i in range(n)]))]
    dot_general x3 -> x6, matrix products: 9.35 us -> 12.6 us  [the longest x1 8.64 us: per_device(): lax.dot_general(up_factor_matrix, cotangent, (((0,), (1,)), ((), ())), pr...]
    dynamic_update_slice x2 -> x1, local copies, waits for them, and re-layouts: 2.13 us -> 0.01 us  [all_gather(): out = lax.dynamic_update_index_in_dim(out, x, me, 0)]
  transfers between devices with their start and end apart: 15 -> 15, of which waited for: 12 -> 9; matrix products, arithmetic and copies ran while one was open for 21% -> 15% of each run, Pallas kernels for 0% -> 0%
where the time goes in v3:
time: 60.2 us; the launch traced here: 60 us
  starting transfers between devices  26.4 us (44%)
  matrix products  19.6 us (33%)
  waiting for transfers between devices  12.5 us (21%)
  between operations  0.82 us (1%)
  other arithmetic  0.66 us (1%)
    ppermute x6, starting transfers between devices, exchange(): got.append(lax.ppermute(piece, axis, [(i, (i + d) % n) for i in range(n)]))  11.7 us
    dot_general x1, matrix products, per_device(): lax.dot_general(up_factor_matrix, cotangent, (((0,), (1,)), ((), ())), pr...  8.64 us
    ppermute x6, waiting for transfers between devices, exchange(): got.append(lax.ppermute(piece, axis, [(i, (i + d) % n) for i in range(n)]))  7.35 us
    ppermute x3, starting transfers between devices, per_device(): own = own + lax.ppermute(outer(visiting), 'hidden', back)  6.64 us
    dot_general x1, matrix products, per_device(): jnp.dot(activations, input_sketch, preferred_element_type=jnp.float32)  6.43 us
    ppermute x3, starting transfers between devices, per_device(): lax.ppermute(rank_own, 'hidden', [(i, (i + d) % shards) for i in range(sh...  5.04 us
    dot_general x4, matrix products, outer(): return jnp.einsum('aes,esb->eab', rows, input_rows, precision=HI)  3.42 us
    ppermute x3, starting transfers between devices, all_gather(): got = lax.ppermute(x, axis, [(i, (i + d) % n) for i in range(n)])  3.03 us
  transfers between devices with their start and end apart: 15, of which 9 were waited for; matrix products, arithmetic and copies ran while one was open for 15% of the time, Pallas kernels for 0%

profile of v3, /device:TPU:0, one launch (start us, length us, event | category | flops | bytes accessed | tf_op | source)
XLA Modules:
  0.0 60.0 jit_solution(13058355314221678437)
XLA Ops:
  0.7 8.6 %fusion.8 = f32[64,3072]{1,0:T(8,128)S(1)} fusion(bf16[2048,64]{0,1:T(8,128)(2,1)} %param.7, bf16[3072,2048]{1,0:T(8,128)(2,1)} %param.6), kind=kOutput, calls=%fused_computation.26 | convolution fusion | flops 805306368 | bytes 13631488 | tf_op jit(solution)/shard_map/dot_general | solution.py:52
  9.3 0.6 convolution_bitcast_fusion
  9.9 3.1 %collective-permute-start = (f32[8,3072]{1,0:T(8,128)S(1)}, f32[8,3072]{1,0:T(8,128)S(1)}, u32[]{:S(2)}, u32[]{:S(2)}) collective-permute-start(f32[8,3072]{1,0:T(8,128)S(1)} %get-tuple-element.2), channel_id=1, source_target_pairs={{0,1},{1,2},{2,3},{3,0},{4,5},{5,6},{6,7},{7,4},{8,9},{9,10},{10,1... | collective-permute-start | bytes 294920 | tf_op jit(solution)/shard_map/ppermute | solution.py:19
  13.1 2.6 %collective-permute-start.1 = (f32[8,3072]{1,0:T(8,128)S(1)}, f32[8,3072]{1,0:T(8,128)S(1)}, u32[]{:S(2)}, u32[]{:S(2)}) collective-permute-start(f32[8,3072]{1,0:T(8,128)S(1)} %get-tuple-element.4), channel_id=1, source_target_pairs={{0,2},{1,3},{2,0},{3,1},{4,6},{5,7},{6,4},{7,5},{8,10},{9,11},{10,... | collective-permute-start | bytes 294920 | tf_op jit(solution)/shard_map/ppermute | solution.py:19
  15.6 1.3 %collective-permute-start.2 = (f32[8,3072]{1,0:T(8,128)S(1)}, f32[8,3072]{1,0:T(8,128)S(1)}, u32[]{:S(2)}, u32[]{:S(2)}) collective-permute-start(f32[8,3072]{1,0:T(8,128)S(1)} %get-tuple-element.3), channel_id=1, source_target_pairs={{0,3},{1,0},{2,1},{3,2},{4,7},{5,4},{6,5},{7,6},{8,11},{9,8},{10,9... | collective-permute-start | bytes 294920 | tf_op jit(solution)/shard_map/ppermute | solution.py:19
  17.0 1.7 %collective-permute-done = f32[8,3072]{1,0:T(8,128)S(1)} collective-permute-done((f32[8,3072]{1,0:T(8,128)S(1)}, f32[8,3072]{1,0:T(8,128)S(1)}, u32[]{:S(2)}, u32[]{:S(2)}) %collective-permute-start) | collective-permute-done | bytes 98336 | tf_op jit(solution)/shard_map/ppermute | solution.py:19
  18.7 3.5 %collective-permute-done.1 = f32[8,3072]{1,0:T(8,128)S(1)} collective-permute-done((f32[8,3072]{1,0:T(8,128)S(1)}, f32[8,3072]{1,0:T(8,128)S(1)}, u32[]{:S(2)}, u32[]{:S(2)}) %collective-permute-start.1) | collective-permute-done | bytes 98336 | tf_op jit(solution)/shard_map/ppermute | solution.py:19
  22.3 2.6 %collective-permute-start.3 = (f32[8,3072]{1,0:T(8,128)S(1)}, f32[8,3072]{1,0:T(8,128)S(1)}, u32[]{:S(2)}, u32[]{:S(2)}) collective-permute-start(f32[8,3072]{1,0:T(8,128)S(1)} %fusion.4), channel_id=1, source_target_pairs={{0,1},{1,2},{2,3},{3,0},{4,5},{5,6},{6,7},{7,4},{8,9},{9,10},{10,1... | collective-permute-start | bytes 294920 | tf_op jit(solution)/shard_map/ppermute | solution.py:66
  24.9 6.4 %fusion.9 = f32[3072,128]{1,0:T(8,128)S(1)} fusion(bf16[3072,2048]{1,0:T(8,128)(2,1)} %param.5, bf16[2048,128]{1,0:T(8,128)(2,1)S(1)} %copy-done), kind=kOutput, calls=%fused_computation.27 | convolution fusion | flops 1610612736 | bytes 14680064 | tf_op jit(solution)/shard_map/dot_general | solution.py:57
  31.3 1.7 %collective-permute-start.5 = (f32[8,3072]{1,0:T(8,128)S(1)}, f32[8,3072]{1,0:T(8,128)S(1)}, u32[]{:S(2)}, u32[]{:S(2)}) collective-permute-start(f32[8,3072]{1,0:T(8,128)S(1)} %fusion.4), channel_id=1, source_target_pairs={{0,2},{1,3},{2,0},{3,1},{4,6},{5,7},{6,4},{7,5},{8,10},{9,11},{10,... | collective-permute-start | bytes 294920 | tf_op jit(solution)/shard_map/ppermute | solution.py:66
  33.0 0.8 %collective-permute-start.7 = (f32[8,3072]{1,0:T(8,128)S(1)}, f32[8,3072]{1,0:T(8,128)S(1)}, u32[]{:S(2)}, u32[]{:S(2)}) collective-permute-start(f32[8,3072]{1,0:T(8,128)S(1)} %fusion.4), channel_id=1, source_target_pairs={{0,3},{1,0},{2,1},{3,2},{4,7},{5,4},{6,5},{7,6},{8,11},{9,8},{10,9... | collective-permute-start | bytes 294920 | tf_op jit(solution)/shard_map/ppermute | solution.py:66
  33.8 0.9 %fusion.10 = f32[6,8,128]{2,1,0:T(8,128)S(1)} fusion(f32[8,6,512]{2,0,1:T(8,128)S(1)} %bitcast.71, f32[6,512,128]{2,1,0:T(8,128)S(1)} %bitcast.63), kind=kOutput, calls=%fused_computation.28 | convolution fusion | flops 37748736 | bytes 1695744 | tf_op jit(solution)/shard_map/aes,esb->eab/dot_general | solution.py:62
  34.6 2.1 %collective-permute-start.4 = (f32[6,8,128]{2,1,0:T(8,128)S(1)}, f32[6,8,128]{2,1,0:T(8,128)S(1)}, u32[]{:S(2)}, u32[]{:S(2)}) collective-permute-start(f32[6,8,128]{2,1,0:T(8,128)S(1)} %fusion.10), channel_id=1, source_target_pairs={{0,3},{1,0},{2,1},{3,2},{4,7},{5,4},{6,5},{7,6},{8,11},{9,8},{10,9... | collective-permute-start | bytes 73736 | tf_op jit(solution)/shard_map/ppermute | solution.py:68
  36.7 2.0 %collective-permute-done.5 = f32[8,3072]{1,0:T(8,128)S(1)} collective-permute-done((f32[8,3072]{1,0:T(8,128)S(1)}, f32[8,3072]{1,0:T(8,128)S(1)}, u32[]{:S(2)}, u32[]{:S(2)}) %collective-permute-start.5) | collective-permute-done | bytes 98336 | tf_op jit(solution)/shard_map/ppermute | solution.py:66
  38.7 0.9 %fusion.11 = f32[6,8,128]{2,1,0:T(8,128)S(1)} fusion(f32[8,6,512]{2,0,1:T(8,128)S(1)} %bitcast.70, f32[6,512,128]{2,1,0:T(8,128)S(1)} %bitcast.64), kind=kOutput, calls=%fused_computation.29 | convolution fusion | flops 37748736 | bytes 1695744 | tf_op jit(solution)/shard_map/aes,esb->eab/dot_general | solution.py:62
  39.6 0.6 collective-permute-start.6
  40.1 0.9 %fusion.12 = f32[6,8,128]{2,1,0:T(8,128)S(1)} fusion(f32[8,6,512]{2,0,1:T(8,128)S(1)} %bitcast.69, f32[6,512,128]{2,1,0:T(8,128)S(1)} %bitcast.65), kind=kOutput, calls=%fused_computation.30 | convolution fusion | flops 37748736 | bytes 1695744 | tf_op jit(solution)/shard_map/aes,esb->eab/dot_general | solution.py:62
  41.0 4.0 %collective-permute-start.8 = (f32[6,8,128]{2,1,0:T(8,128)S(1)}, f32[6,8,128]{2,1,0:T(8,128)S(1)}, u32[]{:S(2)}, u32[]{:S(2)}) collective-permute-start(f32[6,8,128]{2,1,0:T(8,128)S(1)} %fusion.12), channel_id=1, source_target_pairs={{0,1},{1,2},{2,3},{3,0},{4,5},{5,6},{6,7},{7,4},{8,9},{9,10},{10,1... | collective-permute-start | bytes 73736 | tf_op jit(solution)/shard_map/ppermute | solution.py:68
  45.0 1.6 %collective-permute-done.8 = f32[6,8,128]{2,1,0:T(8,128)S(1)} collective-permute-done((f32[6,8,128]{2,1,0:T(8,128)S(1)}, f32[6,8,128]{2,1,0:T(8,128)S(1)}, u32[]{:S(2)}, u32[]{:S(2)}) %collective-permute-start.8) | collective-permute-done | bytes 24608 | tf_op jit(solution)/shard_map/ppermute | solution.py:68
  46.7 0.9 %fusion.2 = bf16[6,8,128]{2,1,0:T(8,128)(2,1)S(1)} fusion(f32[6,8,128]{2,1,0:T(8,128)S(1)} %collective-permute-done.8, f32[6,8,128]{2,1,0:T(8,128)S(1)} %collective-permute-done.6, f32[6,8,128]{2,1,0:T(8,128)S(1)} %collective-permute-done.4, f32[8,6,512]{2,0,1:T(8,128)S(1)} %bitcast.67, f32[6,512,128]{2,1,0:T(8,128)S(1)} %bitcast.66), kind=kOutput, calls=%fused_computation.4 | convolution fusion | flops 37773312 | bytes 1757184 | tf_op jit(solution)/shard_map/aes,esb->eab/dot_general | solution.py:62
  47.7 1.6 %collective-permute-start.10 = (bf16[6,1024]{1,0:T(8,128)(2,1)S(1)}, bf16[6,1024]{1,0:T(8,128)(2,1)S(1)}, u32[]{:S(2)}, u32[]{:S(2)}) collective-permute-start(bf16[6,1024]{1,0:T(8,128)(2,1)S(1)} %bitcast.73), channel_id=1, source_target_pairs={{0,8},{4,12},{8,0},{12,4},{1,9},{5,13},{9,1},{13,5},{2,10},{6,14},... | collective-permute-start | bytes 36872 | tf_op jit(solution)/shard_map/ppermute | solution.py:37
  49.3 1.4 %collective-permute-start.11 = (bf16[6,1024]{1,0:T(8,128)(2,1)S(1)}, bf16[6,1024]{1,0:T(8,128)(2,1)S(1)}, u32[]{:S(2)}, u32[]{:S(2)}) collective-permute-start(bf16[6,1024]{1,0:T(8,128)(2,1)S(1)} %bitcast.74), channel_id=1, source_target_pairs={{0,12},{4,0},{8,4},{12,8},{1,13},{5,1},{9,5},{13,9},{2,14},{6,2},{... | collective-permute-start | bytes 36872 | tf_op jit(solution)/shard_map/ppermute | solution.py:37
  50.7 0.2 collective-permute-done.9
  50.8 0.7 %collective-permute-done.10 = bf16[6,1024]{1,0:T(8,128)(2,1)S(1)} collective-permute-done((bf16[6,1024]{1,0:T(8,128)(2,1)S(1)}, bf16[6,1024]{1,0:T(8,128)(2,1)S(1)}, u32[]{:S(2)}, u32[]{:S(2)}) %collective-permute-start.10) | collective-permute-done | bytes 12320 | tf_op jit(solution)/shard_map/ppermute | solution.py:37
  51.5 0.6 %collective-permute-done.11 = bf16[6,1024]{1,0:T(8,128)(2,1)S(1)} collective-permute-done((bf16[6,1024]{1,0:T(8,128)(2,1)S(1)}, bf16[6,1024]{1,0:T(8,128)(2,1)S(1)}, u32[]{:S(2)}, u32[]{:S(2)}) %collective-permute-start.11) | collective-permute-done | bytes 12320 | tf_op jit(solution)/shard_map/ppermute | solution.py:37
  52.2 0.5 fusion.13
  52.7 2.2 %collective-permute-start.12 = (f32[6,6]{1,0:T(8,128)S(1)}, f32[6,6]{1,0:T(8,128)S(1)}, u32[]{:S(2)}, u32[]{:S(2)}) collective-permute-start(f32[6,6]{1,0:T(8,128)S(1)} %get-tuple-element.5), channel_id=1, source_target_pairs={{0,1},{1,2},{2,3},{3,0},{4,5},{5,6},{6,7},{7,4},{8,9},{9,10},{10,1... | collective-permute-start | bytes 440 | tf_op jit(solution)/shard_map/ppermute | solution.py:19
  54.9 0.3 collective-permute-start.13
  55.1 2.2 %collective-permute-start.14 = (f32[6,6]{1,0:T(8,128)S(1)}, f32[6,6]{1,0:T(8,128)S(1)}, u32[]{:S(2)}, u32[]{:S(2)}) collective-permute-start(f32[6,6]{1,0:T(8,128)S(1)} %get-tuple-element.6), channel_id=1, source_target_pairs={{0,3},{1,0},{2,1},{3,2},{4,7},{5,4},{6,5},{7,6},{8,11},{9,8},{10,9... | collective-permute-start | bytes 440 | tf_op jit(solution)/shard_map/ppermute | solution.py:19
  57.3 0.8 %collective-permute-done.12 = f32[6,6]{1,0:T(8,128)S(1)} collective-permute-done((f32[6,6]{1,0:T(8,128)S(1)}, f32[6,6]{1,0:T(8,128)S(1)}, u32[]{:S(2)}, u32[]{:S(2)}) %collective-permute-start.12) | collective-permute-done | bytes 176 | tf_op jit(solution)/shard_map/ppermute | solution.py:19
  58.1 1.3 %collective-permute-done.13 = f32[6,6]{1,0:T(8,128)S(1)} collective-permute-done((f32[6,6]{1,0:T(8,128)S(1)}, f32[6,6]{1,0:T(8,128)S(1)}, u32[]{:S(2)}, u32[]{:S(2)}) %collective-permute-start.13) | collective-permute-done | bytes 176 | tf_op jit(solution)/shard_map/ppermute | solution.py:19
  59.4 0.6 fusion.7
  (27 shorter events, 0.3 us)
Async XLA Ops:
  0.6 24.3 %copy-start = (bf16[2048,128]{1,0:T(8,128)(2,1)S(1)}, bf16[2048,128]{1,0:T(8,128)(2,1)}, u32[]{:S(2)}) copy-start(bf16[2048,128]{1,0:T(8,128)(2,1)} %param.8) | copy-start | bytes 1572868
  0.7 8.7 %copy-start.1 = (f32[64,32]{0,1:T(8,128)S(1)}, f32[64,32]{0,1:T(8,128)}, u32[]{:S(2)}) copy-start(f32[64,32]{0,1:T(8,128)} %param.9) | copy-start | bytes 24580
  9.9 8.8 %collective-permute-start = (f32[8,3072]{1,0:T(8,128)S(1)}, f32[8,3072]{1,0:T(8,128)S(1)}, u32[]{:S(2)}, u32[]{:S(2)}) collective-permute-start(f32[8,3072]{1,0:T(8,128)S(1)} %get-tuple-element.2), channel_id=1, source_target_pairs={{0,1},{1,2},{2,3},{3,0},{4,5},{5,6},{6,7},{7,4},{8,9},{9,10},{10,1... | collective-permute-start | bytes 294920 | tf_op jit(solution)/shard_map/ppermute | solution.py:19
  13.1 9.2 %collective-permute-start.1 = (f32[8,3072]{1,0:T(8,128)S(1)}, f32[8,3072]{1,0:T(8,128)S(1)}, u32[]{:S(2)}, u32[]{:S(2)}) collective-permute-start(f32[8,3072]{1,0:T(8,128)S(1)} %get-tuple-element.4), channel_id=1, source_target_pairs={{0,2},{1,3},{2,0},{3,1},{4,6},{5,7},{6,4},{7,5},{8,10},{9,11},{10,... | collective-permute-start | bytes 294920 | tf_op jit(solution)/shard_map/ppermute | solution.py:19
  15.6 6.6 %collective-permute-start.2 = (f32[8,3072]{1,0:T(8,128)S(1)}, f32[8,3072]{1,0:T(8,128)S(1)}, u32[]{:S(2)}, u32[]{:S(2)}) collective-permute-start(f32[8,3072]{1,0:T(8,128)S(1)} %get-tuple-element.3), channel_id=1, source_target_pairs={{0,3},{1,0},{2,1},{3,2},{4,7},{5,4},{6,5},{7,6},{8,11},{9,8},{10,9... | collective-permute-start | bytes 294920 | tf_op jit(solution)/shard_map/ppermute | solution.py:19
  22.3 11.5 %collective-permute-start.3 = (f32[8,3072]{1,0:T(8,128)S(1)}, f32[8,3072]{1,0:T(8,128)S(1)}, u32[]{:S(2)}, u32[]{:S(2)}) collective-permute-start(f32[8,3072]{1,0:T(8,128)S(1)} %fusion.4), channel_id=1, source_target_pairs={{0,1},{1,2},{2,3},{3,0},{4,5},{5,6},{6,7},{7,4},{8,9},{9,10},{10,1... | collective-permute-start | bytes 294920 | tf_op jit(solution)/shard_map/ppermute | solution.py:66
  31.3 7.4 %collective-permute-start.5 = (f32[8,3072]{1,0:T(8,128)S(1)}, f32[8,3072]{1,0:T(8,128)S(1)}, u32[]{:S(2)}, u32[]{:S(2)}) collective-permute-start(f32[8,3072]{1,0:T(8,128)S(1)} %fusion.4), channel_id=1, source_target_pairs={{0,2},{1,3},{2,0},{3,1},{4,6},{5,7},{6,4},{7,5},{8,10},{9,11},{10,... | collective-permute-start | bytes 294920 | tf_op jit(solution)/shard_map/ppermute | solution.py:66
  33.0 7.1 %collective-permute-start.7 = (f32[8,3072]{1,0:T(8,128)S(1)}, f32[8,3072]{1,0:T(8,128)S(1)}, u32[]{:S(2)}, u32[]{:S(2)}) collective-permute-start(f32[8,3072]{1,0:T(8,128)S(1)} %fusion.4), channel_id=1, source_target_pairs={{0,3},{1,0},{2,1},{3,2},{4,7},{5,4},{6,5},{7,6},{8,11},{9,8},{10,9... | collective-permute-start | bytes 294920 | tf_op jit(solution)/shard_map/ppermute | solution.py:66
  34.6 10.4 %collective-permute-start.4 = (f32[6,8,128]{2,1,0:T(8,128)S(1)}, f32[6,8,128]{2,1,0:T(8,128)S(1)}, u32[]{:S(2)}, u32[]{:S(2)}) collective-permute-start(f32[6,8,128]{2,1,0:T(8,128)S(1)} %fusion.10), channel_id=1, source_target_pairs={{0,3},{1,0},{2,1},{3,2},{4,7},{5,4},{6,5},{7,6},{8,11},{9,8},{10,9... | collective-permute-start | bytes 73736 | tf_op jit(solution)/shard_map/ppermute | solution.py:68
  39.6 5.5 %collective-permute-start.6 = (f32[6,8,128]{2,1,0:T(8,128)S(1)}, f32[6,8,128]{2,1,0:T(8,128)S(1)}, u32[]{:S(2)}, u32[]{:S(2)}) collective-permute-start(f32[6,8,128]{2,1,0:T(8,128)S(1)} %fusion.11), channel_id=1, source_target_pairs={{0,2},{1,3},{2,0},{3,1},{4,6},{5,7},{6,4},{7,5},{8,10},{9,11},{10,... | collective-permute-start | bytes 73736 | tf_op jit(solution)/shard_map/ppermute | solution.py:68
  41.0 5.7 %collective-permute-start.8 = (f32[6,8,128]{2,1,0:T(8,128)S(1)}, f32[6,8,128]{2,1,0:T(8,128)S(1)}, u32[]{:S(2)}, u32[]{:S(2)}) collective-permute-start(f32[6,8,128]{2,1,0:T(8,128)S(1)} %fusion.12), channel_id=1, source_target_pairs={{0,1},{1,2},{2,3},{3,0},{4,5},{5,6},{6,7},{7,4},{8,9},{9,10},{10,1... | collective-permute-start | bytes 73736 | tf_op jit(solution)/shard_map/ppermute | solution.py:68
  47.6 12.4 %copy-start.2 = (bf16[1,6,8,128]{3,1,2,0:T(8,128)(2,1)}, bf16[1,6,8,128]{3,1,2,0:T(8,128)(2,1)S(1)}, u32[]{:S(2)}) copy-start(bf16[1,6,8,128]{3,1,2,0:T(8,128)(2,1)S(1)} %copy.9) | copy-start | bytes 36868
  47.6 3.2 %collective-permute-start.9 = (bf16[6,1024]{1,0:T(8,128)(2,1)S(1)}, bf16[6,1024]{1,0:T(8,128)(2,1)S(1)}, u32[]{:S(2)}, u32[]{:S(2)}) collective-permute-start(bf16[6,1024]{1,0:T(8,128)(2,1)S(1)} %bitcast.72), channel_id=1, source_target_pairs={{0,4},{4,8},{8,12},{12,0},{1,5},{5,9},{9,13},{13,1},{2,6},{6,10},{... | collective-permute-start | bytes 36872 | tf_op jit(solution)/shard_map/ppermute | solution.py:37
  47.7 3.8 %collective-permute-start.10 = (bf16[6,1024]{1,0:T(8,128)(2,1)S(1)}, bf16[6,1024]{1,0:T(8,128)(2,1)S(1)}, u32[]{:S(2)}, u32[]{:S(2)}) collective-permute-start(bf16[6,1024]{1,0:T(8,128)(2,1)S(1)} %bitcast.73), channel_id=1, source_target_pairs={{0,8},{4,12},{8,0},{12,4},{1,9},{5,13},{9,1},{13,5},{2,10},{6,14},... | collective-permute-start | bytes 36872 | tf_op jit(solution)/shard_map/ppermute | solution.py:37
  49.3 2.8 %collective-permute-start.11 = (bf16[6,1024]{1,0:T(8,128)(2,1)S(1)}, bf16[6,1024]{1,0:T(8,128)(2,1)S(1)}, u32[]{:S(2)}, u32[]{:S(2)}) collective-permute-start(bf16[6,1024]{1,0:T(8,128)(2,1)S(1)} %bitcast.74), channel_id=1, source_target_pairs={{0,12},{4,0},{8,4},{12,8},{1,13},{5,1},{9,5},{13,9},{2,14},{6,2},{... | collective-permute-start | bytes 36872 | tf_op jit(solution)/shard_map/ppermute | solution.py:37
  52.7 5.4 %collective-permute-start.12 = (f32[6,6]{1,0:T(8,128)S(1)}, f32[6,6]{1,0:T(8,128)S(1)}, u32[]{:S(2)}, u32[]{:S(2)}) collective-permute-start(f32[6,6]{1,0:T(8,128)S(1)} %get-tuple-element.5), channel_id=1, source_target_pairs={{0,1},{1,2},{2,3},{3,0},{4,5},{5,6},{6,7},{7,4},{8,9},{9,10},{10,1... | collective-permute-start | bytes 440 | tf_op jit(solution)/shard_map/ppermute | solution.py:19
  54.9 4.5 %collective-permute-start.13 = (f32[6,6]{1,0:T(8,128)S(1)}, f32[6,6]{1,0:T(8,128)S(1)}, u32[]{:S(2)}, u32[]{:S(2)}) collective-permute-start(f32[6,6]{1,0:T(8,128)S(1)} %get-tuple-element.7), channel_id=1, source_target_pairs={{0,2},{1,3},{2,0},{3,1},{4,6},{5,7},{6,4},{7,5},{8,10},{9,11},{10,... | collective-permute-start | bytes 440 | tf_op jit(solution)/shard_map/ppermute | solution.py:19
  55.1 4.3 %collective-permute-start.14 = (f32[6,6]{1,0:T(8,128)S(1)}, f32[6,6]{1,0:T(8,128)S(1)}, u32[]{:S(2)}, u32[]{:S(2)}) collective-permute-start(f32[6,6]{1,0:T(8,128)S(1)} %get-tuple-element.6), channel_id=1, source_target_pairs={{0,3},{1,0},{2,1},{3,2},{4,7},{5,4},{6,5},{7,6},{8,11},{9,8},{10,9... | collective-permute-start | bytes 440 | tf_op jit(solution)/shard_map/ppermute | solution.py:19

commit v4 on v3

--- a/solution.py
+++ b/solution.py
@@ -8,6 +8,71 @@
 SEQ = 512
 epsilon = 1e-05
 HI = lax.Precision.HIGHEST
+
+
+from jax.experimental import pallas as pl
+from jax.experimental.pallas import tpu as pltpu
+
+ROWS = 512
+
+
+def _split(x):
+    hi = x.astype(jnp.bfloat16)
+    return hi, (x - hi.astype(jnp.float32)).astype(jnp.bfloat16)
+
+
+def _rank_kernel(cot_ref, bt_ref, srt_ref, out_ref):
+    back_t = lax.dot_general(bt_ref[...], cot_ref[...], (((1,), (1,)), ((), ())),
+                             preferred_element_type=jnp.float32)
+    b_hi, b_lo = _split(back_t)
+    s_hi, s_lo = _split(srt_ref[...])
+    f32 = jnp.float32
+    out = jnp.dot(s_hi, b_hi, preferred_element_type=f32)
+    out = out + jnp.dot(s_hi, b_lo, preferred_element_type=f32)
+    out = out + jnp.dot(s_lo, b_hi, preferred_element_type=f32)
+    out_ref[...] = out
+
+
+def rank_side_t(cotangent, up_factor_matrix, rank_sketch, interpret=False):
+    tokens, width = cotangent.shape
+    low = up_factor_matrix.shape[1]
+    k_r = rank_sketch.shape[1]
+    return pl.pallas_call(
+        _rank_kernel,
+        grid=(tokens // ROWS,),
+        in_specs=[
+            pl.BlockSpec((ROWS, width), lambda i: (i, 0)),
+            pl.BlockSpec((low, width), lambda i: (0, 0)),
+            pl.BlockSpec((k_r, low), lambda i: (0, 0)),
+        ],
+        out_specs=pl.BlockSpec((k_r, ROWS), lambda i: (0, i)),
+        out_shape=jax.ShapeDtypeStruct((k_r, tokens), jnp.float32),
+        cost_estimate=pl.CostEstimate(flops=2 * tokens * width * low, transcendentals=0,
+                                      bytes_accessed=2 * tokens * width + 4 * tokens * k_r),
+        interpret=interpret,
+    )(cotangent, up_factor_matrix.T, rank_sketch.T)
+
+
+def _input_kernel(act_ref, s_ref, out_ref):
+    out_ref[...] = jnp.dot(act_ref[...], s_ref[...], preferred_element_type=jnp.float32)
+
+
+def input_side(activations, input_sketch, interpret=False):
+    tokens, width = activations.shape
+    k_in = input_sketch.shape[1]
+    return pl.pallas_call(
+        _input_kernel,
+        grid=(tokens // ROWS,),
+        in_specs=[
+            pl.BlockSpec((ROWS, width), lambda i: (i, 0)),
+            pl.BlockSpec((width, k_in), lambda i: (0, 0)),
+        ],
+        out_specs=pl.BlockSpec((ROWS, k_in), lambda i: (i, 0)),
+        out_shape=jax.ShapeDtypeStruct((tokens, k_in), jnp.float32),
+        cost_estimate=pl.CostEstimate(flops=2 * tokens * width * k_in, transcendentals=0,
+                                      bytes_accessed=2 * tokens * width + 4 * tokens * k_in),
+        interpret=interpret,
+    )(activations, input_sketch)
 
 
 def exchange(blocks, axis):
@@ -49,12 +114,10 @@
     shards = lax.axis_size("hidden")
     me = lax.axis_index("hidden")
     examples = activations.shape[0] // SEQ
-    backward_t = lax.dot_general(up_factor_matrix, cotangent, (((0,), (1,)), ((), ())),
-                                 preferred_element_type=jnp.float32)
-    rank_t = lax.dot_general(rank_sketch, backward_t, (((0,), (0,)), ((), ())), precision=HI)
+    rank_t = rank_side_t(cotangent, up_factor_matrix, rank_sketch)
     own_a = rank_t.shape[0] // shards
     rank_own = reduce_scatter(rank_t.reshape(shards, own_a, -1), "hidden")
-    input_part = jnp.dot(activations, input_sketch, preferred_element_type=jnp.float32)
+    input_part = input_side(activations, input_sketch)
     input_rows = input_part.reshape(examples, SEQ, input_part.shape[1])
 
     def outer(rank_block):

time: 60.2 us -> 64.6 us (1.073)
  Pallas kernels: 0 us -> 18.4 us
  matrix products: 19.6 us -> 5.35 us
  waiting for transfers between devices: 12.5 us -> 11.3 us
  local copies, waits for them, and re-layouts: 0.14 us -> 1.1 us
  other arithmetic: 0.66 us -> 1.56 us
    pallas_call x0 -> x2, Pallas kernels: none -> 18.4 us  [the longest x1 9.44 us: rank_side_t(): pl.pallas_call(_rank_kernel, grid=(tokens // ROWS,), in_specs=[pl.BlockSp...]
    dot_general x3 -> x0, matrix products: 15.6 us -> none  [the longest x1 8.64 us: per_device(): lax.dot_general(up_factor_matrix, cotangent, (((0,), (1,)), ((), ())), pr...]
    ppermute x3, waiting for transfers between devices: 2.02 us -> 0.62 us  [per_device(): lax.ppermute(rank_own, 'hidden', [(i, (i + d) % shards) for i in range(sh...]
    dot_general x4, matrix products: 3.42 us -> 4.82 us  [outer(): return jnp.einsum('aes,esb->eab', rows, input_rows, precision=HI)]
    squeeze x2, local copies, waits for them, and re-layouts: 0.04 us -> 1.01 us  [exchange(): piece = lax.dynamic_index_in_dim(blocks, (me + d) % n, 0, keepdims=False)]
    add x1, other arithmetic: 0.02 us -> 0.91 us  [reduce_scatter(): acc = acc + g]
  transfers between devices with their start and end apart: 15 -> 15, of which waited for: 9 -> 9; matrix products, arithmetic and copies ran while one was open for 15% -> 6% of each run, Pallas kernels for 0% -> 14%
where the time goes in v4:
time: 64.6 us; the launch traced here: 64.2 us
  starting transfers between devices  25.8 us (40%)
  Pallas kernels  18.4 us (28%)
  waiting for transfers between devices  11.3 us (17%)
  matrix products  5.35 us (8%)
  other arithmetic  1.56 us (2%)
  local copies, waits for them, and re-layouts  1.1 us (2%)
  between operations  0.78 us (1%)
    ppermute x6, starting transfers between devices, exchange(): got.append(lax.ppermute(piece, axis, [(i, (i + d) % n) for i in range(n)]))  11.4 us
    pallas_call x1, Pallas kernels, rank_side_t(): pl.pallas_call(_rank_kernel, grid=(tokens // ROWS,), in_specs=[pl.BlockSp...  9.44 us
    pallas_call x1, Pallas kernels, input_side(): pl.pallas_call(_input_kernel, grid=(tokens // ROWS,), in_specs=[pl.BlockS...  8.93 us
    ppermute x6, waiting for transfers between devices, exchange(): got.append(lax.ppermute(piece, axis, [(i, (i + d) % n) for i in range(n)]))  7.34 us
    ppermute x3, starting transfers between devices, per_device(): own = own + lax.ppermute(outer(visiting), 'hidden', back)  6.38 us
    ppermute x3, starting transfers between devices, per_device(): lax.ppermute(rank_own, 'hidden', [(i, (i + d) % shards) for i in range(sh...  4.98 us
    dot_general x4, matrix products, outer(): return jnp.einsum('aes,esb->eab', rows, input_rows, precision=HI)  4.82 us
    ppermute x3, starting transfers between devices, all_gather(): got = lax.ppermute(x, axis, [(i, (i + d) % n) for i in range(n)])  3.03 us
  transfers between devices with their start and end apart: 15, of which 9 were waited for; matrix products, arithmetic and copies ran while one was open for 6% of the time, Pallas kernels for 14%

profile of v4, /device:TPU:0, one launch (start us, length us, event | category | flops | bytes accessed | tf_op | source)
XLA Modules:
  0.0 64.2 jit_solution(395039127830603021)
XLA Ops:
  0.7 9.4 %shard_map.68 = f32[32,3072]{1,0:T(8,128)} custom-call(bf16[3072,2048]{1,0:T(8,128)(2,1)} %cot_ref.1, bf16[64,2048]{1,0:T(8,128)(2,1)} %bitcast.63, f32[32,64]{1,0:T(8,128)} %bitcast.68), custom_call_target="tpu_custom_call" | custom-call | flops 805306368 | bytes 12976128 | tf_op jit(solution)/shard_map/pallas_call | solution.py:40
  10.1 1.0 %dynamic-slice_bitcast_fusion.2 = (f32[8,3072]{1,0:T(8,128)S(1)}, f32[8,3072]{1,0:T(8,128)S(1)}, f32[8,3072]{1,0:T(8,128)S(1)}) fusion(f32[4,8,3072]{2,1,0:T(8,128)} %bitcast.60, s32[]{:T(128)S(6)} %select_n.66, s32[]{:T(128)S(6)} %select_n.70, s32[]{:T(128)S(6)} %select_n.68), kind=kLoop, calls=%fused_computation.10 | loop fusion | bytes 589836 | tf_op jit(solution)/shard_map/jit(dynamic_index_in_dim)/squeeze | solution.py:83
  11.1 3.1 %collective-permute-start = (f32[8,3072]{1,0:T(8,128)S(1)}, f32[8,3072]{1,0:T(8,128)S(1)}, u32[]{:S(2)}, u32[]{:S(2)}) collective-permute-start(f32[8,3072]{1,0:T(8,128)S(1)} %get-tuple-element.2), channel_id=1, source_target_pairs={{0,1},{1,2},{2,3},{3,0},{4,5},{5,6},{6,7},{7,4},{8,9},{9,10},{10,1... | collective-permute-start | bytes 294920 | tf_op jit(solution)/shard_map/ppermute | solution.py:84
  14.2 2.6 %collective-permute-start.1 = (f32[8,3072]{1,0:T(8,128)S(1)}, f32[8,3072]{1,0:T(8,128)S(1)}, u32[]{:S(2)}, u32[]{:S(2)}) collective-permute-start(f32[8,3072]{1,0:T(8,128)S(1)} %get-tuple-element.4), channel_id=1, source_target_pairs={{0,2},{1,3},{2,0},{3,1},{4,6},{5,7},{6,4},{7,5},{8,10},{9,11},{10,... | collective-permute-start | bytes 294920 | tf_op jit(solution)/shard_map/ppermute | solution.py:84
  16.8 1.4 %collective-permute-start.2 = (f32[8,3072]{1,0:T(8,128)S(1)}, f32[8,3072]{1,0:T(8,128)S(1)}, u32[]{:S(2)}, u32[]{:S(2)}) collective-permute-start(f32[8,3072]{1,0:T(8,128)S(1)} %get-tuple-element.3), channel_id=1, source_target_pairs={{0,3},{1,0},{2,1},{3,2},{4,7},{5,4},{6,5},{7,6},{8,11},{9,8},{10,9... | collective-permute-start | bytes 294920 | tf_op jit(solution)/shard_map/ppermute | solution.py:84
  18.2 1.7 %collective-permute-done = f32[8,3072]{1,0:T(8,128)S(1)} collective-permute-done((f32[8,3072]{1,0:T(8,128)S(1)}, f32[8,3072]{1,0:T(8,128)S(1)}, u32[]{:S(2)}, u32[]{:S(2)}) %collective-permute-start) | collective-permute-done | bytes 98336 | tf_op jit(solution)/shard_map/ppermute | solution.py:84
  19.9 3.5 %collective-permute-done.1 = f32[8,3072]{1,0:T(8,128)S(1)} collective-permute-done((f32[8,3072]{1,0:T(8,128)S(1)}, f32[8,3072]{1,0:T(8,128)S(1)}, u32[]{:S(2)}, u32[]{:S(2)}) %collective-permute-start.1) | collective-permute-done | bytes 98336 | tf_op jit(solution)/shard_map/ppermute | solution.py:84
  23.4 0.9 %fusion.4 = f32[8,3072]{1,0:T(8,128)S(1)} fusion(f32[8,3072]{1,0:T(8,128)S(1)} %collective-permute-done.2, f32[8,3072]{1,0:T(8,128)S(1)} %collective-permute-done.1, f32[8,3072]{1,0:T(8,128)S(1)} %collective-permute-done, f32[4,8,3072]{2,1,0:T(8,128)} %bitcast.61, s32[]{:T(128)S(6)} %select_n.64), kind=kLoop, calls=%fused_computation.7 | loop fusion | flops 73728 | bytes 491524 | tf_op jit(solution)/shard_map/add | solution.py:92
  24.3 2.6 %collective-permute-start.3 = (f32[8,3072]{1,0:T(8,128)S(1)}, f32[8,3072]{1,0:T(8,128)S(1)}, u32[]{:S(2)}, u32[]{:S(2)}) collective-permute-start(f32[8,3072]{1,0:T(8,128)S(1)} %fusion.4), channel_id=1, source_target_pairs={{0,1},{1,2},{2,3},{3,0},{4,5},{5,6},{6,7},{7,4},{8,9},{9,10},{10,1... | collective-permute-start | bytes 294920 | tf_op jit(solution)/shard_map/ppermute | solution.py:129
  26.9 8.9 %shard_map.69 = f32[3072,128]{1,0:T(8,128)} custom-call(bf16[3072,2048]{1,0:T(8,128)(2,1)} %act_ref.1, bf16[2048,128]{1,0:T(8,128)(2,1)} %s_ref.1), custom_call_target="tpu_custom_call" | custom-call | flops 1610612736 | bytes 14155776 | tf_op jit(solution)/shard_map/pallas_call | solution.py:63
  35.9 1.6 %collective-permute-start.5 = (f32[8,3072]{1,0:T(8,128)S(1)}, f32[8,3072]{1,0:T(8,128)S(1)}, u32[]{:S(2)}, u32[]{:S(2)}) collective-permute-start(f32[8,3072]{1,0:T(8,128)S(1)} %fusion.4), channel_id=1, source_target_pairs={{0,2},{1,3},{2,0},{3,1},{4,6},{5,7},{6,4},{7,5},{8,10},{9,11},{10,... | collective-permute-start | bytes 294920 | tf_op jit(solution)/shard_map/ppermute | solution.py:129
  37.5 0.8 %collective-permute-start.7 = (f32[8,3072]{1,0:T(8,128)S(1)}, f32[8,3072]{1,0:T(8,128)S(1)}, u32[]{:S(2)}, u32[]{:S(2)}) collective-permute-start(f32[8,3072]{1,0:T(8,128)S(1)} %fusion.4), channel_id=1, source_target_pairs={{0,3},{1,0},{2,1},{3,2},{4,7},{5,4},{6,5},{7,6},{8,11},{9,8},{10,9... | collective-permute-start | bytes 294920 | tf_op jit(solution)/shard_map/ppermute | solution.py:129
  38.3 2.3 %fusion.8 = f32[6,8,128]{2,1,0:T(8,128)S(1)} fusion(f32[8,6,512]{2,0,1:T(8,128)S(1)} %bitcast.67, f32[6,512,128]{2,1,0:T(8,128)} %bitcast.56), kind=kOutput, calls=%fused_computation.25 | convolution fusion | flops 37748736 | bytes 1695744 | tf_op jit(solution)/shard_map/aes,esb->eab/dot_general | solution.py:125
  40.5 2.1 %collective-permute-start.4 = (f32[6,8,128]{2,1,0:T(8,128)S(1)}, f32[6,8,128]{2,1,0:T(8,128)S(1)}, u32[]{:S(2)}, u32[]{:S(2)}) collective-permute-start(f32[6,8,128]{2,1,0:T(8,128)S(1)} %fusion.8), channel_id=1, source_target_pairs={{0,3},{1,0},{2,1},{3,2},{4,7},{5,4},{6,5},{7,6},{8,11},{9,8},{10,9... | collective-permute-start | bytes 73736 | tf_op jit(solution)/shard_map/ppermute | solution.py:131
  42.6 0.6 collective-permute-done.5
  43.2 0.9 %fusion.9 = f32[6,8,128]{2,1,0:T(8,128)S(1)} fusion(f32[8,6,512]{2,0,1:T(8,128)S(1)} %bitcast.66, f32[6,512,128]{2,1,0:T(8,128)S(1)} %bitcast.57), kind=kOutput, calls=%fused_computation.26 | convolution fusion | flops 37748736 | bytes 1695744 | tf_op jit(solution)/shard_map/aes,esb->eab/dot_general | solution.py:125
  44.0 0.6 collective-permute-start.6
  44.6 0.9 %fusion.10 = f32[6,8,128]{2,1,0:T(8,128)S(1)} fusion(f32[8,6,512]{2,0,1:T(8,128)S(1)} %bitcast.65, f32[6,512,128]{2,1,0:T(8,128)S(1)} %bitcast.58), kind=kOutput, calls=%fused_computation.27 | convolution fusion | flops 37748736 | bytes 1695744 | tf_op jit(solution)/shard_map/aes,esb->eab/dot_general | solution.py:125
  45.5 3.8 %collective-permute-start.8 = (f32[6,8,128]{2,1,0:T(8,128)S(1)}, f32[6,8,128]{2,1,0:T(8,128)S(1)}, u32[]{:S(2)}, u32[]{:S(2)}) collective-permute-start(f32[6,8,128]{2,1,0:T(8,128)S(1)} %fusion.10), channel_id=1, source_target_pairs={{0,1},{1,2},{2,3},{3,0},{4,5},{5,6},{6,7},{7,4},{8,9},{9,10},{10,1... | collective-permute-start | bytes 73736 | tf_op jit(solution)/shard_map/ppermute | solution.py:131
  49.2 1.9 %collective-permute-done.8 = f32[6,8,128]{2,1,0:T(8,128)S(1)} collective-permute-done((f32[6,8,128]{2,1,0:T(8,128)S(1)}, f32[6,8,128]{2,1,0:T(8,128)S(1)}, u32[]{:S(2)}, u32[]{:S(2)}) %collective-permute-start.8) | collective-permute-done | bytes 24608 | tf_op jit(solution)/shard_map/ppermute | solution.py:131
  51.2 0.9 %fusion.2 = bf16[6,8,128]{2,1,0:T(8,128)(2,1)S(1)} fusion(f32[6,8,128]{2,1,0:T(8,128)S(1)} %collective-permute-done.8, f32[6,8,128]{2,1,0:T(8,128)S(1)} %collective-permute-done.6, f32[6,8,128]{2,1,0:T(8,128)S(1)} %collective-permute-done.4, f32[8,6,512]{2,0,1:T(8,128)S(1)} %bitcast.62, f32[6,512,128]{2,1,0:T(8,128)S(1)} %bitcast.59), kind=kOutput, calls=%fused_computation.3 | convolution fusion | flops 37773312 | bytes 1757184 | tf_op jit(solution)/shard_map/aes,esb->eab/dot_general | solution.py:125
  52.2 1.6 %collective-permute-start.10 = (bf16[6,1024]{1,0:T(8,128)(2,1)S(1)}, bf16[6,1024]{1,0:T(8,128)(2,1)S(1)}, u32[]{:S(2)}, u32[]{:S(2)}) collective-permute-start(bf16[6,1024]{1,0:T(8,128)(2,1)S(1)} %bitcast.70), channel_id=1, source_target_pairs={{0,8},{4,12},{8,0},{12,4},{1,9},{5,13},{9,1},{13,5},{2,10},{6,14},... | collective-permute-start | bytes 36872 | tf_op jit(solution)/shard_map/ppermute | solution.py:102
  53.7 1.4 %collective-permute-start.11 = (bf16[6,1024]{1,0:T(8,128)(2,1)S(1)}, bf16[6,1024]{1,0:T(8,128)(2,1)S(1)}, u32[]{:S(2)}, u32[]{:S(2)}) collective-permute-start(bf16[6,1024]{1,0:T(8,128)(2,1)S(1)} %bitcast.71), channel_id=1, source_target_pairs={{0,12},{4,0},{8,4},{12,8},{1,13},{5,1},{9,5},{13,9},{2,14},{6,2},{... | collective-permute-start | bytes 36872 | tf_op jit(solution)/shard_map/ppermute | solution.py:102
  55.3 0.7 %collective-permute-done.10 = bf16[6,1024]{1,0:T(8,128)(2,1)S(1)} collective-permute-done((bf16[6,1024]{1,0:T(8,128)(2,1)S(1)}, bf16[6,1024]{1,0:T(8,128)(2,1)S(1)}, u32[]{:S(2)}, u32[]{:S(2)}) %collective-permute-start.10) | collective-permute-done | bytes 12320 | tf_op jit(solution)/shard_map/ppermute | solution.py:102
  56.0 0.6 collective-permute-done.11
  56.7 0.5 fusion.11
  57.2 1.9 %collective-permute-start.12 = (f32[6,6]{1,0:T(8,128)S(1)}, f32[6,6]{1,0:T(8,128)S(1)}, u32[]{:S(2)}, u32[]{:S(2)}) collective-permute-start(f32[6,6]{1,0:T(8,128)S(1)} %get-tuple-element.5), channel_id=1, source_target_pairs={{0,1},{1,2},{2,3},{3,0},{4,5},{5,6},{6,7},{7,4},{8,9},{9,10},{10,1... | collective-permute-start | bytes 440 | tf_op jit(solution)/shard_map/ppermute | solution.py:84
  59.1 0.3 collective-permute-start.13
  59.4 2.2 %collective-permute-start.14 = (f32[6,6]{1,0:T(8,128)S(1)}, f32[6,6]{1,0:T(8,128)S(1)}, u32[]{:S(2)}, u32[]{:S(2)}) collective-permute-start(f32[6,6]{1,0:T(8,128)S(1)} %get-tuple-element.6), channel_id=1, source_target_pairs={{0,3},{1,0},{2,1},{3,2},{4,7},{5,4},{6,5},{7,6},{8,11},{9,8},{10,9... | collective-permute-start | bytes 440 | tf_op jit(solution)/shard_map/ppermute | solution.py:84
  61.6 1.1 %collective-permute-done.12 = f32[6,6]{1,0:T(8,128)S(1)} collective-permute-done((f32[6,6]{1,0:T(8,128)S(1)}, f32[6,6]{1,0:T(8,128)S(1)}, u32[]{:S(2)}, u32[]{:S(2)}) %collective-permute-start.12) | collective-permute-done | bytes 176 | tf_op jit(solution)/shard_map/ppermute | solution.py:84
  62.6 1.0 %collective-permute-done.13 = f32[6,6]{1,0:T(8,128)S(1)} collective-permute-done((f32[6,6]{1,0:T(8,128)S(1)}, f32[6,6]{1,0:T(8,128)S(1)}, u32[]{:S(2)}, u32[]{:S(2)}) %collective-permute-start.13) | collective-permute-done | bytes 176 | tf_op jit(solution)/shard_map/ppermute | solution.py:84
  63.6 0.6 fusion.7
  (24 shorter events, 0.4 us)
Async XLA Ops:
  11.1 8.8 %collective-permute-start = (f32[8,3072]{1,0:T(8,128)S(1)}, f32[8,3072]{1,0:T(8,128)S(1)}, u32[]{:S(2)}, u32[]{:S(2)}) collective-permute-start(f32[8,3072]{1,0:T(8,128)S(1)} %get-tuple-element.2), channel_id=1, source_target_pairs={{0,1},{1,2},{2,3},{3,0},{4,5},{5,6},{6,7},{7,4},{8,9},{9,10},{10,1... | collective-permute-start | bytes 294920 | tf_op jit(solution)/shard_map/ppermute | solution.py:84
  14.2 9.2 %collective-permute-start.1 = (f32[8,3072]{1,0:T(8,128)S(1)}, f32[8,3072]{1,0:T(8,128)S(1)}, u32[]{:S(2)}, u32[]{:S(2)}) collective-permute-start(f32[8,3072]{1,0:T(8,128)S(1)} %get-tuple-element.4), channel_id=1, source_target_pairs={{0,2},{1,3},{2,0},{3,1},{4,6},{5,7},{6,4},{7,5},{8,10},{9,11},{10,... | collective-permute-start | bytes 294920 | tf_op jit(solution)/shard_map/ppermute | solution.py:84
  16.8 6.6 %collective-permute-start.2 = (f32[8,3072]{1,0:T(8,128)S(1)}, f32[8,3072]{1,0:T(8,128)S(1)}, u32[]{:S(2)}, u32[]{:S(2)}) collective-permute-start(f32[8,3072]{1,0:T(8,128)S(1)} %get-tuple-element.3), channel_id=1, source_target_pairs={{0,3},{1,0},{2,1},{3,2},{4,7},{5,4},{6,5},{7,6},{8,11},{9,8},{10,9... | collective-permute-start | bytes 294920 | tf_op jit(solution)/shard_map/ppermute | solution.py:84
  24.3 13.9 %collective-permute-start.3 = (f32[8,3072]{1,0:T(8,128)S(1)}, f32[8,3072]{1,0:T(8,128)S(1)}, u32[]{:S(2)}, u32[]{:S(2)}) collective-permute-start(f32[8,3072]{1,0:T(8,128)S(1)} %fusion.4), channel_id=1, source_target_pairs={{0,1},{1,2},{2,3},{3,0},{4,5},{5,6},{6,7},{7,4},{8,9},{9,10},{10,1... | collective-permute-start | bytes 294920 | tf_op jit(solution)/shard_map/ppermute | solution.py:129
  35.9 7.3 %copy-start = (f32[3072,128]{1,0:T(8,128)S(1)}, f32[3072,128]{1,0:T(8,128)}, u32[]{:S(2)}) copy-start(f32[3072,128]{1,0:T(8,128)} %shard_map.69) | copy-start | bytes 4718596
  35.9 7.3 %collective-permute-start.5 = (f32[8,3072]{1,0:T(8,128)S(1)}, f32[8,3072]{1,0:T(8,128)S(1)}, u32[]{:S(2)}, u32[]{:S(2)}) collective-permute-start(f32[8,3072]{1,0:T(8,128)S(1)} %fusion.4), channel_id=1, source_target_pairs={{0,2},{1,3},{2,0},{3,1},{4,6},{5,7},{6,4},{7,5},{8,10},{9,11},{10,... | collective-permute-start | bytes 294920 | tf_op jit(solution)/shard_map/ppermute | solution.py:129
  37.5 7.1 %collective-permute-start.7 = (f32[8,3072]{1,0:T(8,128)S(1)}, f32[8,3072]{1,0:T(8,128)S(1)}, u32[]{:S(2)}, u32[]{:S(2)}) collective-permute-start(f32[8,3072]{1,0:T(8,128)S(1)} %fusion.4), channel_id=1, source_target_pairs={{0,3},{1,0},{2,1},{3,2},{4,7},{5,4},{6,5},{7,6},{8,11},{9,8},{10,9... | collective-permute-start | bytes 294920 | tf_op jit(solution)/shard_map/ppermute | solution.py:129
  40.5 8.7 %collective-permute-start.4 = (f32[6,8,128]{2,1,0:T(8,128)S(1)}, f32[6,8,128]{2,1,0:T(8,128)S(1)}, u32[]{:S(2)}, u32[]{:S(2)}) collective-permute-start(f32[6,8,128]{2,1,0:T(8,128)S(1)} %fusion.8), channel_id=1, source_target_pairs={{0,3},{1,0},{2,1},{3,2},{4,7},{5,4},{6,5},{7,6},{8,11},{9,8},{10,9... | collective-permute-start | bytes 73736 | tf_op jit(solution)/shard_map/ppermute | solution.py:131
  44.0 5.2 %collective-permute-start.6 = (f32[6,8,128]{2,1,0:T(8,128)S(1)}, f32[6,8,128]{2,1,0:T(8,128)S(1)}, u32[]{:S(2)}, u32[]{:S(2)}) collective-permute-start(f32[6,8,128]{2,1,0:T(8,128)S(1)} %fusion.9), channel_id=1, source_target_pairs={{0,2},{1,3},{2,0},{3,1},{4,6},{5,7},{6,4},{7,5},{8,10},{9,11},{10,... | collective-permute-start | bytes 73736 | tf_op jit(solution)/shard_map/ppermute | solution.py:131
  45.5 5.7 %collective-permute-start.8 = (f32[6,8,128]{2,1,0:T(8,128)S(1)}, f32[6,8,128]{2,1,0:T(8,128)S(1)}, u32[]{:S(2)}, u32[]{:S(2)}) collective-permute-start(f32[6,8,128]{2,1,0:T(8,128)S(1)} %fusion.10), channel_id=1, source_target_pairs={{0,1},{1,2},{2,3},{3,0},{4,5},{5,6},{6,7},{7,4},{8,9},{9,10},{10,1... | collective-permute-start | bytes 73736 | tf_op jit(solution)/shard_map/ppermute | solution.py:131
  52.1 12.2 %copy-start.1 = (bf16[1,6,8,128]{3,1,2,0:T(8,128)(2,1)}, bf16[1,6,8,128]{3,1,2,0:T(8,128)(2,1)S(1)}, u32[]{:S(2)}) copy-start(bf16[1,6,8,128]{3,1,2,0:T(8,128)(2,1)S(1)} %copy.9) | copy-start | bytes 36868
  52.1 3.2 %collective-permute-start.9 = (bf16[6,1024]{1,0:T(8,128)(2,1)S(1)}, bf16[6,1024]{1,0:T(8,128)(2,1)S(1)}, u32[]{:S(2)}, u32[]{:S(2)}) collective-permute-start(bf16[6,1024]{1,0:T(8,128)(2,1)S(1)} %bitcast.69), channel_id=1, source_target_pairs={{0,4},{4,8},{8,12},{12,0},{1,5},{5,9},{9,13},{13,1},{2,6},{6,10},{... | collective-permute-start | bytes 36872 | tf_op jit(solution)/shard_map/ppermute | solution.py:102
  52.2 3.8 %collective-permute-start.10 = (bf16[6,1024]{1,0:T(8,128)(2,1)S(1)}, bf16[6,1024]{1,0:T(8,128)(2,1)S(1)}, u32[]{:S(2)}, u32[]{:S(2)}) collective-permute-start(bf16[6,1024]{1,0:T(8,128)(2,1)S(1)} %bitcast.70), channel_id=1, source_target_pairs={{0,8},{4,12},{8,0},{12,4},{1,9},{5,13},{9,1},{13,5},{2,10},{6,14},... | collective-permute-start | bytes 36872 | tf_op jit(solution)/shard_map/ppermute | solution.py:102
  53.7 2.8 %collective-permute-start.11 = (bf16[6,1024]{1,0:T(8,128)(2,1)S(1)}, bf16[6,1024]{1,0:T(8,128)(2,1)S(1)}, u32[]{:S(2)}, u32[]{:S(2)}) collective-permute-start(bf16[6,1024]{1,0:T(8,128)(2,1)S(1)} %bitcast.71), channel_id=1, source_target_pairs={{0,12},{4,0},{8,4},{12,8},{1,13},{5,1},{9,5},{13,9},{2,14},{6,2},{... | collective-permute-start | bytes 36872 | tf_op jit(solution)/shard_map/ppermute | solution.py:102
  57.2 5.4 %collective-permute-start.12 = (f32[6,6]{1,0:T(8,128)S(1)}, f32[6,6]{1,0:T(8,128)S(1)}, u32[]{:S(2)}, u32[]{:S(2)}) collective-permute-start(f32[6,6]{1,0:T(8,128)S(1)} %get-tuple-element.5), channel_id=1, source_target_pairs={{0,1},{1,2},{2,3},{3,0},{4,5},{5,6},{6,7},{7,4},{8,9},{9,10},{10,1... | collective-permute-start | bytes 440 | tf_op jit(solution)/shard_map/ppermute | solution.py:84
  59.1 4.5 %collective-permute-start.13 = (f32[6,6]{1,0:T(8,128)S(1)}, f32[6,6]{1,0:T(8,128)S(1)}, u32[]{:S(2)}, u32[]{:S(2)}) collective-permute-start(f32[6,6]{1,0:T(8,128)S(1)} %get-tuple-element.7), channel_id=1, source_target_pairs={{0,2},{1,3},{2,0},{3,1},{4,6},{5,7},{6,4},{7,5},{8,10},{9,11},{10,... | collective-permute-start | bytes 440 | tf_op jit(solution)/shard_map/ppermute | solution.py:84
  59.4 4.3 %collective-permute-start.14 = (f32[6,6]{1,0:T(8,128)S(1)}, f32[6,6]{1,0:T(8,128)S(1)}, u32[]{:S(2)}, u32[]{:S(2)}) collective-permute-start(f32[6,6]{1,0:T(8,128)S(1)} %get-tuple-element.6), channel_id=1, source_target_pairs={{0,3},{1,0},{2,1},{3,2},{4,7},{5,4},{6,5},{7,6},{8,11},{9,8},{10,9... | collective-permute-start | bytes 440 | tf_op jit(solution)/shard_map/ppermute | solution.py:84

commit v5 on v3

--- a/solution.py
+++ b/solution.py
@@ -20,29 +20,53 @@
     return got
 
 
+def _bits(n):
+    k = n.bit_length() - 1
+    return k if n == 1 << k else None
+
+
+def _swap(x, axis, bit):
+    n = lax.axis_size(axis)
+    return lax.ppermute(x, axis, [(i, i ^ (1 << bit)) for i in range(n)])
+
+
 def reduce_scatter(blocks, axis):
-    got = exchange(blocks, axis)
-    acc = got[0]
-    for g in got[1:]:
-        acc = acc + g
-    return acc
+    n = lax.axis_size(axis)
+    k = _bits(n)
+    if k is None:
+        got = exchange(blocks, axis)
+        acc = got[0]
+        for g in got[1:]:
+            acc = acc + g
+        return acc
+    me = lax.axis_index(axis)
+    cur = blocks.reshape((2,) * k + blocks.shape[1:])
+    for bit in range(k):
+        dim = k - 1 - bit
+        mine = (me >> bit) & 1
+        keep = lax.dynamic_index_in_dim(cur, mine, dim, keepdims=False)
+        give = lax.dynamic_index_in_dim(cur, 1 - mine, dim, keepdims=False)
+        cur = keep + _swap(give, axis, bit)
+    return cur
 
 
 def all_gather(x, axis):
     n = lax.axis_size(axis)
     me = lax.axis_index(axis)
-    out = jnp.zeros((n,) + x.shape, x.dtype)
-    out = lax.dynamic_update_index_in_dim(out, x, me, 0)
-    for d in range(1, n):
-        got = lax.ppermute(x, axis, [(i, (i + d) % n) for i in range(n)])
-        out = lax.dynamic_update_index_in_dim(out, got, (me - d) % n, 0)
-    return out
-
-
-def all_reduce(x, axis):
-    n = lax.axis_size(axis)
-    acc = reduce_scatter(x.reshape((n, -1) + x.shape[1:]), axis)
-    return all_gather(acc, axis).reshape(x.shape)
+    k = _bits(n)
+    if k is None:
+        out = jnp.zeros((n,) + x.shape, x.dtype)
+        out = lax.dynamic_update_index_in_dim(out, x, me, 0)
+        for d in range(1, n):
+            got = lax.ppermute(x, axis, [(i, (i + d) % n) for i in range(n)])
+            out = lax.dynamic_update_index_in_dim(out, got, (me - d) % n, 0)
+        return out
+    cur = x
+    for step, bit in enumerate(reversed(range(k))):
+        other = _swap(cur, axis, bit)
+        low = ((me >> bit) & 1) == 0
+        cur = jnp.stack([jnp.where(low, cur, other), jnp.where(low, other, cur)], axis=step)
+    return cur.reshape((n,) + x.shape)
 
 
 def per_device(activations, cotangent, up_factor_matrix, input_sketch, rank_sketch):
@@ -58,14 +82,12 @@
     input_rows = input_part.reshape(examples, SEQ, input_part.shape[1])
 
     def outer(rank_block):
-        rows = rank_block.reshape(own_a, examples, SEQ)
+        rows = rank_block.reshape(rank_block.shape[0], examples, SEQ)
         return jnp.einsum("aes,esb->eab", rows, input_rows, precision=HI)
 
-    own = outer(rank_own)
-    for d in range(1, shards):
-        visiting = lax.ppermute(rank_own, "hidden", [(i, (i + d) % shards) for i in range(shards)])
-        back = [(i, (i - d) % shards) for i in range(shards)]
-        own = own + lax.ppermute(outer(visiting), "hidden", back)
+    rank_full = all_gather(rank_own, "hidden").reshape(rank_t.shape)
+    partial = outer(rank_full)
+    own = reduce_scatter(partial.reshape(examples, shards, own_a, -1).transpose(1, 0, 2, 3), "hidden")
     features = own.reshape(examples, -1).astype(jnp.bfloat16)
     widened = features.astype(jnp.float32)
     every = all_gather(features, "dp").reshape(-1, features.shape[1]).astype(jnp.float32)

time: 60.2 us -> 63.6 us (1.056)
  waiting for transfers between devices: 12.5 us -> 25 us
  starting transfers between devices: 26.4 us -> 19.2 us
  matrix products: 19.6 us -> 17.3 us
    ppermute x15 -> x10, waiting for transfers between devices: 12.5 us -> 25 us  [_swap(): return lax.ppermute(x, axis, [(i, i ^ 1 << bit) for i in range(n)])]
    ppermute x15 -> x10, starting transfers between devices: 26.4 us -> 19.2 us  [_swap(): return lax.ppermute(x, axis, [(i, i ^ 1 << bit) for i in range(n)])]
    dot_general x4 -> x1, matrix products: 3.42 us -> 1.09 us  [outer(): return jnp.einsum('aes,esb->eab', rows, input_rows, precision=HI)]
  transfers between devices with their start and end apart: 15 -> 10, of which waited for: 9 -> 9; matrix products, arithmetic and copies ran while one was open for 15% -> 10% of each run, Pallas kernels for 0% -> 0%
where the time goes in v5:
time: 63.6 us; the launch traced here: 63.5 us
  waiting for transfers between devices  25 us (39%)
  starting transfers between devices  19.2 us (30%)
  matrix products  17.3 us (27%)
  between operations  0.9 us (1%)
  other arithmetic  0.85 us (1%)
    ppermute x10, waiting for transfers between devices, _swap(): return lax.ppermute(x, axis, [(i, i ^ 1 << bit) for i in range(n)])  25 us
    ppermute x10, starting transfers between devices, _swap(): return lax.ppermute(x, axis, [(i, i ^ 1 << bit) for i in range(n)])  19.2 us
    dot_general x1, matrix products, per_device(): lax.dot_general(up_factor_matrix, cotangent, (((0,), (1,)), ((), ())), pr...  8.64 us
    dot_general x1, matrix products, per_device(): jnp.dot(activations, input_sketch, preferred_element_type=jnp.float32)  6.44 us
  transfers between devices with their start and end apart: 10, of which 9 were waited for; matrix products, arithmetic and copies ran while one was open for 10% of the time, Pallas kernels for 0%

profile of v5, /device:TPU:0, one launch (start us, length us, event | category | flops | bytes accessed | tf_op | source)
XLA Modules:
  0.0 63.5 jit_solution(6395940661166694534)
XLA Ops:
  0.6 0.0 copy-start
  0.6 0.0 copy-start.1
  0.7 8.6 %fusion.4 = f32[64,3072]{1,0:T(8,128)S(1)} fusion(bf16[2048,64]{0,1:T(8,128)(2,1)} %param.7, bf16[3072,2048]{1,0:T(8,128)(2,1)} %param.6), kind=kOutput, calls=%fused_computation.37 | convolution fusion | flops 805306368 | bytes 13631488 | tf_op jit(solution)/shard_map/dot_general | solution.py:76
  9.3 0.0 copy-done.1
  9.3 0.6 fusion.5
  9.9 3.1 %collective-permute-start = (f32[2,8,3072]{2,1,0:T(8,128)S(1)}, f32[2,8,3072]{2,1,0:T(8,128)S(1)}, u32[]{:S(2)}, u32[]{:S(2)}) collective-permute-start(f32[2,8,3072]{2,1,0:T(8,128)S(1)} %dynamic-slice_bitcast_fusion), channel_id=1, source_target_pairs={{0,1},{1,0},{2,3},{3,2},{4,5},{5,4},{6,7},{7,6},{8,9},{9,8},{10,11... | collective-permute-start | bytes 589832 | tf_op jit(solution)/shard_map/ppermute | solution.py:30
  13.0 4.9 %collective-permute-done = f32[2,8,3072]{2,1,0:T(8,128)S(1)} collective-permute-done((f32[2,8,3072]{2,1,0:T(8,128)S(1)}, f32[2,8,3072]{2,1,0:T(8,128)S(1)}, u32[]{:S(2)}, u32[]{:S(2)}) %collective-permute-start) | collective-permute-done | bytes 196640 | tf_op jit(solution)/shard_map/ppermute | solution.py:30
  18.0 2.8 %collective-permute-start.1 = (f32[8,3072]{1,0:T(8,128)S(1)}, f32[8,3072]{1,0:T(8,128)S(1)}, u32[]{:S(2)}, u32[]{:S(2)}) collective-permute-start(f32[8,3072]{1,0:T(8,128)S(1)} %dynamic-slice_bitcast_fusion.1), channel_id=1, source_target_pairs={{0,2},{1,3},{2,0},{3,1},{4,6},{5,7},{6,4},{7,5},{8,10},{9,11},{10,... | collective-permute-start | bytes 294920 | tf_op jit(solution)/shard_map/ppermute | solution.py:30
  20.8 4.2 %collective-permute-done.1 = f32[8,3072]{1,0:T(8,128)S(1)} collective-permute-done((f32[8,3072]{1,0:T(8,128)S(1)}, f32[8,3072]{1,0:T(8,128)S(1)}, u32[]{:S(2)}, u32[]{:S(2)}) %collective-permute-start.1) | collective-permute-done | bytes 98336 | tf_op jit(solution)/shard_map/ppermute | solution.py:30
  25.0 1.5 %collective-permute-start.2 = (f32[8,3072]{1,0:T(8,128)S(1)}, f32[8,3072]{1,0:T(8,128)S(1)}, u32[]{:S(2)}, u32[]{:S(2)}) collective-permute-start(f32[8,3072]{1,0:T(8,128)S(1)} %bitcast_add_fusion.1), channel_id=1, source_target_pairs={{0,2},{1,3},{2,0},{3,1},{4,6},{5,7},{6,4},{7,5},{8,10},{9,11},{10,... | collective-permute-start | bytes 294920 | tf_op jit(solution)/shard_map/ppermute | solution.py:30
  26.5 5.3 %collective-permute-done.2 = f32[8,3072]{1,0:T(8,128)S(1)} collective-permute-done((f32[8,3072]{1,0:T(8,128)S(1)}, f32[8,3072]{1,0:T(8,128)S(1)}, u32[]{:S(2)}, u32[]{:S(2)}) %collective-permute-start.2) | collective-permute-done | bytes 98336 | tf_op jit(solution)/shard_map/ppermute | solution.py:30
  31.8 0.1 collective-permute-start.3
  31.9 0.0 copy-done
  31.9 6.4 %fusion.6 = f32[3072,128]{1,0:T(8,128)S(1)} fusion(bf16[3072,2048]{1,0:T(8,128)(2,1)} %param.5, bf16[2048,128]{1,0:T(8,128)(2,1)S(1)} %copy-done), kind=kOutput, calls=%fused_computation.39 | convolution fusion | flops 1610612736 | bytes 14680064 | tf_op jit(solution)/shard_map/dot_general | solution.py:81
  38.3 0.0 collective-permute-done.3
  38.4 0.2 reshape_reshape_reshape.3
  38.6 1.1 %convolution_bitcast_fusion = f32[6,4,8,128]{3,2,1,0:T(8,128)S(1)} fusion(f32[6,512,128]{2,1,0:T(8,128)S(1)} %bitcast.82, f32[32,6,512]{2,1,0:T(8,128)S(1)} %reshape_reshape_reshape.3), kind=kOutput, calls=%fused_computation | convolution fusion | flops 150994944 | bytes 2064384 | tf_op jit(solution)/shard_map/aes,esb->eab/dot_general | solution.py:86
  39.8 2.0 %collective-permute-start.4 = (f32[2,6,8,128]{3,2,1,0:T(8,128)S(1)}, f32[2,6,8,128]{3,2,1,0:T(8,128)S(1)}, u32[]{:S(2)}, u32[]{:S(2)}) collective-permute-start(f32[2,6,8,128]{3,2,1,0:T(8,128)S(1)} %dynamic-slice_bitcast_fusion.2), channel_id=1, source_target_pairs={{0,1},{1,0},{2,3},{3,2},{4,5},{5,4},{6,7},{7,6},{8,9},{9,8},{10,11... | collective-permute-start | bytes 147464 | tf_op jit(solution)/shard_map/ppermute | solution.py:30
  41.8 2.1 %collective-permute-done.4 = f32[2,6,8,128]{3,2,1,0:T(8,128)S(1)} collective-permute-done((f32[2,6,8,128]{3,2,1,0:T(8,128)S(1)}, f32[2,6,8,128]{3,2,1,0:T(8,128)S(1)}, u32[]{:S(2)}, u32[]{:S(2)}) %collective-permute-start.4) | collective-permute-done | bytes 49184 | tf_op jit(solution)/shard_map/ppermute | solution.py:30
  44.0 3.0 %collective-permute-start.5 = (f32[6,8,128]{2,1,0:T(8,128)S(1)}, f32[6,8,128]{2,1,0:T(8,128)S(1)}, u32[]{:S(2)}, u32[]{:S(2)}) collective-permute-start(f32[6,8,128]{2,1,0:T(8,128)S(1)} %dynamic-slice_bitcast_fusion.3), channel_id=1, source_target_pairs={{0,2},{1,3},{2,0},{3,1},{4,6},{5,7},{6,4},{7,5},{8,10},{9,11},{10,... | collective-permute-start | bytes 73736 | tf_op jit(solution)/shard_map/ppermute | solution.py:30
  47.0 1.8 %collective-permute-done.5 = f32[6,8,128]{2,1,0:T(8,128)S(1)} collective-permute-done((f32[6,8,128]{2,1,0:T(8,128)S(1)}, f32[6,8,128]{2,1,0:T(8,128)S(1)}, u32[]{:S(2)}, u32[]{:S(2)}) %collective-permute-start.5) | collective-permute-done | bytes 24608 | tf_op jit(solution)/shard_map/ppermute | solution.py:30
  48.8 0.0 copy-start.2
  48.8 1.6 %collective-permute-start.6 = (bf16[6,1024]{1,0:T(8,128)(2,1)S(1)}, bf16[6,1024]{1,0:T(8,128)(2,1)S(1)}, u32[]{:S(2)}, u32[]{:S(2)}) collective-permute-start(bf16[6,1024]{1,0:T(8,128)(2,1)S(1)} %bitcast.91), channel_id=1, source_target_pairs={{0,8},{4,12},{8,0},{12,4},{1,9},{5,13},{9,1},{13,5},{2,10},{6,14},... | collective-permute-start | bytes 36872 | tf_op jit(solution)/shard_map/ppermute | solution.py:30
  50.4 2.2 %collective-permute-done.6 = bf16[6,1024]{1,0:T(8,128)(2,1)S(1)} collective-permute-done((bf16[6,1024]{1,0:T(8,128)(2,1)S(1)}, bf16[6,1024]{1,0:T(8,128)(2,1)S(1)}, u32[]{:S(2)}, u32[]{:S(2)}) %collective-permute-start.6) | collective-permute-done | bytes 12320 | tf_op jit(solution)/shard_map/ppermute | solution.py:30
  52.6 0.1 collective-permute-start.7
  52.7 1.2 %collective-permute-done.7 = bf16[2,6,1024]{2,1,0:T(8,128)(2,1)S(1)} collective-permute-done((bf16[2,6,1024]{2,1,0:T(8,128)(2,1)S(1)}, bf16[2,6,1024]{2,1,0:T(8,128)(2,1)S(1)}, u32[]{:S(2)}, u32[]{:S(2)}) %collective-permute-start.7) | collective-permute-done | bytes 24608 | tf_op jit(solution)/shard_map/ppermute | solution.py:30
  54.0 0.5 fusion.7
  54.6 2.0 %collective-permute-start.8 = (f32[2,6,6]{2,0,1:T(2,128)S(1)}, f32[2,6,6]{2,0,1:T(2,128)S(1)}, u32[]{:S(2)}, u32[]{:S(2)}) collective-permute-start(f32[2,6,6]{2,0,1:T(2,128)S(1)} %bitcast.93), channel_id=1, source_target_pairs={{0,1},{1,0},{2,3},{3,2},{4,5},{5,4},{6,7},{7,6},{8,9},{9,8},{10,11... | collective-permute-start | bytes 872 | tf_op jit(solution)/shard_map/ppermute | solution.py:30
  56.6 1.7 %collective-permute-done.8 = f32[2,6,6]{2,0,1:T(2,128)S(1)} collective-permute-done((f32[2,6,6]{2,0,1:T(2,128)S(1)}, f32[2,6,6]{2,0,1:T(2,128)S(1)}, u32[]{:S(2)}, u32[]{:S(2)}) %collective-permute-start.8) | collective-permute-done | bytes 320 | tf_op jit(solution)/shard_map/ppermute | solution.py:30
  58.3 3.0 %collective-permute-start.9 = (f32[6,6]{1,0:T(8,128)S(1)}, f32[6,6]{1,0:T(8,128)S(1)}, u32[]{:S(2)}, u32[]{:S(2)}) collective-permute-start(f32[6,6]{1,0:T(8,128)S(1)} %bitcast.94), channel_id=1, source_target_pairs={{0,2},{1,3},{2,0},{3,1},{4,6},{5,7},{6,4},{7,5},{8,10},{9,11},{10,... | collective-permute-start | bytes 440 | tf_op jit(solution)/shard_map/ppermute | solution.py:30
  61.3 1.6 %collective-permute-done.9 = f32[6,6]{1,0:T(8,128)S(1)} collective-permute-done((f32[6,6]{1,0:T(8,128)S(1)}, f32[6,6]{1,0:T(8,128)S(1)}, u32[]{:S(2)}, u32[]{:S(2)}) %collective-permute-start.9) | collective-permute-done | bytes 176 | tf_op jit(solution)/shard_map/ppermute | solution.py:30
  62.9 0.6 fusion.3
  (29 shorter events, 0.4 us)
Async XLA Ops:
  0.6 31.2 %copy-start = (bf16[2048,128]{1,0:T(8,128)(2,1)S(1)}, bf16[2048,128]{1,0:T(8,128)(2,1)}, u32[]{:S(2)}) copy-start(bf16[2048,128]{1,0:T(8,128)(2,1)} %param.8) | copy-start | bytes 1572868
  0.6 8.7 %copy-start.1 = (f32[64,32]{0,1:T(8,128)S(1)}, f32[64,32]{0,1:T(8,128)}, u32[]{:S(2)}) copy-start(f32[64,32]{0,1:T(8,128)} %param.9) | copy-start | bytes 24580
  9.9 8.0 %collective-permute-start = (f32[2,8,3072]{2,1,0:T(8,128)S(1)}, f32[2,8,3072]{2,1,0:T(8,128)S(1)}, u32[]{:S(2)}, u32[]{:S(2)}) collective-permute-start(f32[2,8,3072]{2,1,0:T(8,128)S(1)} %dynamic-slice_bitcast_fusion), channel_id=1, source_target_pairs={{0,1},{1,0},{2,3},{3,2},{4,5},{5,4},{6,7},{7,6},{8,9},{9,8},{10,11... | collective-permute-start | bytes 589832 | tf_op jit(solution)/shard_map/ppermute | solution.py:30
  18.0 7.0 %collective-permute-start.1 = (f32[8,3072]{1,0:T(8,128)S(1)}, f32[8,3072]{1,0:T(8,128)S(1)}, u32[]{:S(2)}, u32[]{:S(2)}) collective-permute-start(f32[8,3072]{1,0:T(8,128)S(1)} %dynamic-slice_bitcast_fusion.1), channel_id=1, source_target_pairs={{0,2},{1,3},{2,0},{3,1},{4,6},{5,7},{6,4},{7,5},{8,10},{9,11},{10,... | collective-permute-start | bytes 294920 | tf_op jit(solution)/shard_map/ppermute | solution.py:30
  25.0 6.7 %collective-permute-start.2 = (f32[8,3072]{1,0:T(8,128)S(1)}, f32[8,3072]{1,0:T(8,128)S(1)}, u32[]{:S(2)}, u32[]{:S(2)}) collective-permute-start(f32[8,3072]{1,0:T(8,128)S(1)} %bitcast_add_fusion.1), channel_id=1, source_target_pairs={{0,2},{1,3},{2,0},{3,1},{4,6},{5,7},{6,4},{7,5},{8,10},{9,11},{10,... | collective-permute-start | bytes 294920 | tf_op jit(solution)/shard_map/ppermute | solution.py:30
  31.8 6.5 %collective-permute-start.3 = (f32[2,8,3072]{2,1,0:T(8,128)S(1)}, f32[2,8,3072]{2,1,0:T(8,128)S(1)}, u32[]{:S(2)}, u32[]{:S(2)}) collective-permute-start(f32[2,8,3072]{2,1,0:T(8,128)S(1)} %pad_maximum_fusion.1), channel_id=1, source_target_pairs={{0,1},{1,0},{2,3},{3,2},{4,5},{5,4},{6,7},{7,6},{8,9},{9,8},{10,11... | collective-permute-start | bytes 589832 | tf_op jit(solution)/shard_map/ppermute | solution.py:30
  39.8 4.2 %collective-permute-start.4 = (f32[2,6,8,128]{3,2,1,0:T(8,128)S(1)}, f32[2,6,8,128]{3,2,1,0:T(8,128)S(1)}, u32[]{:S(2)}, u32[]{:S(2)}) collective-permute-start(f32[2,6,8,128]{3,2,1,0:T(8,128)S(1)} %dynamic-slice_bitcast_fusion.2), channel_id=1, source_target_pairs={{0,1},{1,0},{2,3},{3,2},{4,5},{5,4},{6,7},{7,6},{8,9},{9,8},{10,11... | collective-permute-start | bytes 147464 | tf_op jit(solution)/shard_map/ppermute | solution.py:30
  44.0 4.8 %collective-permute-start.5 = (f32[6,8,128]{2,1,0:T(8,128)S(1)}, f32[6,8,128]{2,1,0:T(8,128)S(1)}, u32[]{:S(2)}, u32[]{:S(2)}) collective-permute-start(f32[6,8,128]{2,1,0:T(8,128)S(1)} %dynamic-slice_bitcast_fusion.3), channel_id=1, source_target_pairs={{0,2},{1,3},{2,0},{3,1},{4,6},{5,7},{6,4},{7,5},{8,10},{9,11},{10,... | collective-permute-start | bytes 73736 | tf_op jit(solution)/shard_map/ppermute | solution.py:30
  48.8 14.7 %copy-start.2 = (bf16[1,6,8,128]{3,1,2,0:T(8,128)(2,1)}, bf16[1,6,8,128]{3,1,2,0:T(8,128)(2,1)S(1)}, u32[]{:S(2)}) copy-start(bf16[1,6,8,128]{3,1,2,0:T(8,128)(2,1)S(1)} %copy.37) | copy-start | bytes 36868
  48.8 3.8 %collective-permute-start.6 = (bf16[6,1024]{1,0:T(8,128)(2,1)S(1)}, bf16[6,1024]{1,0:T(8,128)(2,1)S(1)}, u32[]{:S(2)}, u32[]{:S(2)}) collective-permute-start(bf16[6,1024]{1,0:T(8,128)(2,1)S(1)} %bitcast.91), channel_id=1, source_target_pairs={{0,8},{4,12},{8,0},{12,4},{1,9},{5,13},{9,1},{13,5},{2,10},{6,14},... | collective-permute-start | bytes 36872 | tf_op jit(solution)/shard_map/ppermute | solution.py:30
  52.6 1.3 %collective-permute-start.7 = (bf16[2,6,1024]{2,1,0:T(8,128)(2,1)S(1)}, bf16[2,6,1024]{2,1,0:T(8,128)(2,1)S(1)}, u32[]{:S(2)}, u32[]{:S(2)}) collective-permute-start(bf16[2,6,1024]{2,1,0:T(8,128)(2,1)S(1)} %pad_maximum_fusion.3), channel_id=1, source_target_pairs={{0,4},{4,0},{8,12},{12,8},{1,5},{5,1},{9,13},{13,9},{2,6},{6,2},{1... | collective-permute-start | bytes 73736 | tf_op jit(solution)/shard_map/ppermute | solution.py:30
  54.6 3.7 %collective-permute-start.8 = (f32[2,6,6]{2,0,1:T(2,128)S(1)}, f32[2,6,6]{2,0,1:T(2,128)S(1)}, u32[]{:S(2)}, u32[]{:S(2)}) collective-permute-start(f32[2,6,6]{2,0,1:T(2,128)S(1)} %bitcast.93), channel_id=1, source_target_pairs={{0,1},{1,0},{2,3},{3,2},{4,5},{5,4},{6,7},{7,6},{8,9},{9,8},{10,11... | collective-permute-start | bytes 872 | tf_op jit(solution)/shard_map/ppermute | solution.py:30
  58.3 4.6 %collective-permute-start.9 = (f32[6,6]{1,0:T(8,128)S(1)}, f32[6,6]{1,0:T(8,128)S(1)}, u32[]{:S(2)}, u32[]{:S(2)}) collective-permute-start(f32[6,6]{1,0:T(8,128)S(1)} %bitcast.94), channel_id=1, source_target_pairs={{0,2},{1,3},{2,0},{3,1},{4,6},{5,7},{6,4},{7,5},{8,10},{9,11},{10,... | collective-permute-start | bytes 440 | tf_op jit(solution)/shard_map/ppermute | solution.py:30

commit v6 on v3

--- a/solution.py
+++ b/solution.py
@@ -4,6 +4,7 @@
 import jax.numpy as jnp
 from jax import lax
 from jax.sharding import PartitionSpec as P
+
 
 SEQ = 512
 epsilon = 1e-05
@@ -39,15 +40,8 @@
     return out
 
 
-def all_reduce(x, axis):
-    n = lax.axis_size(axis)
-    acc = reduce_scatter(x.reshape((n, -1) + x.shape[1:]), axis)
-    return all_gather(acc, axis).reshape(x.shape)
-
-
-def per_device(activations, cotangent, up_factor_matrix, input_sketch, rank_sketch):
+def body(activations, cotangent, up_factor_matrix, input_sketch, rank_sketch):
     shards = lax.axis_size("hidden")
-    me = lax.axis_index("hidden")
     examples = activations.shape[0] // SEQ
     backward_t = lax.dot_general(up_factor_matrix, cotangent, (((0,), (1,)), ((), ())),
                                  preferred_element_type=jnp.float32)
@@ -87,7 +81,7 @@
         P(),
     )
     return jax.shard_map(
-        per_device,
+        body,
         mesh=mesh,
         in_specs=placed,
         out_specs=(P(("groups", "dp"), "hidden"), P(("groups", "dp"), "hidden")),

time: 60.2 us -> 60.2 us (level)
  no operation moved by 1% of the time
where the time goes in v6:
time: 60.2 us; the launch traced here: 60 us
  starting transfers between devices  26.4 us (44%)
  matrix products  19.6 us (33%)
  waiting for transfers between devices  12.5 us (21%)
  between operations  0.82 us (1%)
  other arithmetic  0.66 us (1%)
    ppermute x6, starting transfers between devices, exchange(): got.append(lax.ppermute(piece, axis, [(i, (i + d) % n) for i in range(n)]))  11.7 us
    dot_general x1, matrix products, body(): lax.dot_general(up_factor_matrix, cotangent, (((0,), (1,)), ((), ())), pr...  8.64 us
    ppermute x6, waiting for transfers between devices, exchange(): got.append(lax.ppermute(piece, axis, [(i, (i + d) % n) for i in range(n)]))  7.35 us
    ppermute x3, starting transfers between devices, body(): own = own + lax.ppermute(outer(visiting), 'hidden', back)  6.64 us
    dot_general x1, matrix products, body(): jnp.dot(activations, input_sketch, preferred_element_type=jnp.float32)  6.43 us
    ppermute x3, starting transfers between devices, body(): lax.ppermute(rank_own, 'hidden', [(i, (i + d) % shards) for i in range(sh...  5.04 us
    dot_general x4, matrix products, outer(): return jnp.einsum('aes,esb->eab', rows, input_rows, precision=HI)  3.42 us
    ppermute x3, starting transfers between devices, all_gather(): got = lax.ppermute(x, axis, [(i, (i + d) % n) for i in range(n)])  3.03 us
  transfers between devices with their start and end apart: 15, of which 9 were waited for; matrix products, arithmetic and copies ran while one was open for 15% of the time, Pallas kernels for 0%

profile of v6, /device:TPU:0, one launch (start us, length us, event | category | flops | bytes accessed | tf_op | source)
XLA Modules:
  0.0 60.0 jit_solution(13058355314221678437)
XLA Ops:
  0.7 8.6 %fusion.8 = f32[64,3072]{1,0:T(8,128)S(1)} fusion(bf16[2048,64]{0,1:T(8,128)(2,1)} %param.7, bf16[3072,2048]{1,0:T(8,128)(2,1)} %param.6), kind=kOutput, calls=%fused_computation.26 | convolution fusion | flops 805306368 | bytes 13631488 | tf_op jit(solution)/shard_map/dot_general | solution.py:46
  9.3 0.6 convolution_bitcast_fusion
  9.9 3.1 %collective-permute-start = (f32[8,3072]{1,0:T(8,128)S(1)}, f32[8,3072]{1,0:T(8,128)S(1)}, u32[]{:S(2)}, u32[]{:S(2)}) collective-permute-start(f32[8,3072]{1,0:T(8,128)S(1)} %get-tuple-element.2), channel_id=1, source_target_pairs={{0,1},{1,2},{2,3},{3,0},{4,5},{5,6},{6,7},{7,4},{8,9},{9,10},{10,1... | collective-permute-start | bytes 294920 | tf_op jit(solution)/shard_map/ppermute | solution.py:20
  13.1 2.6 %collective-permute-start.1 = (f32[8,3072]{1,0:T(8,128)S(1)}, f32[8,3072]{1,0:T(8,128)S(1)}, u32[]{:S(2)}, u32[]{:S(2)}) collective-permute-start(f32[8,3072]{1,0:T(8,128)S(1)} %get-tuple-element.4), channel_id=1, source_target_pairs={{0,2},{1,3},{2,0},{3,1},{4,6},{5,7},{6,4},{7,5},{8,10},{9,11},{10,... | collective-permute-start | bytes 294920 | tf_op jit(solution)/shard_map/ppermute | solution.py:20
  15.6 1.3 %collective-permute-start.2 = (f32[8,3072]{1,0:T(8,128)S(1)}, f32[8,3072]{1,0:T(8,128)S(1)}, u32[]{:S(2)}, u32[]{:S(2)}) collective-permute-start(f32[8,3072]{1,0:T(8,128)S(1)} %get-tuple-element.3), channel_id=1, source_target_pairs={{0,3},{1,0},{2,1},{3,2},{4,7},{5,4},{6,5},{7,6},{8,11},{9,8},{10,9... | collective-permute-start | bytes 294920 | tf_op jit(solution)/shard_map/ppermute | solution.py:20
  17.0 1.7 %collective-permute-done = f32[8,3072]{1,0:T(8,128)S(1)} collective-permute-done((f32[8,3072]{1,0:T(8,128)S(1)}, f32[8,3072]{1,0:T(8,128)S(1)}, u32[]{:S(2)}, u32[]{:S(2)}) %collective-permute-start) | collective-permute-done | bytes 98336 | tf_op jit(solution)/shard_map/ppermute | solution.py:20
  18.7 3.5 %collective-permute-done.1 = f32[8,3072]{1,0:T(8,128)S(1)} collective-permute-done((f32[8,3072]{1,0:T(8,128)S(1)}, f32[8,3072]{1,0:T(8,128)S(1)}, u32[]{:S(2)}, u32[]{:S(2)}) %collective-permute-start.1) | collective-permute-done | bytes 98336 | tf_op jit(solution)/shard_map/ppermute | solution.py:20
  22.3 2.6 %collective-permute-start.3 = (f32[8,3072]{1,0:T(8,128)S(1)}, f32[8,3072]{1,0:T(8,128)S(1)}, u32[]{:S(2)}, u32[]{:S(2)}) collective-permute-start(f32[8,3072]{1,0:T(8,128)S(1)} %fusion.4), channel_id=1, source_target_pairs={{0,1},{1,2},{2,3},{3,0},{4,5},{5,6},{6,7},{7,4},{8,9},{9,10},{10,1... | collective-permute-start | bytes 294920 | tf_op jit(solution)/shard_map/ppermute | solution.py:60
  24.9 6.4 %fusion.9 = f32[3072,128]{1,0:T(8,128)S(1)} fusion(bf16[3072,2048]{1,0:T(8,128)(2,1)} %param.5, bf16[2048,128]{1,0:T(8,128)(2,1)S(1)} %copy-done), kind=kOutput, calls=%fused_computation.27 | convolution fusion | flops 1610612736 | bytes 14680064 | tf_op jit(solution)/shard_map/dot_general | solution.py:51
  31.3 1.7 %collective-permute-start.5 = (f32[8,3072]{1,0:T(8,128)S(1)}, f32[8,3072]{1,0:T(8,128)S(1)}, u32[]{:S(2)}, u32[]{:S(2)}) collective-permute-start(f32[8,3072]{1,0:T(8,128)S(1)} %fusion.4), channel_id=1, source_target_pairs={{0,2},{1,3},{2,0},{3,1},{4,6},{5,7},{6,4},{7,5},{8,10},{9,11},{10,... | collective-permute-start | bytes 294920 | tf_op jit(solution)/shard_map/ppermute | solution.py:60
  33.0 0.8 %collective-permute-start.7 = (f32[8,3072]{1,0:T(8,128)S(1)}, f32[8,3072]{1,0:T(8,128)S(1)}, u32[]{:S(2)}, u32[]{:S(2)}) collective-permute-start(f32[8,3072]{1,0:T(8,128)S(1)} %fusion.4), channel_id=1, source_target_pairs={{0,3},{1,0},{2,1},{3,2},{4,7},{5,4},{6,5},{7,6},{8,11},{9,8},{10,9... | collective-permute-start | bytes 294920 | tf_op jit(solution)/shard_map/ppermute | solution.py:60
  33.8 0.9 %fusion.10 = f32[6,8,128]{2,1,0:T(8,128)S(1)} fusion(f32[8,6,512]{2,0,1:T(8,128)S(1)} %bitcast.71, f32[6,512,128]{2,1,0:T(8,128)S(1)} %bitcast.63), kind=kOutput, calls=%fused_computation.28 | convolution fusion | flops 37748736 | bytes 1695744 | tf_op jit(solution)/shard_map/aes,esb->eab/dot_general | solution.py:56
  34.6 2.1 %collective-permute-start.4 = (f32[6,8,128]{2,1,0:T(8,128)S(1)}, f32[6,8,128]{2,1,0:T(8,128)S(1)}, u32[]{:S(2)}, u32[]{:S(2)}) collective-permute-start(f32[6,8,128]{2,1,0:T(8,128)S(1)} %fusion.10), channel_id=1, source_target_pairs={{0,3},{1,0},{2,1},{3,2},{4,7},{5,4},{6,5},{7,6},{8,11},{9,8},{10,9... | collective-permute-start | bytes 73736 | tf_op jit(solution)/shard_map/ppermute | solution.py:62
  36.7 2.0 %collective-permute-done.5 = f32[8,3072]{1,0:T(8,128)S(1)} collective-permute-done((f32[8,3072]{1,0:T(8,128)S(1)}, f32[8,3072]{1,0:T(8,128)S(1)}, u32[]{:S(2)}, u32[]{:S(2)}) %collective-permute-start.5) | collective-permute-done | bytes 98336 | tf_op jit(solution)/shard_map/ppermute | solution.py:60
  38.7 0.9 %fusion.11 = f32[6,8,128]{2,1,0:T(8,128)S(1)} fusion(f32[8,6,512]{2,0,1:T(8,128)S(1)} %bitcast.70, f32[6,512,128]{2,1,0:T(8,128)S(1)} %bitcast.64), kind=kOutput, calls=%fused_computation.29 | convolution fusion | flops 37748736 | bytes 1695744 | tf_op jit(solution)/shard_map/aes,esb->eab/dot_general | solution.py:56
  39.6 0.6 collective-permute-start.6
  40.1 0.9 %fusion.12 = f32[6,8,128]{2,1,0:T(8,128)S(1)} fusion(f32[8,6,512]{2,0,1:T(8,128)S(1)} %bitcast.69, f32[6,512,128]{2,1,0:T(8,128)S(1)} %bitcast.65), kind=kOutput, calls=%fused_computation.30 | convolution fusion | flops 37748736 | bytes 1695744 | tf_op jit(solution)/shard_map/aes,esb->eab/dot_general | solution.py:56
  41.0 4.0 %collective-permute-start.8 = (f32[6,8,128]{2,1,0:T(8,128)S(1)}, f32[6,8,128]{2,1,0:T(8,128)S(1)}, u32[]{:S(2)}, u32[]{:S(2)}) collective-permute-start(f32[6,8,128]{2,1,0:T(8,128)S(1)} %fusion.12), channel_id=1, source_target_pairs={{0,1},{1,2},{2,3},{3,0},{4,5},{5,6},{6,7},{7,4},{8,9},{9,10},{10,1... | collective-permute-start | bytes 73736 | tf_op jit(solution)/shard_map/ppermute | solution.py:62
  45.0 1.6 %collective-permute-done.8 = f32[6,8,128]{2,1,0:T(8,128)S(1)} collective-permute-done((f32[6,8,128]{2,1,0:T(8,128)S(1)}, f32[6,8,128]{2,1,0:T(8,128)S(1)}, u32[]{:S(2)}, u32[]{:S(2)}) %collective-permute-start.8) | collective-permute-done | bytes 24608 | tf_op jit(solution)/shard_map/ppermute | solution.py:62
  46.7 0.9 %fusion.2 = bf16[6,8,128]{2,1,0:T(8,128)(2,1)S(1)} fusion(f32[6,8,128]{2,1,0:T(8,128)S(1)} %collective-permute-done.8, f32[6,8,128]{2,1,0:T(8,128)S(1)} %collective-permute-done.6, f32[6,8,128]{2,1,0:T(8,128)S(1)} %collective-permute-done.4, f32[8,6,512]{2,0,1:T(8,128)S(1)} %bitcast.67, f32[6,512,128]{2,1,0:T(8,128)S(1)} %bitcast.66), kind=kOutput, calls=%fused_computation.4 | convolution fusion | flops 37773312 | bytes 1757184 | tf_op jit(solution)/shard_map/aes,esb->eab/dot_general | solution.py:56
  47.7 1.6 %collective-permute-start.10 = (bf16[6,1024]{1,0:T(8,128)(2,1)S(1)}, bf16[6,1024]{1,0:T(8,128)(2,1)S(1)}, u32[]{:S(2)}, u32[]{:S(2)}) collective-permute-start(bf16[6,1024]{1,0:T(8,128)(2,1)S(1)} %bitcast.73), channel_id=1, source_target_pairs={{0,8},{4,12},{8,0},{12,4},{1,9},{5,13},{9,1},{13,5},{2,10},{6,14},... | collective-permute-start | bytes 36872 | tf_op jit(solution)/shard_map/ppermute | solution.py:38
  49.3 1.4 %collective-permute-start.11 = (bf16[6,1024]{1,0:T(8,128)(2,1)S(1)}, bf16[6,1024]{1,0:T(8,128)(2,1)S(1)}, u32[]{:S(2)}, u32[]{:S(2)}) collective-permute-start(bf16[6,1024]{1,0:T(8,128)(2,1)S(1)} %bitcast.74), channel_id=1, source_target_pairs={{0,12},{4,0},{8,4},{12,8},{1,13},{5,1},{9,5},{13,9},{2,14},{6,2},{... | collective-permute-start | bytes 36872 | tf_op jit(solution)/shard_map/ppermute | solution.py:38
  50.7 0.2 collective-permute-done.9
  50.8 0.7 %collective-permute-done.10 = bf16[6,1024]{1,0:T(8,128)(2,1)S(1)} collective-permute-done((bf16[6,1024]{1,0:T(8,128)(2,1)S(1)}, bf16[6,1024]{1,0:T(8,128)(2,1)S(1)}, u32[]{:S(2)}, u32[]{:S(2)}) %collective-permute-start.10) | collective-permute-done | bytes 12320 | tf_op jit(solution)/shard_map/ppermute | solution.py:38
  51.5 0.6 %collective-permute-done.11 = bf16[6,1024]{1,0:T(8,128)(2,1)S(1)} collective-permute-done((bf16[6,1024]{1,0:T(8,128)(2,1)S(1)}, bf16[6,1024]{1,0:T(8,128)(2,1)S(1)}, u32[]{:S(2)}, u32[]{:S(2)}) %collective-permute-start.11) | collective-permute-done | bytes 12320 | tf_op jit(solution)/shard_map/ppermute | solution.py:38
  52.2 0.5 fusion.13
  52.7 2.2 %collective-permute-start.12 = (f32[6,6]{1,0:T(8,128)S(1)}, f32[6,6]{1,0:T(8,128)S(1)}, u32[]{:S(2)}, u32[]{:S(2)}) collective-permute-start(f32[6,6]{1,0:T(8,128)S(1)} %get-tuple-element.5), channel_id=1, source_target_pairs={{0,1},{1,2},{2,3},{3,0},{4,5},{5,6},{6,7},{7,4},{8,9},{9,10},{10,1... | collective-permute-start | bytes 440 | tf_op jit(solution)/shard_map/ppermute | solution.py:20
  54.9 0.3 collective-permute-start.13
  55.1 2.2 %collective-permute-start.14 = (f32[6,6]{1,0:T(8,128)S(1)}, f32[6,6]{1,0:T(8,128)S(1)}, u32[]{:S(2)}, u32[]{:S(2)}) collective-permute-start(f32[6,6]{1,0:T(8,128)S(1)} %get-tuple-element.6), channel_id=1, source_target_pairs={{0,3},{1,0},{2,1},{3,2},{4,7},{5,4},{6,5},{7,6},{8,11},{9,8},{10,9... | collective-permute-start | bytes 440 | tf_op jit(solution)/shard_map/ppermute | solution.py:20
  57.3 0.8 %collective-permute-done.12 = f32[6,6]{1,0:T(8,128)S(1)} collective-permute-done((f32[6,6]{1,0:T(8,128)S(1)}, f32[6,6]{1,0:T(8,128)S(1)}, u32[]{:S(2)}, u32[]{:S(2)}) %collective-permute-start.12) | collective-permute-done | bytes 176 | tf_op jit(solution)/shard_map/ppermute | solution.py:20
  58.1 1.3 %collective-permute-done.13 = f32[6,6]{1,0:T(8,128)S(1)} collective-permute-done((f32[6,6]{1,0:T(8,128)S(1)}, f32[6,6]{1,0:T(8,128)S(1)}, u32[]{:S(2)}, u32[]{:S(2)}) %collective-permute-start.13) | collective-permute-done | bytes 176 | tf_op jit(solution)/shard_map/ppermute | solution.py:20
  59.4 0.6 fusion.7
  (27 shorter events, 0.3 us)
Async XLA Ops:
  0.6 24.3 %copy-start = (bf16[2048,128]{1,0:T(8,128)(2,1)S(1)}, bf16[2048,128]{1,0:T(8,128)(2,1)}, u32[]{:S(2)}) copy-start(bf16[2048,128]{1,0:T(8,128)(2,1)} %param.8) | copy-start | bytes 1572868
  0.7 8.7 %copy-start.1 = (f32[64,32]{0,1:T(8,128)S(1)}, f32[64,32]{0,1:T(8,128)}, u32[]{:S(2)}) copy-start(f32[64,32]{0,1:T(8,128)} %param.9) | copy-start | bytes 24580
  9.9 8.8 %collective-permute-start = (f32[8,3072]{1,0:T(8,128)S(1)}, f32[8,3072]{1,0:T(8,128)S(1)}, u32[]{:S(2)}, u32[]{:S(2)}) collective-permute-start(f32[8,3072]{1,0:T(8,128)S(1)} %get-tuple-element.2), channel_id=1, source_target_pairs={{0,1},{1,2},{2,3},{3,0},{4,5},{5,6},{6,7},{7,4},{8,9},{9,10},{10,1... | collective-permute-start | bytes 294920 | tf_op jit(solution)/shard_map/ppermute | solution.py:20
  13.1 9.2 %collective-permute-start.1 = (f32[8,3072]{1,0:T(8,128)S(1)}, f32[8,3072]{1,0:T(8,128)S(1)}, u32[]{:S(2)}, u32[]{:S(2)}) collective-permute-start(f32[8,3072]{1,0:T(8,128)S(1)} %get-tuple-element.4), channel_id=1, source_target_pairs={{0,2},{1,3},{2,0},{3,1},{4,6},{5,7},{6,4},{7,5},{8,10},{9,11},{10,... | collective-permute-start | bytes 294920 | tf_op jit(solution)/shard_map/ppermute | solution.py:20
  15.6 6.6 %collective-permute-start.2 = (f32[8,3072]{1,0:T(8,128)S(1)}, f32[8,3072]{1,0:T(8,128)S(1)}, u32[]{:S(2)}, u32[]{:S(2)}) collective-permute-start(f32[8,3072]{1,0:T(8,128)S(1)} %get-tuple-element.3), channel_id=1, source_target_pairs={{0,3},{1,0},{2,1},{3,2},{4,7},{5,4},{6,5},{7,6},{8,11},{9,8},{10,9... | collective-permute-start | bytes 294920 | tf_op jit(solution)/shard_map/ppermute | solution.py:20
  22.3 11.5 %collective-permute-start.3 = (f32[8,3072]{1,0:T(8,128)S(1)}, f32[8,3072]{1,0:T(8,128)S(1)}, u32[]{:S(2)}, u32[]{:S(2)}) collective-permute-start(f32[8,3072]{1,0:T(8,128)S(1)} %fusion.4), channel_id=1, source_target_pairs={{0,1},{1,2},{2,3},{3,0},{4,5},{5,6},{6,7},{7,4},{8,9},{9,10},{10,1... | collective-permute-start | bytes 294920 | tf_op jit(solution)/shard_map/ppermute | solution.py:60
  31.3 7.4 %collective-permute-start.5 = (f32[8,3072]{1,0:T(8,128)S(1)}, f32[8,3072]{1,0:T(8,128)S(1)}, u32[]{:S(2)}, u32[]{:S(2)}) collective-permute-start(f32[8,3072]{1,0:T(8,128)S(1)} %fusion.4), channel_id=1, source_target_pairs={{0,2},{1,3},{2,0},{3,1},{4,6},{5,7},{6,4},{7,5},{8,10},{9,11},{10,... | collective-permute-start | bytes 294920 | tf_op jit(solution)/shard_map/ppermute | solution.py:60
  33.0 7.1 %collective-permute-start.7 = (f32[8,3072]{1,0:T(8,128)S(1)}, f32[8,3072]{1,0:T(8,128)S(1)}, u32[]{:S(2)}, u32[]{:S(2)}) collective-permute-start(f32[8,3072]{1,0:T(8,128)S(1)} %fusion.4), channel_id=1, source_target_pairs={{0,3},{1,0},{2,1},{3,2},{4,7},{5,4},{6,5},{7,6},{8,11},{9,8},{10,9... | collective-permute-start | bytes 294920 | tf_op jit(solution)/shard_map/ppermute | solution.py:60
  34.6 10.4 %collective-permute-start.4 = (f32[6,8,128]{2,1,0:T(8,128)S(1)}, f32[6,8,128]{2,1,0:T(8,128)S(1)}, u32[]{:S(2)}, u32[]{:S(2)}) collective-permute-start(f32[6,8,128]{2,1,0:T(8,128)S(1)} %fusion.10), channel_id=1, source_target_pairs={{0,3},{1,0},{2,1},{3,2},{4,7},{5,4},{6,5},{7,6},{8,11},{9,8},{10,9... | collective-permute-start | bytes 73736 | tf_op jit(solution)/shard_map/ppermute | solution.py:62
  39.6 5.5 %collective-permute-start.6 = (f32[6,8,128]{2,1,0:T(8,128)S(1)}, f32[6,8,128]{2,1,0:T(8,128)S(1)}, u32[]{:S(2)}, u32[]{:S(2)}) collective-permute-start(f32[6,8,128]{2,1,0:T(8,128)S(1)} %fusion.11), channel_id=1, source_target_pairs={{0,2},{1,3},{2,0},{3,1},{4,6},{5,7},{6,4},{7,5},{8,10},{9,11},{10,... | collective-permute-start | bytes 73736 | tf_op jit(solution)/shard_map/ppermute | solution.py:62
  41.0 5.7 %collective-permute-start.8 = (f32[6,8,128]{2,1,0:T(8,128)S(1)}, f32[6,8,128]{2,1,0:T(8,128)S(1)}, u32[]{:S(2)}, u32[]{:S(2)}) collective-permute-start(f32[6,8,128]{2,1,0:T(8,128)S(1)} %fusion.12), channel_id=1, source_target_pairs={{0,1},{1,2},{2,3},{3,0},{4,5},{5,6},{6,7},{7,4},{8,9},{9,10},{10,1... | collective-permute-start | bytes 73736 | tf_op jit(solution)/shard_map/ppermute | solution.py:62
  47.6 12.4 %copy-start.2 = (bf16[1,6,8,128]{3,1,2,0:T(8,128)(2,1)}, bf16[1,6,8,128]{3,1,2,0:T(8,128)(2,1)S(1)}, u32[]{:S(2)}) copy-start(bf16[1,6,8,128]{3,1,2,0:T(8,128)(2,1)S(1)} %copy.9) | copy-start | bytes 36868
  47.6 3.2 %collective-permute-start.9 = (bf16[6,1024]{1,0:T(8,128)(2,1)S(1)}, bf16[6,1024]{1,0:T(8,128)(2,1)S(1)}, u32[]{:S(2)}, u32[]{:S(2)}) collective-permute-start(bf16[6,1024]{1,0:T(8,128)(2,1)S(1)} %bitcast.72), channel_id=1, source_target_pairs={{0,4},{4,8},{8,12},{12,0},{1,5},{5,9},{9,13},{13,1},{2,6},{6,10},{... | collective-permute-start | bytes 36872 | tf_op jit(solution)/shard_map/ppermute | solution.py:38
  47.7 3.8 %collective-permute-start.10 = (bf16[6,1024]{1,0:T(8,128)(2,1)S(1)}, bf16[6,1024]{1,0:T(8,128)(2,1)S(1)}, u32[]{:S(2)}, u32[]{:S(2)}) collective-permute-start(bf16[6,1024]{1,0:T(8,128)(2,1)S(1)} %bitcast.73), channel_id=1, source_target_pairs={{0,8},{4,12},{8,0},{12,4},{1,9},{5,13},{9,1},{13,5},{2,10},{6,14},... | collective-permute-start | bytes 36872 | tf_op jit(solution)/shard_map/ppermute | solution.py:38
  49.3 2.8 %collective-permute-start.11 = (bf16[6,1024]{1,0:T(8,128)(2,1)S(1)}, bf16[6,1024]{1,0:T(8,128)(2,1)S(1)}, u32[]{:S(2)}, u32[]{:S(2)}) collective-permute-start(bf16[6,1024]{1,0:T(8,128)(2,1)S(1)} %bitcast.74), channel_id=1, source_target_pairs={{0,12},{4,0},{8,4},{12,8},{1,13},{5,1},{9,5},{13,9},{2,14},{6,2},{... | collective-permute-start | bytes 36872 | tf_op jit(solution)/shard_map/ppermute | solution.py:38
  52.7 5.4 %collective-permute-start.12 = (f32[6,6]{1,0:T(8,128)S(1)}, f32[6,6]{1,0:T(8,128)S(1)}, u32[]{:S(2)}, u32[]{:S(2)}) collective-permute-start(f32[6,6]{1,0:T(8,128)S(1)} %get-tuple-element.5), channel_id=1, source_target_pairs={{0,1},{1,2},{2,3},{3,0},{4,5},{5,6},{6,7},{7,4},{8,9},{9,10},{10,1... | collective-permute-start | bytes 440 | tf_op jit(solution)/shard_map/ppermute | solution.py:20
  54.9 4.5 %collective-permute-start.13 = (f32[6,6]{1,0:T(8,128)S(1)}, f32[6,6]{1,0:T(8,128)S(1)}, u32[]{:S(2)}, u32[]{:S(2)}) collective-permute-start(f32[6,6]{1,0:T(8,128)S(1)} %get-tuple-element.7), channel_id=1, source_target_pairs={{0,2},{1,3},{2,0},{3,1},{4,6},{5,7},{6,4},{7,5},{8,10},{9,11},{10,... | collective-permute-start | bytes 440 | tf_op jit(solution)/shard_map/ppermute | solution.py:20
  55.1 4.3 %collective-permute-start.14 = (f32[6,6]{1,0:T(8,128)S(1)}, f32[6,6]{1,0:T(8,128)S(1)}, u32[]{:S(2)}, u32[]{:S(2)}) collective-permute-start(f32[6,6]{1,0:T(8,128)S(1)} %get-tuple-element.6), channel_id=1, source_target_pairs={{0,3},{1,0},{2,1},{3,2},{4,7},{5,4},{6,5},{7,6},{8,11},{9,8},{10,9... | collective-permute-start | bytes 440 | tf_op jit(solution)/shard_map/ppermute | solution.py:20

commit v7 on v6

--- a/solution.py
+++ b/solution.py
@@ -43,9 +43,8 @@
 def body(activations, cotangent, up_factor_matrix, input_sketch, rank_sketch):
     shards = lax.axis_size("hidden")
     examples = activations.shape[0] // SEQ
-    backward_t = lax.dot_general(up_factor_matrix, cotangent, (((0,), (1,)), ((), ())),
-                                 preferred_element_type=jnp.float32)
-    rank_t = lax.dot_general(rank_sketch, backward_t, (((0,), (0,)), ((), ())), precision=HI)
+    backward_pass = jnp.dot(cotangent, up_factor_matrix, preferred_element_type=jnp.float32)
+    rank_t = jnp.dot(backward_pass, rank_sketch, precision=HI).T
     own_a = rank_t.shape[0] // shards
     rank_own = reduce_scatter(rank_t.reshape(shards, own_a, -1), "hidden")
     input_part = jnp.dot(activations, input_sketch, preferred_element_type=jnp.float32)

time: 60.2 us -> 60.8 us (level)
  waiting for transfers between devices: 12.5 us -> 20.1 us
  starting transfers between devices: 26.4 us -> 20.2 us
  matrix products: 19.6 us -> 18.6 us
    ppermute x3, starting transfers between devices: 6.64 us -> 1.92 us  [body(): own = own + lax.ppermute(outer(visiting), 'hidden', back)]
    ppermute x6, waiting for transfers between devices: 7.35 us -> 11.2 us  [exchange(): got.append(lax.ppermute(piece, axis, [(i, (i + d) % n) for i in range(n)]))]
    ppermute x3, waiting for transfers between devices: 2.02 us -> 4.15 us  [body(): lax.ppermute(rank_own, 'hidden', [(i, (i + d) % shards) for i in range(sh...]
    ppermute x3, waiting for transfers between devices: 1.65 us -> 3.4 us  [body(): own = own + lax.ppermute(outer(visiting), 'hidden', back)]
    dot_general x2, matrix products: 9.19 us -> 8.27 us  [the longest x1 6.54 us: body(): jnp.dot(cotangent, up_factor_matrix, preferred_element_type=jnp.float32)]
    ppermute x6, starting transfers between devices: 11.7 us -> 10.9 us  [exchange(): got.append(lax.ppermute(piece, axis, [(i, (i + d) % n) for i in range(n)]))]
    ppermute x3, starting transfers between devices: 5.04 us -> 4.41 us  [body(): lax.ppermute(rank_own, 'hidden', [(i, (i + d) % shards) for i in range(sh...]
  transfers between devices with their start and end apart: 15 -> 15, of which waited for: 9 -> 10; matrix products, arithmetic and copies ran while one was open for 15% -> 15% of each run, Pallas kernels for 0% -> 0%
where the time goes in v7:
time: 60.8 us; the launch traced here: 60.7 us
  starting transfers between devices  20.2 us (33%)
  waiting for transfers between devices  20.1 us (33%)
  matrix products  18.6 us (31%)
  between operations  0.86 us (1%)
  other arithmetic  0.66 us (1%)
    ppermute x6, waiting for transfers between devices, exchange(): got.append(lax.ppermute(piece, axis, [(i, (i + d) % n) for i in range(n)]))  11.2 us
    ppermute x6, starting transfers between devices, exchange(): got.append(lax.ppermute(piece, axis, [(i, (i + d) % n) for i in range(n)]))  10.9 us
    dot_general x1, matrix products, body(): jnp.dot(cotangent, up_factor_matrix, preferred_element_type=jnp.float32)  6.54 us
    dot_general x1, matrix products, body(): jnp.dot(activations, input_sketch, preferred_element_type=jnp.float32)  6.42 us
    ppermute x3, starting transfers between devices, body(): lax.ppermute(rank_own, 'hidden', [(i, (i + d) % shards) for i in range(sh...  4.41 us
    ppermute x3, waiting for transfers between devices, body(): lax.ppermute(rank_own, 'hidden', [(i, (i + d) % shards) for i in range(sh...  4.15 us
    dot_general x4, matrix products, outer(): return jnp.einsum('aes,esb->eab', rows, input_rows, precision=HI)  3.42 us
    ppermute x3, waiting for transfers between devices, body(): own = own + lax.ppermute(outer(visiting), 'hidden', back)  3.4 us
  transfers between devices with their start and end apart: 15, of which 10 were waited for; matrix products, arithmetic and copies ran while one was open for 15% of the time, Pallas kernels for 0%

profile of v7, /device:TPU:0, one launch (start us, length us, event | category | flops | bytes accessed | tf_op | source)
XLA Modules:
  0.0 60.7 jit_solution(15722663720313645311)
XLA Ops:
  0.7 6.5 %fusion.8 = f32[3072,64]{1,0:T(8,128)S(1)} fusion(bf16[3072,2048]{1,0:T(8,128)(2,1)} %param.6, bf16[2048,64]{0,1:T(8,128)(2,1)} %param.7), kind=kOutput, calls=%fused_computation.26 | convolution fusion | flops 805306368 | bytes 13631488 | tf_op jit(solution)/shard_map/dot_general | solution.py:46
  7.3 1.7 %convolution_bitcast_fusion = f32[4,8,3072]{2,1,0:T(8,128)S(1)} fusion(f32[3072,64]{1,0:T(8,128)S(1)} %fusion.8, f32[64,32]{0,1:T(8,128)S(1)} %copy-done.1), kind=kOutput, calls=%fused_computation | convolution fusion | flops 75497472 | bytes 1187840 | tf_op jit(solution)/shard_map/dot_general | solution.py:47
  9.0 5.1 %collective-permute-start.2 = (f32[8,3072]{1,0:T(8,128)S(1)}, f32[8,3072]{1,0:T(8,128)S(1)}, u32[]{:S(2)}, u32[]{:S(2)}) collective-permute-start(f32[8,3072]{1,0:T(8,128)S(1)} %get-tuple-element.3), channel_id=1, source_target_pairs={{0,3},{1,0},{2,1},{3,2},{4,7},{5,4},{6,5},{7,6},{8,11},{9,8},{10,9... | collective-permute-start | bytes 294920 | tf_op jit(solution)/shard_map/ppermute | solution.py:20
  14.2 1.0 %collective-permute-start = (f32[8,3072]{1,0:T(8,128)S(1)}, f32[8,3072]{1,0:T(8,128)S(1)}, u32[]{:S(2)}, u32[]{:S(2)}) collective-permute-start(f32[8,3072]{1,0:T(8,128)S(1)} %get-tuple-element.2), channel_id=1, source_target_pairs={{0,1},{1,2},{2,3},{3,0},{4,5},{5,6},{6,7},{7,4},{8,9},{9,10},{10,1... | collective-permute-start | bytes 294920 | tf_op jit(solution)/shard_map/ppermute | solution.py:20
  15.2 2.2 %collective-permute-done.2 = f32[8,3072]{1,0:T(8,128)S(1)} collective-permute-done((f32[8,3072]{1,0:T(8,128)S(1)}, f32[8,3072]{1,0:T(8,128)S(1)}, u32[]{:S(2)}, u32[]{:S(2)}) %collective-permute-start.2) | collective-permute-done | bytes 98336 | tf_op jit(solution)/shard_map/ppermute | solution.py:20
  17.4 5.6 %collective-permute-done.1 = f32[8,3072]{1,0:T(8,128)S(1)} collective-permute-done((f32[8,3072]{1,0:T(8,128)S(1)}, f32[8,3072]{1,0:T(8,128)S(1)}, u32[]{:S(2)}, u32[]{:S(2)}) %collective-permute-start.1) | collective-permute-done | bytes 98336 | tf_op jit(solution)/shard_map/ppermute | solution.py:20
  23.0 1.9 %collective-permute-start.7 = (f32[8,3072]{1,0:T(8,128)S(1)}, f32[8,3072]{1,0:T(8,128)S(1)}, u32[]{:S(2)}, u32[]{:S(2)}) collective-permute-start(f32[8,3072]{1,0:T(8,128)S(1)} %fusion.4), channel_id=1, source_target_pairs={{0,3},{1,0},{2,1},{3,2},{4,7},{5,4},{6,5},{7,6},{8,11},{9,8},{10,9... | collective-permute-start | bytes 294920 | tf_op jit(solution)/shard_map/ppermute | solution.py:59
  24.9 6.4 %fusion.9 = f32[3072,128]{1,0:T(8,128)S(1)} fusion(bf16[3072,2048]{1,0:T(8,128)(2,1)} %param.5, bf16[2048,128]{1,0:T(8,128)(2,1)S(1)} %copy-done), kind=kOutput, calls=%fused_computation.27 | convolution fusion | flops 1610612736 | bytes 14680064 | tf_op jit(solution)/shard_map/dot_general | solution.py:50
  31.3 0.5 collective-permute-start.5
  31.8 2.0 %collective-permute-start.3 = (f32[8,3072]{1,0:T(8,128)S(1)}, f32[8,3072]{1,0:T(8,128)S(1)}, u32[]{:S(2)}, u32[]{:S(2)}) collective-permute-start(f32[8,3072]{1,0:T(8,128)S(1)} %fusion.4), channel_id=1, source_target_pairs={{0,1},{1,2},{2,3},{3,0},{4,5},{5,6},{6,7},{7,4},{8,9},{9,10},{10,1... | collective-permute-start | bytes 294920 | tf_op jit(solution)/shard_map/ppermute | solution.py:59
  33.8 0.9 %fusion.12 = f32[6,8,128]{2,1,0:T(8,128)S(1)} fusion(f32[8,6,512]{2,0,1:T(8,128)S(1)} %bitcast.71, f32[6,512,128]{2,1,0:T(8,128)S(1)} %bitcast.63), kind=kOutput, calls=%fused_computation.30 | convolution fusion | flops 37748736 | bytes 1695744 | tf_op jit(solution)/shard_map/aes,esb->eab/dot_general | solution.py:55
  34.7 1.1 %collective-permute-start.8 = (f32[6,8,128]{2,1,0:T(8,128)S(1)}, f32[6,8,128]{2,1,0:T(8,128)S(1)}, u32[]{:S(2)}, u32[]{:S(2)}) collective-permute-start(f32[6,8,128]{2,1,0:T(8,128)S(1)} %fusion.12), channel_id=1, source_target_pairs={{0,1},{1,2},{2,3},{3,0},{4,5},{5,6},{6,7},{7,4},{8,9},{9,10},{10,1... | collective-permute-start | bytes 73736 | tf_op jit(solution)/shard_map/ppermute | solution.py:61
  35.8 4.1 %collective-permute-done.5 = f32[8,3072]{1,0:T(8,128)S(1)} collective-permute-done((f32[8,3072]{1,0:T(8,128)S(1)}, f32[8,3072]{1,0:T(8,128)S(1)}, u32[]{:S(2)}, u32[]{:S(2)}) %collective-permute-start.5) | collective-permute-done | bytes 98336 | tf_op jit(solution)/shard_map/ppermute | solution.py:59
  39.9 0.9 %fusion.11 = f32[6,8,128]{2,1,0:T(8,128)S(1)} fusion(f32[8,6,512]{2,0,1:T(8,128)S(1)} %bitcast.70, f32[6,512,128]{2,1,0:T(8,128)S(1)} %bitcast.64), kind=kOutput, calls=%fused_computation.29 | convolution fusion | flops 37748736 | bytes 1695744 | tf_op jit(solution)/shard_map/aes,esb->eab/dot_general | solution.py:55
  40.8 0.1 collective-permute-start.6
  40.9 0.9 %fusion.10 = f32[6,8,128]{2,1,0:T(8,128)S(1)} fusion(f32[8,6,512]{2,0,1:T(8,128)S(1)} %bitcast.69, f32[6,512,128]{2,1,0:T(8,128)S(1)} %bitcast.65), kind=kOutput, calls=%fused_computation.28 | convolution fusion | flops 37748736 | bytes 1695744 | tf_op jit(solution)/shard_map/aes,esb->eab/dot_general | solution.py:55
  41.7 0.7 %collective-permute-start.4 = (f32[6,8,128]{2,1,0:T(8,128)S(1)}, f32[6,8,128]{2,1,0:T(8,128)S(1)}, u32[]{:S(2)}, u32[]{:S(2)}) collective-permute-start(f32[6,8,128]{2,1,0:T(8,128)S(1)} %fusion.10), channel_id=1, source_target_pairs={{0,3},{1,0},{2,1},{3,2},{4,7},{5,4},{6,5},{7,6},{8,11},{9,8},{10,9... | collective-permute-start | bytes 73736 | tf_op jit(solution)/shard_map/ppermute | solution.py:61
  42.4 3.2 %collective-permute-done.6 = f32[6,8,128]{2,1,0:T(8,128)S(1)} collective-permute-done((f32[6,8,128]{2,1,0:T(8,128)S(1)}, f32[6,8,128]{2,1,0:T(8,128)S(1)}, u32[]{:S(2)}, u32[]{:S(2)}) %collective-permute-start.6) | collective-permute-done | bytes 24608 | tf_op jit(solution)/shard_map/ppermute | solution.py:61
  45.6 0.2 collective-permute-done.4
  45.8 0.9 %fusion.2 = bf16[6,8,128]{2,1,0:T(8,128)(2,1)S(1)} fusion(f32[6,8,128]{2,1,0:T(8,128)S(1)} %collective-permute-done.8, f32[6,8,128]{2,1,0:T(8,128)S(1)} %collective-permute-done.6, f32[6,8,128]{2,1,0:T(8,128)S(1)} %collective-permute-done.4, f32[8,6,512]{2,0,1:T(8,128)S(1)} %bitcast.67, f32[6,512,128]{2,1,0:T(8,128)S(1)} %bitcast.66), kind=kOutput, calls=%fused_computation.4 | convolution fusion | flops 37773312 | bytes 1757184 | tf_op jit(solution)/shard_map/aes,esb->eab/dot_general | solution.py:55
  46.9 1.6 %collective-permute-start.10 = (bf16[6,1024]{1,0:T(8,128)(2,1)S(1)}, bf16[6,1024]{1,0:T(8,128)(2,1)S(1)}, u32[]{:S(2)}, u32[]{:S(2)}) collective-permute-start(bf16[6,1024]{1,0:T(8,128)(2,1)S(1)} %bitcast.73), channel_id=1, source_target_pairs={{0,8},{4,12},{8,0},{12,4},{1,9},{5,13},{9,1},{13,5},{2,10},{6,14},... | collective-permute-start | bytes 36872 | tf_op jit(solution)/shard_map/ppermute | solution.py:38
  48.4 1.4 %collective-permute-start.11 = (bf16[6,1024]{1,0:T(8,128)(2,1)S(1)}, bf16[6,1024]{1,0:T(8,128)(2,1)S(1)}, u32[]{:S(2)}, u32[]{:S(2)}) collective-permute-start(bf16[6,1024]{1,0:T(8,128)(2,1)S(1)} %bitcast.74), channel_id=1, source_target_pairs={{0,12},{4,0},{8,4},{12,8},{1,13},{5,1},{9,5},{13,9},{2,14},{6,2},{... | collective-permute-start | bytes 36872 | tf_op jit(solution)/shard_map/ppermute | solution.py:38
  49.9 0.2 collective-permute-done.9
  50.0 0.7 %collective-permute-done.10 = bf16[6,1024]{1,0:T(8,128)(2,1)S(1)} collective-permute-done((bf16[6,1024]{1,0:T(8,128)(2,1)S(1)}, bf16[6,1024]{1,0:T(8,128)(2,1)S(1)}, u32[]{:S(2)}, u32[]{:S(2)}) %collective-permute-start.10) | collective-permute-done | bytes 12320 | tf_op jit(solution)/shard_map/ppermute | solution.py:38
  50.7 0.6 %collective-permute-done.11 = bf16[6,1024]{1,0:T(8,128)(2,1)S(1)} collective-permute-done((bf16[6,1024]{1,0:T(8,128)(2,1)S(1)}, bf16[6,1024]{1,0:T(8,128)(2,1)S(1)}, u32[]{:S(2)}, u32[]{:S(2)}) %collective-permute-start.11) | collective-permute-done | bytes 12320 | tf_op jit(solution)/shard_map/ppermute | solution.py:38
  51.4 0.5 fusion.13
  51.9 2.2 %collective-permute-start.14 = (f32[6,6]{1,0:T(8,128)S(1)}, f32[6,6]{1,0:T(8,128)S(1)}, u32[]{:S(2)}, u32[]{:S(2)}) collective-permute-start(f32[6,6]{1,0:T(8,128)S(1)} %get-tuple-element.6), channel_id=1, source_target_pairs={{0,3},{1,0},{2,1},{3,2},{4,7},{5,4},{6,5},{7,6},{8,11},{9,8},{10,9... | collective-permute-start | bytes 440 | tf_op jit(solution)/shard_map/ppermute | solution.py:20
  54.1 0.5 collective-permute-start.13
  54.7 2.0 %collective-permute-start.12 = (f32[6,6]{1,0:T(8,128)S(1)}, f32[6,6]{1,0:T(8,128)S(1)}, u32[]{:S(2)}, u32[]{:S(2)}) collective-permute-start(f32[6,6]{1,0:T(8,128)S(1)} %get-tuple-element.5), channel_id=1, source_target_pairs={{0,1},{1,2},{2,3},{3,0},{4,5},{5,6},{6,7},{7,4},{8,9},{9,10},{10,1... | collective-permute-start | bytes 440 | tf_op jit(solution)/shard_map/ppermute | solution.py:20
  56.6 2.0 %collective-permute-done.13 = f32[6,6]{1,0:T(8,128)S(1)} collective-permute-done((f32[6,6]{1,0:T(8,128)S(1)}, f32[6,6]{1,0:T(8,128)S(1)}, u32[]{:S(2)}, u32[]{:S(2)}) %collective-permute-start.13) | collective-permute-done | bytes 176 | tf_op jit(solution)/shard_map/ppermute | solution.py:20
  58.6 1.4 %collective-permute-done.12 = f32[6,6]{1,0:T(8,128)S(1)} collective-permute-done((f32[6,6]{1,0:T(8,128)S(1)}, f32[6,6]{1,0:T(8,128)S(1)}, u32[]{:S(2)}, u32[]{:S(2)}) %collective-permute-start.12) | collective-permute-done | bytes 176 | tf_op jit(solution)/shard_map/ppermute | solution.py:20
  60.1 0.6 fusion.7
  (27 shorter events, 0.3 us)
Async XLA Ops:
  0.6 24.3 %copy-start = (bf16[2048,128]{1,0:T(8,128)(2,1)S(1)}, bf16[2048,128]{1,0:T(8,128)(2,1)}, u32[]{:S(2)}) copy-start(bf16[2048,128]{1,0:T(8,128)(2,1)} %param.8) | copy-start | bytes 1572868
  0.7 6.6 %copy-start.1 = (f32[64,32]{0,1:T(8,128)S(1)}, f32[64,32]{0,1:T(8,128)}, u32[]{:S(2)}) copy-start(f32[64,32]{0,1:T(8,128)} %param.9) | copy-start | bytes 24580
  9.0 8.3 %collective-permute-start.2 = (f32[8,3072]{1,0:T(8,128)S(1)}, f32[8,3072]{1,0:T(8,128)S(1)}, u32[]{:S(2)}, u32[]{:S(2)}) collective-permute-start(f32[8,3072]{1,0:T(8,128)S(1)} %get-tuple-element.3), channel_id=1, source_target_pairs={{0,3},{1,0},{2,1},{3,2},{4,7},{5,4},{6,5},{7,6},{8,11},{9,8},{10,9... | collective-permute-start | bytes 294920 | tf_op jit(solution)/shard_map/ppermute | solution.py:20
  14.2 8.8 %collective-permute-start.1 = (f32[8,3072]{1,0:T(8,128)S(1)}, f32[8,3072]{1,0:T(8,128)S(1)}, u32[]{:S(2)}, u32[]{:S(2)}) collective-permute-start(f32[8,3072]{1,0:T(8,128)S(1)} %get-tuple-element.4), channel_id=1, source_target_pairs={{0,2},{1,3},{2,0},{3,1},{4,6},{5,7},{6,4},{7,5},{8,10},{9,11},{10,... | collective-permute-start | bytes 294920 | tf_op jit(solution)/shard_map/ppermute | solution.py:20
  14.2 8.8 %collective-permute-start = (f32[8,3072]{1,0:T(8,128)S(1)}, f32[8,3072]{1,0:T(8,128)S(1)}, u32[]{:S(2)}, u32[]{:S(2)}) collective-permute-start(f32[8,3072]{1,0:T(8,128)S(1)} %get-tuple-element.2), channel_id=1, source_target_pairs={{0,1},{1,2},{2,3},{3,0},{4,5},{5,6},{6,7},{7,4},{8,9},{9,10},{10,1... | collective-permute-start | bytes 294920 | tf_op jit(solution)/shard_map/ppermute | solution.py:20
  23.0 10.8 %collective-permute-start.7 = (f32[8,3072]{1,0:T(8,128)S(1)}, f32[8,3072]{1,0:T(8,128)S(1)}, u32[]{:S(2)}, u32[]{:S(2)}) collective-permute-start(f32[8,3072]{1,0:T(8,128)S(1)} %fusion.4), channel_id=1, source_target_pairs={{0,3},{1,0},{2,1},{3,2},{4,7},{5,4},{6,5},{7,6},{8,11},{9,8},{10,9... | collective-permute-start | bytes 294920 | tf_op jit(solution)/shard_map/ppermute | solution.py:59
  31.3 8.6 %collective-permute-start.5 = (f32[8,3072]{1,0:T(8,128)S(1)}, f32[8,3072]{1,0:T(8,128)S(1)}, u32[]{:S(2)}, u32[]{:S(2)}) collective-permute-start(f32[8,3072]{1,0:T(8,128)S(1)} %fusion.4), channel_id=1, source_target_pairs={{0,2},{1,3},{2,0},{3,1},{4,6},{5,7},{6,4},{7,5},{8,10},{9,11},{10,... | collective-permute-start | bytes 294920 | tf_op jit(solution)/shard_map/ppermute | solution.py:59
  31.8 9.1 %collective-permute-start.3 = (f32[8,3072]{1,0:T(8,128)S(1)}, f32[8,3072]{1,0:T(8,128)S(1)}, u32[]{:S(2)}, u32[]{:S(2)}) collective-permute-start(f32[8,3072]{1,0:T(8,128)S(1)} %fusion.4), channel_id=1, source_target_pairs={{0,1},{1,2},{2,3},{3,0},{4,5},{5,6},{6,7},{7,4},{8,9},{9,10},{10,1... | collective-permute-start | bytes 294920 | tf_op jit(solution)/shard_map/ppermute | solution.py:59
  34.7 7.8 %collective-permute-start.8 = (f32[6,8,128]{2,1,0:T(8,128)S(1)}, f32[6,8,128]{2,1,0:T(8,128)S(1)}, u32[]{:S(2)}, u32[]{:S(2)}) collective-permute-start(f32[6,8,128]{2,1,0:T(8,128)S(1)} %fusion.12), channel_id=1, source_target_pairs={{0,1},{1,2},{2,3},{3,0},{4,5},{5,6},{6,7},{7,4},{8,9},{9,10},{10,1... | collective-permute-start | bytes 73736 | tf_op jit(solution)/shard_map/ppermute | solution.py:61
  40.8 4.8 %collective-permute-start.6 = (f32[6,8,128]{2,1,0:T(8,128)S(1)}, f32[6,8,128]{2,1,0:T(8,128)S(1)}, u32[]{:S(2)}, u32[]{:S(2)}) collective-permute-start(f32[6,8,128]{2,1,0:T(8,128)S(1)} %fusion.11), channel_id=1, source_target_pairs={{0,2},{1,3},{2,0},{3,1},{4,6},{5,7},{6,4},{7,5},{8,10},{9,11},{10,... | collective-permute-start | bytes 73736 | tf_op jit(solution)/shard_map/ppermute | solution.py:61
  41.7 4.1 %collective-permute-start.4 = (f32[6,8,128]{2,1,0:T(8,128)S(1)}, f32[6,8,128]{2,1,0:T(8,128)S(1)}, u32[]{:S(2)}, u32[]{:S(2)}) collective-permute-start(f32[6,8,128]{2,1,0:T(8,128)S(1)} %fusion.10), channel_id=1, source_target_pairs={{0,3},{1,0},{2,1},{3,2},{4,7},{5,4},{6,5},{7,6},{8,11},{9,8},{10,9... | collective-permute-start | bytes 73736 | tf_op jit(solution)/shard_map/ppermute | solution.py:61
  46.8 13.9 %copy-start.2 = (bf16[1,6,8,128]{3,1,2,0:T(8,128)(2,1)}, bf16[1,6,8,128]{3,1,2,0:T(8,128)(2,1)S(1)}, u32[]{:S(2)}) copy-start(bf16[1,6,8,128]{3,1,2,0:T(8,128)(2,1)S(1)} %copy.9) | copy-start | bytes 36868
  46.8 3.2 %collective-permute-start.9 = (bf16[6,1024]{1,0:T(8,128)(2,1)S(1)}, bf16[6,1024]{1,0:T(8,128)(2,1)S(1)}, u32[]{:S(2)}, u32[]{:S(2)}) collective-permute-start(bf16[6,1024]{1,0:T(8,128)(2,1)S(1)} %bitcast.72), channel_id=1, source_target_pairs={{0,4},{4,8},{8,12},{12,0},{1,5},{5,9},{9,13},{13,1},{2,6},{6,10},{... | collective-permute-start | bytes 36872 | tf_op jit(solution)/shard_map/ppermute | solution.py:38
  46.9 3.8 %collective-permute-start.10 = (bf16[6,1024]{1,0:T(8,128)(2,1)S(1)}, bf16[6,1024]{1,0:T(8,128)(2,1)S(1)}, u32[]{:S(2)}, u32[]{:S(2)}) collective-permute-start(bf16[6,1024]{1,0:T(8,128)(2,1)S(1)} %bitcast.73), channel_id=1, source_target_pairs={{0,8},{4,12},{8,0},{12,4},{1,9},{5,13},{9,1},{13,5},{2,10},{6,14},... | collective-permute-start | bytes 36872 | tf_op jit(solution)/shard_map/ppermute | solution.py:38
  48.4 2.8 %collective-permute-start.11 = (bf16[6,1024]{1,0:T(8,128)(2,1)S(1)}, bf16[6,1024]{1,0:T(8,128)(2,1)S(1)}, u32[]{:S(2)}, u32[]{:S(2)}) collective-permute-start(bf16[6,1024]{1,0:T(8,128)(2,1)S(1)} %bitcast.74), channel_id=1, source_target_pairs={{0,12},{4,0},{8,4},{12,8},{1,13},{5,1},{9,5},{13,9},{2,14},{6,2},{... | collective-permute-start | bytes 36872 | tf_op jit(solution)/shard_map/ppermute | solution.py:38
  51.9 4.7 %collective-permute-start.14 = (f32[6,6]{1,0:T(8,128)S(1)}, f32[6,6]{1,0:T(8,128)S(1)}, u32[]{:S(2)}, u32[]{:S(2)}) collective-permute-start(f32[6,6]{1,0:T(8,128)S(1)} %get-tuple-element.6), channel_id=1, source_target_pairs={{0,3},{1,0},{2,1},{3,2},{4,7},{5,4},{6,5},{7,6},{8,11},{9,8},{10,9... | collective-permute-start | bytes 440 | tf_op jit(solution)/shard_map/ppermute | solution.py:20
  54.1 4.5 %collective-permute-start.13 = (f32[6,6]{1,0:T(8,128)S(1)}, f32[6,6]{1,0:T(8,128)S(1)}, u32[]{:S(2)}, u32[]{:S(2)}) collective-permute-start(f32[6,6]{1,0:T(8,128)S(1)} %get-tuple-element.7), channel_id=1, source_target_pairs={{0,2},{1,3},{2,0},{3,1},{4,6},{5,7},{6,4},{7,5},{8,10},{9,11},{10,... | collective-permute-start | bytes 440 | tf_op jit(solution)/shard_map/ppermute | solution.py:20
  54.7 5.4 %collective-permute-start.12 = (f32[6,6]{1,0:T(8,128)S(1)}, f32[6,6]{1,0:T(8,128)S(1)}, u32[]{:S(2)}, u32[]{:S(2)}) collective-permute-start(f32[6,6]{1,0:T(8,128)S(1)} %get-tuple-element.5), channel_id=1, source_target_pairs={{0,1},{1,2},{2,3},{3,0},{4,5},{5,6},{6,7},{7,4},{8,9},{9,10},{10,1... | collective-permute-start | bytes 440 | tf_op jit(solution)/shard_map/ppermute | solution.py:20

commit v8 on v7

--- a/solution.py
+++ b/solution.py
@@ -43,8 +43,15 @@
 def body(activations, cotangent, up_factor_matrix, input_sketch, rank_sketch):
     shards = lax.axis_size("hidden")
     examples = activations.shape[0] // SEQ
-    backward_pass = jnp.dot(cotangent, up_factor_matrix, preferred_element_type=jnp.float32)
-    rank_t = jnp.dot(backward_pass, rank_sketch, precision=HI).T
+    k_r = rank_sketch.shape[1]
+    folded = jnp.dot(up_factor_matrix.astype(jnp.float32), rank_sketch, precision=HI)
+    high_f32 = lax.reduce_precision(folded, exponent_bits=8, mantissa_bits=7)
+    high = high_f32.astype(jnp.bfloat16)
+    low = (folded - high_f32).astype(jnp.bfloat16)
+    pad = jnp.zeros((folded.shape[0], max(128 - 2 * k_r, 0)), jnp.bfloat16)
+    both = jnp.dot(cotangent, jnp.concatenate([high, low, pad], axis=1),
+                   preferred_element_type=jnp.float32)
+    rank_t = (both[:, :k_r] + both[:, k_r:2 * k_r]).T
     own_a = rank_t.shape[0] // shards
     rank_own = reduce_scatter(rank_t.reshape(shards, own_a, -1), "hidden")
     input_part = jnp.dot(activations, input_sketch, preferred_element_type=jnp.float32)

time: 60.8 us -> 63.7 us (1.048)
  matrix products: 18.6 us -> 20.9 us
    dot_general x2, matrix products: 8.27 us -> 10.5 us  [the longest x1 9.22 us: body(): jnp.dot(cotangent, jnp.concatenate([high, low, pad], axis=1), preferred_e...]
  transfers between devices with their start and end apart: 15 -> 15, of which waited for: 10 -> 10; matrix products, arithmetic and copies ran while one was open for 15% -> 14% of each run, Pallas kernels for 0% -> 0%
where the time goes in v8:
time: 63.7 us; the launch traced here: 63.6 us
  matrix products  20.9 us (33%)
  starting transfers between devices  20.2 us (32%)
  waiting for transfers between devices  20.1 us (32%)
  between operations  0.87 us (1%)
  local copies, waits for them, and re-layouts  0.76 us (1%)
  other arithmetic  0.71 us (1%)
    ppermute x6, waiting for transfers between devices, exchange(): got.append(lax.ppermute(piece, axis, [(i, (i + d) % n) for i in range(n)]))  11.2 us
    ppermute x6, starting transfers between devices, exchange(): got.append(lax.ppermute(piece, axis, [(i, (i + d) % n) for i in range(n)]))  10.9 us
    dot_general x1, matrix products, body(): jnp.dot(cotangent, jnp.concatenate([high, low, pad], axis=1), preferred_e...  9.22 us
    dot_general x1, matrix products, body(): jnp.dot(activations, input_sketch, preferred_element_type=jnp.float32)  6.42 us
    ppermute x3, starting transfers between devices, body(): lax.ppermute(rank_own, 'hidden', [(i, (i + d) % shards) for i in range(sh...  4.41 us
    ppermute x3, waiting for transfers between devices, body(): lax.ppermute(rank_own, 'hidden', [(i, (i + d) % shards) for i in range(sh...  4.14 us
    dot_general x4, matrix products, outer(): return jnp.einsum('aes,esb->eab', rows, input_rows, precision=HI)  3.42 us
    ppermute x3, waiting for transfers between devices, body(): own = own + lax.ppermute(outer(visiting), 'hidden', back)  3.4 us
  transfers between devices with their start and end apart: 15, of which 10 were waited for; matrix products, arithmetic and copies ran while one was open for 14% of the time, Pallas kernels for 0%

profile of v8, /device:TPU:0, one launch (start us, length us, event | category | flops | bytes accessed | tf_op | source)
XLA Modules:
  0.0 63.6 jit_solution(2678147218909790072)
XLA Ops:
  0.7 1.3 %reduce-precision_convert_fusion = (bf16[2048,32]{0,1:T(8,128)(2,1)S(1)}, bf16[2048,32]{0,1:T(8,128)(2,1)S(1)}) fusion(bf16[2048,64]{0,1:T(8,128)(2,1)} %param.7, f32[64,32]{0,1:T(8,128)} %param.9), kind=kOutput, calls=%fused_computation.12 | convolution fusion | flops 50593792 | bytes 532480 | tf_op jit(solution)/shard_map/dot_general | solution.py:47
  2.0 0.3 copy.8
  2.2 0.3 copy.7
  2.6 9.2 %convolution_bitcast_fusion = f32[3072,128]{0,1:T(8,128)S(1)} fusion(bf16[3072,2048]{1,0:T(8,128)(2,1)} %param.6, bf16[2048,32]{1,0:T(8,128)(2,1)S(1)} %copy.8, bf16[2048,32]{1,0:T(8,128)(2,1)S(1)} %copy.7, bf16[128]{0:T(256)(128)(2,1)S(1)} %pad.2.clone), kind=kOutput, calls=%fused_computation | convolution fusion | flops 1612185600 | bytes 14418176 | tf_op jit(solution)/shard_map/dot_general | solution.py:52
  11.9 5.1 %collective-permute-start.2 = (f32[8,3072]{1,0:T(8,128)S(1)}, f32[8,3072]{1,0:T(8,128)S(1)}, u32[]{:S(2)}, u32[]{:S(2)}) collective-permute-start(f32[8,3072]{1,0:T(8,128)S(1)} %get-tuple-element.3), channel_id=1, source_target_pairs={{0,3},{1,0},{2,1},{3,2},{4,7},{5,4},{6,5},{7,6},{8,11},{9,8},{10,9... | collective-permute-start | bytes 294920 | tf_op jit(solution)/shard_map/ppermute | solution.py:20
  17.1 1.0 %collective-permute-start = (f32[8,3072]{1,0:T(8,128)S(1)}, f32[8,3072]{1,0:T(8,128)S(1)}, u32[]{:S(2)}, u32[]{:S(2)}) collective-permute-start(f32[8,3072]{1,0:T(8,128)S(1)} %get-tuple-element.2), channel_id=1, source_target_pairs={{0,1},{1,2},{2,3},{3,0},{4,5},{5,6},{6,7},{7,4},{8,9},{9,10},{10,1... | collective-permute-start | bytes 294920 | tf_op jit(solution)/shard_map/ppermute | solution.py:20
  18.1 2.2 %collective-permute-done.2 = f32[8,3072]{1,0:T(8,128)S(1)} collective-permute-done((f32[8,3072]{1,0:T(8,128)S(1)}, f32[8,3072]{1,0:T(8,128)S(1)}, u32[]{:S(2)}, u32[]{:S(2)}) %collective-permute-start.2) | collective-permute-done | bytes 98336 | tf_op jit(solution)/shard_map/ppermute | solution.py:20
  20.3 5.6 %collective-permute-done.1 = f32[8,3072]{1,0:T(8,128)S(1)} collective-permute-done((f32[8,3072]{1,0:T(8,128)S(1)}, f32[8,3072]{1,0:T(8,128)S(1)}, u32[]{:S(2)}, u32[]{:S(2)}) %collective-permute-start.1) | collective-permute-done | bytes 98336 | tf_op jit(solution)/shard_map/ppermute | solution.py:20
  25.8 1.9 %collective-permute-start.7 = (f32[8,3072]{1,0:T(8,128)S(1)}, f32[8,3072]{1,0:T(8,128)S(1)}, u32[]{:S(2)}, u32[]{:S(2)}) collective-permute-start(f32[8,3072]{1,0:T(8,128)S(1)} %fusion.11), channel_id=1, source_target_pairs={{0,3},{1,0},{2,1},{3,2},{4,7},{5,4},{6,5},{7,6},{8,11},{9,8},{10,9... | collective-permute-start | bytes 294920 | tf_op jit(solution)/shard_map/ppermute | solution.py:66
  27.8 6.4 %fusion.16 = f32[3072,128]{1,0:T(8,128)S(1)} fusion(bf16[3072,2048]{1,0:T(8,128)(2,1)} %param.5, bf16[2048,128]{1,0:T(8,128)(2,1)S(1)} %copy-done), kind=kOutput, calls=%fused_computation.37 | convolution fusion | flops 1610612736 | bytes 14680064 | tf_op jit(solution)/shard_map/dot_general | solution.py:57
  34.2 0.5 collective-permute-start.5
  34.7 2.0 %collective-permute-start.3 = (f32[8,3072]{1,0:T(8,128)S(1)}, f32[8,3072]{1,0:T(8,128)S(1)}, u32[]{:S(2)}, u32[]{:S(2)}) collective-permute-start(f32[8,3072]{1,0:T(8,128)S(1)} %fusion.11), channel_id=1, source_target_pairs={{0,1},{1,2},{2,3},{3,0},{4,5},{5,6},{6,7},{7,4},{8,9},{9,10},{10,1... | collective-permute-start | bytes 294920 | tf_op jit(solution)/shard_map/ppermute | solution.py:66
  36.7 0.9 %fusion.19 = f32[6,8,128]{2,1,0:T(8,128)S(1)} fusion(f32[8,6,512]{2,0,1:T(8,128)S(1)} %bitcast.72, f32[6,512,128]{2,1,0:T(8,128)S(1)} %bitcast.64), kind=kOutput, calls=%fused_computation.40 | convolution fusion | flops 37748736 | bytes 1695744 | tf_op jit(solution)/shard_map/aes,esb->eab/dot_general | solution.py:62
  37.5 1.1 %collective-permute-start.8 = (f32[6,8,128]{2,1,0:T(8,128)S(1)}, f32[6,8,128]{2,1,0:T(8,128)S(1)}, u32[]{:S(2)}, u32[]{:S(2)}) collective-permute-start(f32[6,8,128]{2,1,0:T(8,128)S(1)} %fusion.19), channel_id=1, source_target_pairs={{0,1},{1,2},{2,3},{3,0},{4,5},{5,6},{6,7},{7,4},{8,9},{9,10},{10,1... | collective-permute-start | bytes 73736 | tf_op jit(solution)/shard_map/ppermute | solution.py:68
  38.7 4.1 %collective-permute-done.5 = f32[8,3072]{1,0:T(8,128)S(1)} collective-permute-done((f32[8,3072]{1,0:T(8,128)S(1)}, f32[8,3072]{1,0:T(8,128)S(1)}, u32[]{:S(2)}, u32[]{:S(2)}) %collective-permute-start.5) | collective-permute-done | bytes 98336 | tf_op jit(solution)/shard_map/ppermute | solution.py:66
  42.8 0.9 %fusion.18 = f32[6,8,128]{2,1,0:T(8,128)S(1)} fusion(f32[8,6,512]{2,0,1:T(8,128)S(1)} %bitcast.71, f32[6,512,128]{2,1,0:T(8,128)S(1)} %bitcast.65), kind=kOutput, calls=%fused_computation.39 | convolution fusion | flops 37748736 | bytes 1695744 | tf_op jit(solution)/shard_map/aes,esb->eab/dot_general | solution.py:62
  43.8 0.9 %fusion.17 = f32[6,8,128]{2,1,0:T(8,128)S(1)} fusion(f32[8,6,512]{2,0,1:T(8,128)S(1)} %bitcast.70, f32[6,512,128]{2,1,0:T(8,128)S(1)} %bitcast.66), kind=kOutput, calls=%fused_computation.38 | convolution fusion | flops 37748736 | bytes 1695744 | tf_op jit(solution)/shard_map/aes,esb->eab/dot_general | solution.py:62
  44.6 0.7 %collective-permute-start.4 = (f32[6,8,128]{2,1,0:T(8,128)S(1)}, f32[6,8,128]{2,1,0:T(8,128)S(1)}, u32[]{:S(2)}, u32[]{:S(2)}) collective-permute-start(f32[6,8,128]{2,1,0:T(8,128)S(1)} %fusion.17), channel_id=1, source_target_pairs={{0,3},{1,0},{2,1},{3,2},{4,7},{5,4},{6,5},{7,6},{8,11},{9,8},{10,9... | collective-permute-start | bytes 73736 | tf_op jit(solution)/shard_map/ppermute | solution.py:68
  45.3 3.2 %collective-permute-done.6 = f32[6,8,128]{2,1,0:T(8,128)S(1)} collective-permute-done((f32[6,8,128]{2,1,0:T(8,128)S(1)}, f32[6,8,128]{2,1,0:T(8,128)S(1)}, u32[]{:S(2)}, u32[]{:S(2)}) %collective-permute-start.6) | collective-permute-done | bytes 24608 | tf_op jit(solution)/shard_map/ppermute | solution.py:68
  48.5 0.2 collective-permute-done.4
  48.7 0.9 %fusion.2 = bf16[6,8,128]{2,1,0:T(8,128)(2,1)S(1)} fusion(f32[6,8,128]{2,1,0:T(8,128)S(1)} %collective-permute-done.8, f32[6,8,128]{2,1,0:T(8,128)S(1)} %collective-permute-done.6, f32[6,8,128]{2,1,0:T(8,128)S(1)} %collective-permute-done.4, f32[8,6,512]{2,0,1:T(8,128)S(1)} %bitcast.68, f32[6,512,128]{2,1,0:T(8,128)S(1)} %bitcast.67), kind=kOutput, calls=%fused_computation.4 | convolution fusion | flops 37773312 | bytes 1757184 | tf_op jit(solution)/shard_map/aes,esb->eab/dot_general | solution.py:62
  49.7 1.6 %collective-permute-start.10 = (bf16[6,1024]{1,0:T(8,128)(2,1)S(1)}, bf16[6,1024]{1,0:T(8,128)(2,1)S(1)}, u32[]{:S(2)}, u32[]{:S(2)}) collective-permute-start(bf16[6,1024]{1,0:T(8,128)(2,1)S(1)} %bitcast.74), channel_id=1, source_target_pairs={{0,8},{4,12},{8,0},{12,4},{1,9},{5,13},{9,1},{13,5},{2,10},{6,14},... | collective-permute-start | bytes 36872 | tf_op jit(solution)/shard_map/ppermute | solution.py:38
  51.4 1.4 %collective-permute-start.11 = (bf16[6,1024]{1,0:T(8,128)(2,1)S(1)}, bf16[6,1024]{1,0:T(8,128)(2,1)S(1)}, u32[]{:S(2)}, u32[]{:S(2)}) collective-permute-start(bf16[6,1024]{1,0:T(8,128)(2,1)S(1)} %bitcast.75), channel_id=1, source_target_pairs={{0,12},{4,0},{8,4},{12,8},{1,13},{5,1},{9,5},{13,9},{2,14},{6,2},{... | collective-permute-start | bytes 36872 | tf_op jit(solution)/shard_map/ppermute | solution.py:38
  52.9 0.7 %collective-permute-done.10 = bf16[6,1024]{1,0:T(8,128)(2,1)S(1)} collective-permute-done((bf16[6,1024]{1,0:T(8,128)(2,1)S(1)}, bf16[6,1024]{1,0:T(8,128)(2,1)S(1)}, u32[]{:S(2)}, u32[]{:S(2)}) %collective-permute-start.10) | collective-permute-done | bytes 12320 | tf_op jit(solution)/shard_map/ppermute | solution.py:38
  53.6 0.6 collective-permute-done.11
  54.3 0.5 fusion.20
  54.8 2.2 %collective-permute-start.14 = (f32[6,6]{1,0:T(8,128)S(1)}, f32[6,6]{1,0:T(8,128)S(1)}, u32[]{:S(2)}, u32[]{:S(2)}) collective-permute-start(f32[6,6]{1,0:T(8,128)S(1)} %get-tuple-element.8), channel_id=1, source_target_pairs={{0,3},{1,0},{2,1},{3,2},{4,7},{5,4},{6,5},{7,6},{8,11},{9,8},{10,9... | collective-permute-start | bytes 440 | tf_op jit(solution)/shard_map/ppermute | solution.py:20
  57.0 0.5 collective-permute-start.13
  57.6 2.0 %collective-permute-start.12 = (f32[6,6]{1,0:T(8,128)S(1)}, f32[6,6]{1,0:T(8,128)S(1)}, u32[]{:S(2)}, u32[]{:S(2)}) collective-permute-start(f32[6,6]{1,0:T(8,128)S(1)} %get-tuple-element.7), channel_id=1, source_target_pairs={{0,1},{1,2},{2,3},{3,0},{4,5},{5,6},{6,7},{7,4},{8,9},{9,10},{10,1... | collective-permute-start | bytes 440 | tf_op jit(solution)/shard_map/ppermute | solution.py:20
  59.5 2.0 %collective-permute-done.13 = f32[6,6]{1,0:T(8,128)S(1)} collective-permute-done((f32[6,6]{1,0:T(8,128)S(1)}, f32[6,6]{1,0:T(8,128)S(1)}, u32[]{:S(2)}, u32[]{:S(2)}) %collective-permute-start.13) | collective-permute-done | bytes 176 | tf_op jit(solution)/shard_map/ppermute | solution.py:20
  61.5 1.4 %collective-permute-done.12 = f32[6,6]{1,0:T(8,128)S(1)} collective-permute-done((f32[6,6]{1,0:T(8,128)S(1)}, f32[6,6]{1,0:T(8,128)S(1)}, u32[]{:S(2)}, u32[]{:S(2)}) %collective-permute-start.12) | collective-permute-done | bytes 176 | tf_op jit(solution)/shard_map/ppermute | solution.py:20
  63.0 0.6 fusion.14
  (30 shorter events, 0.6 us)
Async XLA Ops:
  0.6 27.2 %copy-start = (bf16[2048,128]{1,0:T(8,128)(2,1)S(1)}, bf16[2048,128]{1,0:T(8,128)(2,1)}, u32[]{:S(2)}) copy-start(bf16[2048,128]{1,0:T(8,128)(2,1)} %param.8) | copy-start | bytes 1572868
  11.9 8.3 %collective-permute-start.2 = (f32[8,3072]{1,0:T(8,128)S(1)}, f32[8,3072]{1,0:T(8,128)S(1)}, u32[]{:S(2)}, u32[]{:S(2)}) collective-permute-start(f32[8,3072]{1,0:T(8,128)S(1)} %get-tuple-element.3), channel_id=1, source_target_pairs={{0,3},{1,0},{2,1},{3,2},{4,7},{5,4},{6,5},{7,6},{8,11},{9,8},{10,9... | collective-permute-start | bytes 294920 | tf_op jit(solution)/shard_map/ppermute | solution.py:20
  17.1 8.7 %collective-permute-start.1 = (f32[8,3072]{1,0:T(8,128)S(1)}, f32[8,3072]{1,0:T(8,128)S(1)}, u32[]{:S(2)}, u32[]{:S(2)}) collective-permute-start(f32[8,3072]{1,0:T(8,128)S(1)} %get-tuple-element.4), channel_id=1, source_target_pairs={{0,2},{1,3},{2,0},{3,1},{4,6},{5,7},{6,4},{7,5},{8,10},{9,11},{10,... | collective-permute-start | bytes 294920 | tf_op jit(solution)/shard_map/ppermute | solution.py:20
  17.1 8.7 %collective-permute-start = (f32[8,3072]{1,0:T(8,128)S(1)}, f32[8,3072]{1,0:T(8,128)S(1)}, u32[]{:S(2)}, u32[]{:S(2)}) collective-permute-start(f32[8,3072]{1,0:T(8,128)S(1)} %get-tuple-element.2), channel_id=1, source_target_pairs={{0,1},{1,2},{2,3},{3,0},{4,5},{5,6},{6,7},{7,4},{8,9},{9,10},{10,1... | collective-permute-start | bytes 294920 | tf_op jit(solution)/shard_map/ppermute | solution.py:20
  25.8 10.8 %collective-permute-start.7 = (f32[8,3072]{1,0:T(8,128)S(1)}, f32[8,3072]{1,0:T(8,128)S(1)}, u32[]{:S(2)}, u32[]{:S(2)}) collective-permute-start(f32[8,3072]{1,0:T(8,128)S(1)} %fusion.11), channel_id=1, source_target_pairs={{0,3},{1,0},{2,1},{3,2},{4,7},{5,4},{6,5},{7,6},{8,11},{9,8},{10,9... | collective-permute-start | bytes 294920 | tf_op jit(solution)/shard_map/ppermute | solution.py:66
  34.2 8.6 %collective-permute-start.5 = (f32[8,3072]{1,0:T(8,128)S(1)}, f32[8,3072]{1,0:T(8,128)S(1)}, u32[]{:S(2)}, u32[]{:S(2)}) collective-permute-start(f32[8,3072]{1,0:T(8,128)S(1)} %fusion.11), channel_id=1, source_target_pairs={{0,2},{1,3},{2,0},{3,1},{4,6},{5,7},{6,4},{7,5},{8,10},{9,11},{10,... | collective-permute-start | bytes 294920 | tf_op jit(solution)/shard_map/ppermute | solution.py:66
  34.7 9.1 %collective-permute-start.3 = (f32[8,3072]{1,0:T(8,128)S(1)}, f32[8,3072]{1,0:T(8,128)S(1)}, u32[]{:S(2)}, u32[]{:S(2)}) collective-permute-start(f32[8,3072]{1,0:T(8,128)S(1)} %fusion.11), channel_id=1, source_target_pairs={{0,1},{1,2},{2,3},{3,0},{4,5},{5,6},{6,7},{7,4},{8,9},{9,10},{10,1... | collective-permute-start | bytes 294920 | tf_op jit(solution)/shard_map/ppermute | solution.py:66
  37.5 7.8 %collective-permute-start.8 = (f32[6,8,128]{2,1,0:T(8,128)S(1)}, f32[6,8,128]{2,1,0:T(8,128)S(1)}, u32[]{:S(2)}, u32[]{:S(2)}) collective-permute-start(f32[6,8,128]{2,1,0:T(8,128)S(1)} %fusion.19), channel_id=1, source_target_pairs={{0,1},{1,2},{2,3},{3,0},{4,5},{5,6},{6,7},{7,4},{8,9},{9,10},{10,1... | collective-permute-start | bytes 73736 | tf_op jit(solution)/shard_map/ppermute | solution.py:68
  43.7 4.8 %collective-permute-start.6 = (f32[6,8,128]{2,1,0:T(8,128)S(1)}, f32[6,8,128]{2,1,0:T(8,128)S(1)}, u32[]{:S(2)}, u32[]{:S(2)}) collective-permute-start(f32[6,8,128]{2,1,0:T(8,128)S(1)} %fusion.18), channel_id=1, source_target_pairs={{0,2},{1,3},{2,0},{3,1},{4,6},{5,7},{6,4},{7,5},{8,10},{9,11},{10,... | collective-permute-start | bytes 73736 | tf_op jit(solution)/shard_map/ppermute | solution.py:68
  44.6 4.1 %collective-permute-start.4 = (f32[6,8,128]{2,1,0:T(8,128)S(1)}, f32[6,8,128]{2,1,0:T(8,128)S(1)}, u32[]{:S(2)}, u32[]{:S(2)}) collective-permute-start(f32[6,8,128]{2,1,0:T(8,128)S(1)} %fusion.17), channel_id=1, source_target_pairs={{0,3},{1,0},{2,1},{3,2},{4,7},{5,4},{6,5},{7,6},{8,11},{9,8},{10,9... | collective-permute-start | bytes 73736 | tf_op jit(solution)/shard_map/ppermute | solution.py:68
  49.7 13.9 %copy-start.1 = (bf16[1,6,8,128]{3,1,2,0:T(8,128)(2,1)}, bf16[1,6,8,128]{3,1,2,0:T(8,128)(2,1)S(1)}, u32[]{:S(2)}) copy-start(bf16[1,6,8,128]{3,1,2,0:T(8,128)(2,1)S(1)} %copy.11) | copy-start | bytes 36868
  49.7 3.2 %collective-permute-start.9 = (bf16[6,1024]{1,0:T(8,128)(2,1)S(1)}, bf16[6,1024]{1,0:T(8,128)(2,1)S(1)}, u32[]{:S(2)}, u32[]{:S(2)}) collective-permute-start(bf16[6,1024]{1,0:T(8,128)(2,1)S(1)} %bitcast.73), channel_id=1, source_target_pairs={{0,4},{4,8},{8,12},{12,0},{1,5},{5,9},{9,13},{13,1},{2,6},{6,10},{... | collective-permute-start | bytes 36872 | tf_op jit(solution)/shard_map/ppermute | solution.py:38
  49.7 3.8 %collective-permute-start.10 = (bf16[6,1024]{1,0:T(8,128)(2,1)S(1)}, bf16[6,1024]{1,0:T(8,128)(2,1)S(1)}, u32[]{:S(2)}, u32[]{:S(2)}) collective-permute-start(bf16[6,1024]{1,0:T(8,128)(2,1)S(1)} %bitcast.74), channel_id=1, source_target_pairs={{0,8},{4,12},{8,0},{12,4},{1,9},{5,13},{9,1},{13,5},{2,10},{6,14},... | collective-permute-start | bytes 36872 | tf_op jit(solution)/shard_map/ppermute | solution.py:38
  51.4 2.8 %collective-permute-start.11 = (bf16[6,1024]{1,0:T(8,128)(2,1)S(1)}, bf16[6,1024]{1,0:T(8,128)(2,1)S(1)}, u32[]{:S(2)}, u32[]{:S(2)}) collective-permute-start(bf16[6,1024]{1,0:T(8,128)(2,1)S(1)} %bitcast.75), channel_id=1, source_target_pairs={{0,12},{4,0},{8,4},{12,8},{1,13},{5,1},{9,5},{13,9},{2,14},{6,2},{... | collective-permute-start | bytes 36872 | tf_op jit(solution)/shard_map/ppermute | solution.py:38
  54.8 4.7 %collective-permute-start.14 = (f32[6,6]{1,0:T(8,128)S(1)}, f32[6,6]{1,0:T(8,128)S(1)}, u32[]{:S(2)}, u32[]{:S(2)}) collective-permute-start(f32[6,6]{1,0:T(8,128)S(1)} %get-tuple-element.8), channel_id=1, source_target_pairs={{0,3},{1,0},{2,1},{3,2},{4,7},{5,4},{6,5},{7,6},{8,11},{9,8},{10,9... | collective-permute-start | bytes 440 | tf_op jit(solution)/shard_map/ppermute | solution.py:20
  57.0 4.5 %collective-permute-start.13 = (f32[6,6]{1,0:T(8,128)S(1)}, f32[6,6]{1,0:T(8,128)S(1)}, u32[]{:S(2)}, u32[]{:S(2)}) collective-permute-start(f32[6,6]{1,0:T(8,128)S(1)} %get-tuple-element.9), channel_id=1, source_target_pairs={{0,2},{1,3},{2,0},{3,1},{4,6},{5,7},{6,4},{7,5},{8,10},{9,11},{10,... | collective-permute-start | bytes 440 | tf_op jit(solution)/shard_map/ppermute | solution.py:20
  57.6 5.4 %collective-permute-start.12 = (f32[6,6]{1,0:T(8,128)S(1)}, f32[6,6]{1,0:T(8,128)S(1)}, u32[]{:S(2)}, u32[]{:S(2)}) collective-permute-start(f32[6,6]{1,0:T(8,128)S(1)} %get-tuple-element.7), channel_id=1, source_target_pairs={{0,1},{1,2},{2,3},{3,0},{4,5},{5,6},{6,7},{7,4},{8,9},{9,10},{10,1... | collective-permute-start | bytes 440 | tf_op jit(solution)/shard_map/ppermute | solution.py:20

commit v9 on v6

--- a/solution.py
+++ b/solution.py
@@ -8,7 +8,6 @@
 
 SEQ = 512
 epsilon = 1e-05
-HI = lax.Precision.HIGHEST
 
 
 def exchange(blocks, axis):
@@ -45,7 +44,7 @@
     examples = activations.shape[0] // SEQ
     backward_t = lax.dot_general(up_factor_matrix, cotangent, (((0,), (1,)), ((), ())),
                                  preferred_element_type=jnp.float32)
-    rank_t = lax.dot_general(rank_sketch, backward_t, (((0,), (0,)), ((), ())), precision=HI)
+    rank_t = lax.dot_general(rank_sketch, backward_t, (((0,), (0,)), ((), ())), precision=lax.Precision.HIGH)
     own_a = rank_t.shape[0] // shards
     rank_own = reduce_scatter(rank_t.reshape(shards, own_a, -1), "hidden")
     input_part = jnp.dot(activations, input_sketch, preferred_element_type=jnp.float32)
@@ -53,7 +52,7 @@
 
     def outer(rank_block):
         rows = rank_block.reshape(own_a, examples, SEQ)
-        return jnp.einsum("aes,esb->eab", rows, input_rows, precision=HI)
+        return jnp.einsum("aes,esb->eab", rows, input_rows, precision=lax.Precision.HIGH)
 
     own = outer(rank_own)
     for d in range(1, shards):
@@ -65,7 +64,7 @@
     every = all_gather(features, "dp").reshape(-1, features.shape[1]).astype(jnp.float32)
     all_count = every.shape[0]
     weight = 1.0 / (jnp.sum(every * every, axis=0) / all_count + epsilon)
-    partial_scores = jnp.dot(widened * weight, every.T, precision=HI)
+    partial_scores = jnp.dot(widened * weight, every.T, precision=lax.Precision.HIGH)
     feat_total = features.shape[1] * shards
     score_blocks = partial_scores.reshape(examples, shards, -1).transpose(1, 0, 2)
     scores = reduce_scatter(score_blocks, "hidden") / math.sqrt(feat_total)

time: 60.2 us -> 58.7 us (0.975)
  matrix products: 19.6 us -> 17.7 us
    dot_general x5, matrix products: 3.95 us -> 2.32 us  [the longest x4 1.93 us: outer(): jnp.einsum('aes,esb->eab', rows, input_rows, precision=lax.Precision.HIGH)]
  transfers between devices with their start and end apart: 15 -> 15, of which waited for: 9 -> 9; matrix products, arithmetic and copies ran while one was open for 15% -> 13% of each run, Pallas kernels for 0% -> 0%
where the time goes in v9:
time: 58.7 us; the launch traced here: 58.6 us
  starting transfers between devices  26.2 us (45%)
  matrix products  17.7 us (30%)
  waiting for transfers between devices  13.1 us (22%)
  between operations  0.81 us (1%)
  other arithmetic  0.66 us (1%)
    ppermute x6, starting transfers between devices, exchange(): got.append(lax.ppermute(piece, axis, [(i, (i + d) % n) for i in range(n)]))  11.5 us
    dot_general x1, matrix products, body(): lax.dot_general(up_factor_matrix, cotangent, (((0,), (1,)), ((), ())), pr...  8.64 us
    ppermute x6, waiting for transfers between devices, exchange(): got.append(lax.ppermute(piece, axis, [(i, (i + d) % n) for i in range(n)]))  7.39 us
    ppermute x3, starting transfers between devices, body(): own = own + lax.ppermute(outer(visiting), 'hidden', back)  6.64 us
    dot_general x1, matrix products, body(): jnp.dot(activations, input_sketch, preferred_element_type=jnp.float32)  6.42 us
    ppermute x3, starting transfers between devices, body(): lax.ppermute(rank_own, 'hidden', [(i, (i + d) % shards) for i in range(sh...  5.04 us
    ppermute x3, starting transfers between devices, all_gather(): got = lax.ppermute(x, axis, [(i, (i + d) % n) for i in range(n)])  3.02 us
    ppermute x3, waiting for transfers between devices, body(): lax.ppermute(rank_own, 'hidden', [(i, (i + d) % shards) for i in range(sh...  2.41 us
  transfers between devices with their start and end apart: 15, of which 9 were waited for; matrix products, arithmetic and copies ran while one was open for 13% of the time, Pallas kernels for 0%

profile of v9, /device:TPU:0, one launch (start us, length us, event | category | flops | bytes accessed | tf_op | source)
XLA Modules:
  0.0 58.6 jit_solution(17013483356945433103)
XLA Ops:
  0.7 8.6 %fusion.8 = f32[64,3072]{1,0:T(8,128)S(1)} fusion(bf16[2048,64]{0,1:T(8,128)(2,1)} %param.7, bf16[3072,2048]{1,0:T(8,128)(2,1)} %param.6), kind=kOutput, calls=%fused_computation.26 | convolution fusion | flops 805306368 | bytes 13631488 | tf_op jit(solution)/shard_map/dot_general | solution.py:45
  9.3 0.3 convolution_bitcast_fusion
  9.7 3.1 %collective-permute-start = (f32[8,3072]{1,0:T(8,128)S(1)}, f32[8,3072]{1,0:T(8,128)S(1)}, u32[]{:S(2)}, u32[]{:S(2)}) collective-permute-start(f32[8,3072]{1,0:T(8,128)S(1)} %get-tuple-element.2), channel_id=1, source_target_pairs={{0,1},{1,2},{2,3},{3,0},{4,5},{5,6},{6,7},{7,4},{8,9},{9,10},{10,1... | collective-permute-start | bytes 294920 | tf_op jit(solution)/shard_map/ppermute | solution.py:19
  12.8 2.6 %collective-permute-start.1 = (f32[8,3072]{1,0:T(8,128)S(1)}, f32[8,3072]{1,0:T(8,128)S(1)}, u32[]{:S(2)}, u32[]{:S(2)}) collective-permute-start(f32[8,3072]{1,0:T(8,128)S(1)} %get-tuple-element.4), channel_id=1, source_target_pairs={{0,2},{1,3},{2,0},{3,1},{4,6},{5,7},{6,4},{7,5},{8,10},{9,11},{10,... | collective-permute-start | bytes 294920 | tf_op jit(solution)/shard_map/ppermute | solution.py:19
  15.4 1.3 %collective-permute-start.2 = (f32[8,3072]{1,0:T(8,128)S(1)}, f32[8,3072]{1,0:T(8,128)S(1)}, u32[]{:S(2)}, u32[]{:S(2)}) collective-permute-start(f32[8,3072]{1,0:T(8,128)S(1)} %get-tuple-element.3), channel_id=1, source_target_pairs={{0,3},{1,0},{2,1},{3,2},{4,7},{5,4},{6,5},{7,6},{8,11},{9,8},{10,9... | collective-permute-start | bytes 294920 | tf_op jit(solution)/shard_map/ppermute | solution.py:19
  16.8 1.7 %collective-permute-done = f32[8,3072]{1,0:T(8,128)S(1)} collective-permute-done((f32[8,3072]{1,0:T(8,128)S(1)}, f32[8,3072]{1,0:T(8,128)S(1)}, u32[]{:S(2)}, u32[]{:S(2)}) %collective-permute-start) | collective-permute-done | bytes 98336 | tf_op jit(solution)/shard_map/ppermute | solution.py:19
  18.5 3.5 %collective-permute-done.1 = f32[8,3072]{1,0:T(8,128)S(1)} collective-permute-done((f32[8,3072]{1,0:T(8,128)S(1)}, f32[8,3072]{1,0:T(8,128)S(1)}, u32[]{:S(2)}, u32[]{:S(2)}) %collective-permute-start.1) | collective-permute-done | bytes 98336 | tf_op jit(solution)/shard_map/ppermute | solution.py:19
  22.1 2.6 %collective-permute-start.3 = (f32[8,3072]{1,0:T(8,128)S(1)}, f32[8,3072]{1,0:T(8,128)S(1)}, u32[]{:S(2)}, u32[]{:S(2)}) collective-permute-start(f32[8,3072]{1,0:T(8,128)S(1)} %fusion.4), channel_id=1, source_target_pairs={{0,1},{1,2},{2,3},{3,0},{4,5},{5,6},{6,7},{7,4},{8,9},{9,10},{10,1... | collective-permute-start | bytes 294920 | tf_op jit(solution)/shard_map/ppermute | solution.py:59
  24.7 6.4 %fusion.9 = f32[3072,128]{1,0:T(8,128)S(1)} fusion(bf16[3072,2048]{1,0:T(8,128)(2,1)} %param.5, bf16[2048,128]{1,0:T(8,128)(2,1)S(1)} %copy-done), kind=kOutput, calls=%fused_computation.27 | convolution fusion | flops 1610612736 | bytes 14680064 | tf_op jit(solution)/shard_map/dot_general | solution.py:50
  31.1 1.7 %collective-permute-start.5 = (f32[8,3072]{1,0:T(8,128)S(1)}, f32[8,3072]{1,0:T(8,128)S(1)}, u32[]{:S(2)}, u32[]{:S(2)}) collective-permute-start(f32[8,3072]{1,0:T(8,128)S(1)} %fusion.4), channel_id=1, source_target_pairs={{0,2},{1,3},{2,0},{3,1},{4,6},{5,7},{6,4},{7,5},{8,10},{9,11},{10,... | collective-permute-start | bytes 294920 | tf_op jit(solution)/shard_map/ppermute | solution.py:59
  32.8 0.8 %collective-permute-start.7 = (f32[8,3072]{1,0:T(8,128)S(1)}, f32[8,3072]{1,0:T(8,128)S(1)}, u32[]{:S(2)}, u32[]{:S(2)}) collective-permute-start(f32[8,3072]{1,0:T(8,128)S(1)} %fusion.4), channel_id=1, source_target_pairs={{0,3},{1,0},{2,1},{3,2},{4,7},{5,4},{6,5},{7,6},{8,11},{9,8},{10,9... | collective-permute-start | bytes 294920 | tf_op jit(solution)/shard_map/ppermute | solution.py:59
  33.6 0.5 fusion.10
  34.0 2.0 %collective-permute-start.4 = (f32[6,8,128]{2,1,0:T(8,128)S(1)}, f32[6,8,128]{2,1,0:T(8,128)S(1)}, u32[]{:S(2)}, u32[]{:S(2)}) collective-permute-start(f32[6,8,128]{2,1,0:T(8,128)S(1)} %fusion.10), channel_id=1, source_target_pairs={{0,3},{1,0},{2,1},{3,2},{4,7},{5,4},{6,5},{7,6},{8,11},{9,8},{10,9... | collective-permute-start | bytes 73736 | tf_op jit(solution)/shard_map/ppermute | solution.py:61
  36.1 2.4 %collective-permute-done.5 = f32[8,3072]{1,0:T(8,128)S(1)} collective-permute-done((f32[8,3072]{1,0:T(8,128)S(1)}, f32[8,3072]{1,0:T(8,128)S(1)}, u32[]{:S(2)}, u32[]{:S(2)}) %collective-permute-start.5) | collective-permute-done | bytes 98336 | tf_op jit(solution)/shard_map/ppermute | solution.py:59
  38.5 0.5 fusion.11
  39.0 0.7 %collective-permute-start.6 = (f32[6,8,128]{2,1,0:T(8,128)S(1)}, f32[6,8,128]{2,1,0:T(8,128)S(1)}, u32[]{:S(2)}, u32[]{:S(2)}) collective-permute-start(f32[6,8,128]{2,1,0:T(8,128)S(1)} %fusion.11), channel_id=1, source_target_pairs={{0,2},{1,3},{2,0},{3,1},{4,6},{5,7},{6,4},{7,5},{8,10},{9,11},{10,... | collective-permute-start | bytes 73736 | tf_op jit(solution)/shard_map/ppermute | solution.py:61
  39.7 0.5 fusion.12
  40.2 3.8 %collective-permute-start.8 = (f32[6,8,128]{2,1,0:T(8,128)S(1)}, f32[6,8,128]{2,1,0:T(8,128)S(1)}, u32[]{:S(2)}, u32[]{:S(2)}) collective-permute-start(f32[6,8,128]{2,1,0:T(8,128)S(1)} %fusion.12), channel_id=1, source_target_pairs={{0,1},{1,2},{2,3},{3,0},{4,5},{5,6},{6,7},{7,4},{8,9},{9,10},{10,1... | collective-permute-start | bytes 73736 | tf_op jit(solution)/shard_map/ppermute | solution.py:61
  44.1 1.8 %collective-permute-done.8 = f32[6,8,128]{2,1,0:T(8,128)S(1)} collective-permute-done((f32[6,8,128]{2,1,0:T(8,128)S(1)}, f32[6,8,128]{2,1,0:T(8,128)S(1)}, u32[]{:S(2)}, u32[]{:S(2)}) %collective-permute-start.8) | collective-permute-done | bytes 24608 | tf_op jit(solution)/shard_map/ppermute | solution.py:61
  45.9 0.5 fusion.2
  46.5 1.6 %collective-permute-start.10 = (bf16[6,1024]{1,0:T(8,128)(2,1)S(1)}, bf16[6,1024]{1,0:T(8,128)(2,1)S(1)}, u32[]{:S(2)}, u32[]{:S(2)}) collective-permute-start(bf16[6,1024]{1,0:T(8,128)(2,1)S(1)} %bitcast.73), channel_id=1, source_target_pairs={{0,8},{4,12},{8,0},{12,4},{1,9},{5,13},{9,1},{13,5},{2,10},{6,14},... | collective-permute-start | bytes 36872 | tf_op jit(solution)/shard_map/ppermute | solution.py:37
  48.1 1.4 %collective-permute-start.11 = (bf16[6,1024]{1,0:T(8,128)(2,1)S(1)}, bf16[6,1024]{1,0:T(8,128)(2,1)S(1)}, u32[]{:S(2)}, u32[]{:S(2)}) collective-permute-start(bf16[6,1024]{1,0:T(8,128)(2,1)S(1)} %bitcast.74), channel_id=1, source_target_pairs={{0,12},{4,0},{8,4},{12,8},{1,13},{5,1},{9,5},{13,9},{2,14},{6,2},{... | collective-permute-start | bytes 36872 | tf_op jit(solution)/shard_map/ppermute | solution.py:37
  49.5 0.2 collective-permute-done.9
  49.7 0.7 %collective-permute-done.10 = bf16[6,1024]{1,0:T(8,128)(2,1)S(1)} collective-permute-done((bf16[6,1024]{1,0:T(8,128)(2,1)S(1)}, bf16[6,1024]{1,0:T(8,128)(2,1)S(1)}, u32[]{:S(2)}, u32[]{:S(2)}) %collective-permute-start.10) | collective-permute-done | bytes 12320 | tf_op jit(solution)/shard_map/ppermute | solution.py:37
  50.3 0.6 %collective-permute-done.11 = bf16[6,1024]{1,0:T(8,128)(2,1)S(1)} collective-permute-done((bf16[6,1024]{1,0:T(8,128)(2,1)S(1)}, bf16[6,1024]{1,0:T(8,128)(2,1)S(1)}, u32[]{:S(2)}, u32[]{:S(2)}) %collective-permute-start.11) | collective-permute-done | bytes 12320 | tf_op jit(solution)/shard_map/ppermute | solution.py:37
  51.0 0.4 fusion.13
  51.4 2.0 %collective-permute-start.12 = (f32[6,6]{1,0:T(8,128)S(1)}, f32[6,6]{1,0:T(8,128)S(1)}, u32[]{:S(2)}, u32[]{:S(2)}) collective-permute-start(f32[6,6]{1,0:T(8,128)S(1)} %get-tuple-element.5), channel_id=1, source_target_pairs={{0,1},{1,2},{2,3},{3,0},{4,5},{5,6},{6,7},{7,4},{8,9},{9,10},{10,1... | collective-permute-start | bytes 440 | tf_op jit(solution)/shard_map/ppermute | solution.py:19
  53.4 0.4 collective-permute-start.13
  53.8 2.1 %collective-permute-start.14 = (f32[6,6]{1,0:T(8,128)S(1)}, f32[6,6]{1,0:T(8,128)S(1)}, u32[]{:S(2)}, u32[]{:S(2)}) collective-permute-start(f32[6,6]{1,0:T(8,128)S(1)} %get-tuple-element.6), channel_id=1, source_target_pairs={{0,3},{1,0},{2,1},{3,2},{4,7},{5,4},{6,5},{7,6},{8,11},{9,8},{10,9... | collective-permute-start | bytes 440 | tf_op jit(solution)/shard_map/ppermute | solution.py:19
  55.9 1.0 %collective-permute-done.12 = f32[6,6]{1,0:T(8,128)S(1)} collective-permute-done((f32[6,6]{1,0:T(8,128)S(1)}, f32[6,6]{1,0:T(8,128)S(1)}, u32[]{:S(2)}, u32[]{:S(2)}) %collective-permute-start.12) | collective-permute-done | bytes 176 | tf_op jit(solution)/shard_map/ppermute | solution.py:19
  56.8 1.1 %collective-permute-done.13 = f32[6,6]{1,0:T(8,128)S(1)} collective-permute-done((f32[6,6]{1,0:T(8,128)S(1)}, f32[6,6]{1,0:T(8,128)S(1)}, u32[]{:S(2)}, u32[]{:S(2)}) %collective-permute-start.13) | collective-permute-done | bytes 176 | tf_op jit(solution)/shard_map/ppermute | solution.py:19
  58.0 0.6 %fusion.7 = f32[6,6]{1,0:T(8,128)} fusion(f32[6,6]{1,0:T(8,128)S(1)} %collective-permute-done.14, f32[6,6]{1,0:T(8,128)S(1)} %collective-permute-done.13, f32[6,6]{1,0:T(8,128)S(1)} %collective-permute-done.12, f32[6,4,6]{2,0,1:T(8,128)S(1)} %fusion.13, s32[]{:T(128)S(6)} %select_n.64), kind=kLoop, calls=%fused_computation.20 | loop fusion | flops 144 | bytes 724 | tf_op jit(solution)/shard_map/div | solution.py:70
  (27 shorter events, 0.3 us)
Async XLA Ops:
  0.6 24.0 %copy-start = (bf16[2048,128]{1,0:T(8,128)(2,1)S(1)}, bf16[2048,128]{1,0:T(8,128)(2,1)}, u32[]{:S(2)}) copy-start(bf16[2048,128]{1,0:T(8,128)(2,1)} %param.8) | copy-start | bytes 1572868
  0.7 8.7 %copy-start.1 = (f32[64,32]{0,1:T(8,128)S(1)}, f32[64,32]{0,1:T(8,128)}, u32[]{:S(2)}) copy-start(f32[64,32]{0,1:T(8,128)} %param.9) | copy-start | bytes 24580
  9.7 8.8 %collective-permute-start = (f32[8,3072]{1,0:T(8,128)S(1)}, f32[8,3072]{1,0:T(8,128)S(1)}, u32[]{:S(2)}, u32[]{:S(2)}) collective-permute-start(f32[8,3072]{1,0:T(8,128)S(1)} %get-tuple-element.2), channel_id=1, source_target_pairs={{0,1},{1,2},{2,3},{3,0},{4,5},{5,6},{6,7},{7,4},{8,9},{9,10},{10,1... | collective-permute-start | bytes 294920 | tf_op jit(solution)/shard_map/ppermute | solution.py:19
  12.8 9.2 %collective-permute-start.1 = (f32[8,3072]{1,0:T(8,128)S(1)}, f32[8,3072]{1,0:T(8,128)S(1)}, u32[]{:S(2)}, u32[]{:S(2)}) collective-permute-start(f32[8,3072]{1,0:T(8,128)S(1)} %get-tuple-element.4), channel_id=1, source_target_pairs={{0,2},{1,3},{2,0},{3,1},{4,6},{5,7},{6,4},{7,5},{8,10},{9,11},{10,... | collective-permute-start | bytes 294920 | tf_op jit(solution)/shard_map/ppermute | solution.py:19
  15.4 6.6 %collective-permute-start.2 = (f32[8,3072]{1,0:T(8,128)S(1)}, f32[8,3072]{1,0:T(8,128)S(1)}, u32[]{:S(2)}, u32[]{:S(2)}) collective-permute-start(f32[8,3072]{1,0:T(8,128)S(1)} %get-tuple-element.3), channel_id=1, source_target_pairs={{0,3},{1,0},{2,1},{3,2},{4,7},{5,4},{6,5},{7,6},{8,11},{9,8},{10,9... | collective-permute-start | bytes 294920 | tf_op jit(solution)/shard_map/ppermute | solution.py:19
  22.1 11.5 %collective-permute-start.3 = (f32[8,3072]{1,0:T(8,128)S(1)}, f32[8,3072]{1,0:T(8,128)S(1)}, u32[]{:S(2)}, u32[]{:S(2)}) collective-permute-start(f32[8,3072]{1,0:T(8,128)S(1)} %fusion.4), channel_id=1, source_target_pairs={{0,1},{1,2},{2,3},{3,0},{4,5},{5,6},{6,7},{7,4},{8,9},{9,10},{10,1... | collective-permute-start | bytes 294920 | tf_op jit(solution)/shard_map/ppermute | solution.py:59
  31.1 7.4 %collective-permute-start.5 = (f32[8,3072]{1,0:T(8,128)S(1)}, f32[8,3072]{1,0:T(8,128)S(1)}, u32[]{:S(2)}, u32[]{:S(2)}) collective-permute-start(f32[8,3072]{1,0:T(8,128)S(1)} %fusion.4), channel_id=1, source_target_pairs={{0,2},{1,3},{2,0},{3,1},{4,6},{5,7},{6,4},{7,5},{8,10},{9,11},{10,... | collective-permute-start | bytes 294920 | tf_op jit(solution)/shard_map/ppermute | solution.py:59
  32.8 6.9 %collective-permute-start.7 = (f32[8,3072]{1,0:T(8,128)S(1)}, f32[8,3072]{1,0:T(8,128)S(1)}, u32[]{:S(2)}, u32[]{:S(2)}) collective-permute-start(f32[8,3072]{1,0:T(8,128)S(1)} %fusion.4), channel_id=1, source_target_pairs={{0,3},{1,0},{2,1},{3,2},{4,7},{5,4},{6,5},{7,6},{8,11},{9,8},{10,9... | collective-permute-start | bytes 294920 | tf_op jit(solution)/shard_map/ppermute | solution.py:59
  34.0 10.0 %collective-permute-start.4 = (f32[6,8,128]{2,1,0:T(8,128)S(1)}, f32[6,8,128]{2,1,0:T(8,128)S(1)}, u32[]{:S(2)}, u32[]{:S(2)}) collective-permute-start(f32[6,8,128]{2,1,0:T(8,128)S(1)} %fusion.10), channel_id=1, source_target_pairs={{0,3},{1,0},{2,1},{3,2},{4,7},{5,4},{6,5},{7,6},{8,11},{9,8},{10,9... | collective-permute-start | bytes 73736 | tf_op jit(solution)/shard_map/ppermute | solution.py:61
  39.0 5.1 %collective-permute-start.6 = (f32[6,8,128]{2,1,0:T(8,128)S(1)}, f32[6,8,128]{2,1,0:T(8,128)S(1)}, u32[]{:S(2)}, u32[]{:S(2)}) collective-permute-start(f32[6,8,128]{2,1,0:T(8,128)S(1)} %fusion.11), channel_id=1, source_target_pairs={{0,2},{1,3},{2,0},{3,1},{4,6},{5,7},{6,4},{7,5},{8,10},{9,11},{10,... | collective-permute-start | bytes 73736 | tf_op jit(solution)/shard_map/ppermute | solution.py:61
  40.2 5.7 %collective-permute-start.8 = (f32[6,8,128]{2,1,0:T(8,128)S(1)}, f32[6,8,128]{2,1,0:T(8,128)S(1)}, u32[]{:S(2)}, u32[]{:S(2)}) collective-permute-start(f32[6,8,128]{2,1,0:T(8,128)S(1)} %fusion.12), channel_id=1, source_target_pairs={{0,1},{1,2},{2,3},{3,0},{4,5},{5,6},{6,7},{7,4},{8,9},{9,10},{10,1... | collective-permute-start | bytes 73736 | tf_op jit(solution)/shard_map/ppermute | solution.py:61
  46.5 12.1 %copy-start.2 = (bf16[1,6,8,128]{3,1,2,0:T(8,128)(2,1)}, bf16[1,6,8,128]{3,1,2,0:T(8,128)(2,1)S(1)}, u32[]{:S(2)}) copy-start(bf16[1,6,8,128]{3,1,2,0:T(8,128)(2,1)S(1)} %copy.9) | copy-start | bytes 36868
  46.5 3.2 %collective-permute-start.9 = (bf16[6,1024]{1,0:T(8,128)(2,1)S(1)}, bf16[6,1024]{1,0:T(8,128)(2,1)S(1)}, u32[]{:S(2)}, u32[]{:S(2)}) collective-permute-start(bf16[6,1024]{1,0:T(8,128)(2,1)S(1)} %bitcast.72), channel_id=1, source_target_pairs={{0,4},{4,8},{8,12},{12,0},{1,5},{5,9},{9,13},{13,1},{2,6},{6,10},{... | collective-permute-start | bytes 36872 | tf_op jit(solution)/shard_map/ppermute | solution.py:37
  46.5 3.8 %collective-permute-start.10 = (bf16[6,1024]{1,0:T(8,128)(2,1)S(1)}, bf16[6,1024]{1,0:T(8,128)(2,1)S(1)}, u32[]{:S(2)}, u32[]{:S(2)}) collective-permute-start(bf16[6,1024]{1,0:T(8,128)(2,1)S(1)} %bitcast.73), channel_id=1, source_target_pairs={{0,8},{4,12},{8,0},{12,4},{1,9},{5,13},{9,1},{13,5},{2,10},{6,14},... | collective-permute-start | bytes 36872 | tf_op jit(solution)/shard_map/ppermute | solution.py:37
  48.1 2.8 %collective-permute-start.11 = (bf16[6,1024]{1,0:T(8,128)(2,1)S(1)}, bf16[6,1024]{1,0:T(8,128)(2,1)S(1)}, u32[]{:S(2)}, u32[]{:S(2)}) collective-permute-start(bf16[6,1024]{1,0:T(8,128)(2,1)S(1)} %bitcast.74), channel_id=1, source_target_pairs={{0,12},{4,0},{8,4},{12,8},{1,13},{5,1},{9,5},{13,9},{2,14},{6,2},{... | collective-permute-start | bytes 36872 | tf_op jit(solution)/shard_map/ppermute | solution.py:37
  51.4 5.4 %collective-permute-start.12 = (f32[6,6]{1,0:T(8,128)S(1)}, f32[6,6]{1,0:T(8,128)S(1)}, u32[]{:S(2)}, u32[]{:S(2)}) collective-permute-start(f32[6,6]{1,0:T(8,128)S(1)} %get-tuple-element.5), channel_id=1, source_target_pairs={{0,1},{1,2},{2,3},{3,0},{4,5},{5,6},{6,7},{7,4},{8,9},{9,10},{10,1... | collective-permute-start | bytes 440 | tf_op jit(solution)/shard_map/ppermute | solution.py:19
  53.4 4.5 %collective-permute-start.13 = (f32[6,6]{1,0:T(8,128)S(1)}, f32[6,6]{1,0:T(8,128)S(1)}, u32[]{:S(2)}, u32[]{:S(2)}) collective-permute-start(f32[6,6]{1,0:T(8,128)S(1)} %get-tuple-element.7), channel_id=1, source_target_pairs={{0,2},{1,3},{2,0},{3,1},{4,6},{5,7},{6,4},{7,5},{8,10},{9,11},{10,... | collective-permute-start | bytes 440 | tf_op jit(solution)/shard_map/ppermute | solution.py:19
  53.8 4.2 %collective-permute-start.14 = (f32[6,6]{1,0:T(8,128)S(1)}, f32[6,6]{1,0:T(8,128)S(1)}, u32[]{:S(2)}, u32[]{:S(2)}) collective-permute-start(f32[6,6]{1,0:T(8,128)S(1)} %get-tuple-element.6), channel_id=1, source_target_pairs={{0,3},{1,0},{2,1},{3,2},{4,7},{5,4},{6,5},{7,6},{8,11},{9,8},{10,9... | collective-permute-start | bytes 440 | tf_op jit(solution)/shard_map/ppermute | solution.py:19
